TPU v7x, 512 devices: a whole 4x8x8 slice. The times are simulated.
512 devices in a mesh: param: 32 (over x, z), ex: 16 (over y, core).
Axes of the slice: x: 4, y: 8, z: 8, core: 2. Of those that a mesh axis runs over, the one named last changes fastest.
Arguments:
- adapter_gradients: bfloat16 [512, 131072], P('ex', 'param'), may hold values from -560 to 560
- sign_hash_keys: int32 [4], replicated, may hold values from 1 to 16777215
- target_indices: int32 [256], replicated, may hold values from 0 to 511
Outputs:
- features: float32 [512, 8192], P('ex', 'param')
- scores: float32 [512, 256], P('ex')
All inputs are finite; a program needn't handle non-finite values.
Results may differ from a plain program's by a relative error of at most 0.0003.
Values sent between devices are 32-bit elements; how exact they have to be, the bound alone decides.
No kernel may reach another device: no remote copies, remote signals or barrier semaphores. Data moves between devices by JAX's collectives and lax.ppermute only.
A program may use at most 128 MiB of HBM per device.

v0:
```python
import jax
import jax.numpy as jnp
from jax import lax
from jax.sharding import Mesh, PartitionSpec as P

K = 8192


norm_eps = 1e-06


def sign_block(sign_hash_keys, first_row, row_count, col_ids):
    mult_row = sign_hash_keys[0] | 1
    mult_col = sign_hash_keys[1] | 1
    seed_add = sign_hash_keys[2]
    mix_mult = sign_hash_keys[3] | 1
    row_ids = first_row + lax.iota(jnp.int32, row_count)[:, None]
    hashed = row_ids * mult_row + col_ids[None, :] * mult_col + seed_add
    hashed = hashed ^ lax.shift_right_logical(hashed, jnp.full_like(hashed, 16))
    hashed = hashed * mix_mult
    hashed = hashed ^ lax.shift_right_logical(hashed, jnp.full_like(hashed, 13))
    hashed = hashed * jnp.int32(-1028477387)
    hashed = hashed ^ lax.shift_right_logical(hashed, jnp.full_like(hashed, 16))
    return jnp.where(hashed < 0, 1.0, -1.0).astype(jnp.bfloat16)


def butterfly_sum(values, axis, count):
    distance = 1
    while distance < count:
        pairs = [(j, j ^ distance) for j in range(count)]
        values = values + lax.ppermute(values, axis, pairs)
        distance *= 2
    return values


def local(adapter_gradients, sign_hash_keys, target_indices):
    resident_example, resident_rows = adapter_gradients.shape
    row_base = lax.axis_index("param") * jnp.int32(resident_rows)
    core = lax.axis_index("ec")
    swap = [(0, 1), (1, 0)]
    turn_count = 8
    rows_per_tile = resident_rows // turn_count
    scale_k = jnp.float32(K)
    param_count = lax.psum(1, "param")
    col_width = K // param_count
    half_width = col_width // 2

    unit = ((sign_hash_keys[3] | 1) & 1).astype(jnp.float32)
    partner = lax.ppermute(adapter_gradients.astype(jnp.float32), "ec", swap) * unit
    pair_gradients = jnp.concatenate([adapter_gradients, partner.astype(jnp.bfloat16)], axis=0)
    owner = lax.iota(jnp.int32, param_count)[:, None] * col_width
    col_ids = (owner + core * half_width + lax.iota(jnp.int32, half_width)[None, :]).reshape(-1)
    totals = None
    for tile in range(turn_count):
        start_offset = tile * rows_per_tile
        gradient_slab = pair_gradients[:, start_offset:start_offset + rows_per_tile]
        signs = sign_block(sign_hash_keys, row_base + start_offset, rows_per_tile, col_ids)
        term = jnp.dot(gradient_slab, signs, preferred_element_type=jnp.float32)
        totals = term if totals is None else totals + term

    pair_rows = 2 * resident_example
    blocks = totals.reshape(pair_rows, param_count, half_width)
    blocks = lax.all_to_all(blocks, "param", 1, 1, tiled=True)
    pair_projected = jnp.sum(blocks, axis=1)
    mine = pair_projected[:resident_example]
    theirs = lax.ppermute(pair_projected[resident_example:], "ec", swap)
    projected = jnp.where(core == 0, jnp.concatenate([mine, theirs], axis=1), jnp.concatenate([theirs, mine], axis=1))

    pool_rows = lax.all_gather(pair_projected, "ey", axis=0, tiled=True)
    wanted_core = (target_indices // resident_example) % 2
    positions = (target_indices // pair_rows) * pair_rows + (wanted_core ^ core) * resident_example + target_indices % resident_example
    target_rows = jnp.take(pool_rows, positions, axis=0)
    partial_dots = jnp.dot(pair_projected, target_rows.T, precision=lax.Precision.HIGHEST)
    pair_squares = jnp.sum(pair_projected * pair_projected, axis=1)
    target_squares = jnp.sum(target_rows * target_rows, axis=1)
    outgoing = jnp.concatenate([partial_dots[resident_example:].reshape(-1), pair_squares[resident_example:], target_squares])
    kept = jnp.concatenate([partial_dots[:resident_example].reshape(-1), pair_squares[:resident_example], target_squares])
    packed = kept + lax.ppermute(outgoing, "ec", swap)
    packed = butterfly_sum(packed, "param", param_count)
    dot_count = resident_example * target_rows.shape[0]
    dots = packed[:dot_count].reshape(resident_example, target_rows.shape[0])
    total_sq = packed[dot_count:dot_count + resident_example]
    target_sq = packed[dot_count + resident_example:]
    own_scale = jnp.sqrt(scale_k / (total_sq + norm_eps))
    target_scale = jnp.sqrt(scale_k / (target_sq + norm_eps))
    features = projected * own_scale[:, None]
    scores = dots * own_scale[:, None] * target_scale[None, :] / scale_k
    return (features, scores)


def solution(mesh):
    devices = mesh.devices
    pair_mesh = Mesh(devices.reshape(devices.shape[0], devices.shape[1] // 2, 2), ("param", "ey", "ec"))
    return jax.shard_map(
        local,
        mesh=pair_mesh,
        in_specs=(P(("ey", "ec"), "param"), P(), P()),
        out_specs=(P(("ey", "ec"), "param"), P(("ey", "ec"), None)),
        check_vma=False,
    )
```

profile of v0, /device:TPU:1, one launch (start us, length us, event | category | flops | bytes accessed | tf_op | source)
XLA Modules:
  0.0 153.5 jit_solution(640969799844968073)
XLA Ops:
  1.7 8.8 %collective-permute-start = (f32[32,4096]{1,0:T(8,128)S(1)}, f32[32,4096]{1,0:T(8,128)S(1)}, u32[]{:S(2)}, u32[]{:S(2)}) collective-permute-start(f32[32,4096]{1,0:T(8,128)S(1)} %convert_element_type.33), channel_id=1, source_target_pairs={{0,1},{1,0},{2,3},{3,2},{4,5},{5,4},{6,7},{7,6},{8,9},{9,8},{10,11... | collective-permute-start | bytes 1572872 | tf_op jit(solution)/shard_map/ppermute | solution.py:49
  10.5 1.4 fusion.177
  14.1 4.3 %fusion.87 = f32[64,4096]{1,0:T(8,128)S(1)} fusion(s32[]{:T(128)} %bitcast, s32[]{:T(128)} %bitcast.4, s32[4096]{0:T(1024)S(1)} %multiply_bitcast_fusion, s32[512]{0:T(512)S(1)} %get-tuple-element.23, bf16[32,4096]{1,0:T(8,128)(2,1)S(1)} %copy-done, bf16[32,4096]{1,0:T(8,128)(2,1)S(1)} %multiply_convert_fusion), kind=kOutput, calls=%fused_computation.127 | convolution fusion | flops 295829504 | bytes 1591304 | tf_op jit(solution)/shard_map/dot_general | solution.py:58
  18.4 4.3 %convolution_add_fusion.6 = f32[64,4096]{1,0:T(8,128)S(1)} fusion(f32[64,4096]{1,0:T(8,128)S(1)} %fusion.87, s32[512]{0:T(512)S(1)} %get-tuple-element.22, s32[]{:T(128)} %bitcast, s32[]{:T(128)} %bitcast.4, s32[4096]{0:T(1024)S(1)} %multiply_bitcast_fusion, bf16[32,4096]{1,0:T(8,128)(2,1)S(1)} %copy-done, bf16[32,4096]{1,0:T(8,128)(2,1)S(1)} %multiply_convert_fusion), kind=kOutput, calls=%fused_computation.63 | convolution fusion | flops 296091648 | bytes 2639880 | tf_op jit(solution)/shard_map/dot_general | solution.py:58
  22.7 4.3 %convolution_add_fusion.5 = f32[64,4096]{1,0:T(8,128)S(1)} fusion(f32[64,4096]{1,0:T(8,128)S(1)} %convolution_add_fusion.6, s32[512]{0:T(512)S(1)} %get-tuple-element.21, s32[]{:T(128)} %bitcast, s32[]{:T(128)} %bitcast.4, s32[4096]{0:T(1024)S(1)} %multiply_bitcast_fusion, bf16[32,4096]{1,0:T(8,128)(2,1)S(1)} %copy-done, ...), kind=kOutput, calls=%fused_computation.62 | convolution fusion | flops 296091648 | bytes 2639880 | tf_op jit(solution)/shard_map/dot_general | solution.py:58
  27.0 4.5 %convolution_add_fusion.4 = f32[64,4096]{1,0:T(8,128)S(1)} fusion(f32[64,4096]{1,0:T(8,128)S(1)} %convolution_add_fusion.5, s32[512]{0:T(512)S(1)} %get-tuple-element.20, s32[]{:T(128)} %bitcast, s32[]{:T(128)} %bitcast.4, s32[4096]{0:T(1024)S(1)} %multiply_bitcast_fusion, bf16[32,4096]{1,0:T(8,128)(2,1)S(1)} %copy-done, ...), kind=kOutput, calls=%fused_computation.61 | convolution fusion | flops 296091648 | bytes 2639880 | tf_op jit(solution)/shard_map/dot_general | solution.py:58
  31.5 4.3 %convolution_add_fusion.3 = f32[64,4096]{1,0:T(8,128)S(1)} fusion(f32[64,4096]{1,0:T(8,128)S(1)} %convolution_add_fusion.4, s32[512]{0:T(512)S(1)} %get-tuple-element.19, s32[]{:T(128)} %bitcast, s32[]{:T(128)} %bitcast.4, s32[4096]{0:T(1024)S(1)} %multiply_bitcast_fusion, bf16[32,4096]{1,0:T(8,128)(2,1)S(1)} %copy-done, ...), kind=kOutput, calls=%fused_computation.60 | convolution fusion | flops 296091648 | bytes 2639880 | tf_op jit(solution)/shard_map/dot_general | solution.py:58
  35.8 4.3 %convolution_add_fusion.2 = f32[64,4096]{1,0:T(8,128)S(1)} fusion(f32[64,4096]{1,0:T(8,128)S(1)} %convolution_add_fusion.3, s32[512]{0:T(512)S(1)} %get-tuple-element.18, s32[]{:T(128)} %bitcast, s32[]{:T(128)} %bitcast.4, s32[4096]{0:T(1024)S(1)} %multiply_bitcast_fusion, bf16[32,4096]{1,0:T(8,128)(2,1)S(1)} %copy-done, ...), kind=kOutput, calls=%fused_computation.59 | convolution fusion | flops 296091648 | bytes 2639880 | tf_op jit(solution)/shard_map/dot_general | solution.py:58
  40.2 4.5 %convolution_add_fusion.1 = f32[64,4096]{1,0:T(8,128)S(1)} fusion(f32[64,4096]{1,0:T(8,128)S(1)} %convolution_add_fusion.2, s32[512]{0:T(512)S(1)} %get-tuple-element.17, s32[]{:T(128)} %bitcast, s32[]{:T(128)} %bitcast.4, s32[4096]{0:T(1024)S(1)} %multiply_bitcast_fusion, bf16[32,4096]{1,0:T(8,128)(2,1)S(1)} %copy-done, ...), kind=kOutput, calls=%fused_computation.58 | convolution fusion | flops 296091648 | bytes 2639880 | tf_op jit(solution)/shard_map/dot_general | solution.py:58
  44.7 4.3 %fusion.88 = f32[8,32,8,128]{3,2,1,0:T(8,128)S(1)} fusion(f32[64,4096]{1,0:T(8,128)S(1)} %convolution_add_fusion.1, s32[512]{0:T(512)S(1)} %get-tuple-element.16, s32[]{:T(128)} %bitcast, s32[]{:T(128)} %bitcast.4, s32[4096]{0:T(1024)S(1)} %multiply_bitcast_fusion, bf16[32,4096]{1,0:T(8,128)(2,1)S(1)} %multiply_convert_fusion, bf16[32,4096]{1,0:T(8,128)(2,1)S(1)} %copy-done), kind=kOutput, calls=%fused_computation.128 | convolution fusion | flops 296091648 | bytes 2639880 | tf_op jit(solution)/shard_map/dot_general | solution.py:58
  50.1 7.6 %all-to-all-start = ((f32[64,32,128]{2,0,1:T(8,128)}), f32[64,32,128]{2,0,1:T(8,128)S(1)}, u32[]{:S(2)}, u32[]{:S(2)}) async-start(f32[64,32,128]{2,0,1:T(8,128)} %bitcast.17), calls=%async_computation | async-start | bytes 2097152 | tf_op jit(solution)/shard_map/all_to_all | solution.py:63
  57.8 25.7 %all-to-all-done = f32[64,32,128]{2,0,1:T(8,128)S(1)} async-done(((f32[64,32,128]{2,0,1:T(8,128)}), f32[64,32,128]{2,0,1:T(8,128)S(1)}, u32[]{:S(2)}, u32[]{:S(2)}) %all-to-all-start) | async-done | bytes 1048608 | tf_op jit(solution)/shard_map/all_to_all | solution.py:63
  83.6 20.4 %all_gather.3 = f32[512,128]{1,0:T(8,128)S(1)} all-gather(f32[64,128]{1,0:T(8,128)S(1)} %reduce_sum.27), channel_id=1, replica_groups=mesh['param'=32,'ey'=8,'ec'=2] {'ey'}, dimensions={0}, use_global_device_ids=true | all-gather | bytes 294912 | tf_op jit(solution)/shard_map/all_gather | solution.py:69
  105.5 11.7 %collective-permute-start.2 = (f32[8480]{0:T(1024)S(1)}, f32[8480]{0:T(1024)S(1)}, u32[]{:S(2)}, u32[]{:S(2)}) collective-permute-start(f32[8480]{0:T(1024)S(1)} %concatenate.19), channel_id=1, source_target_pairs={{0,1},{1,0},{2,3},{3,2},{4,5},{5,4},{6,7},{7,6},{8,9},{9,8},{10,11... | collective-permute-start | bytes 101768 | tf_op jit(solution)/shard_map/ppermute | solution.py:78
  118.1 2.9 %collective-permute-start.3 = (f32[8480]{0:T(1024)S(1)}, f32[8480]{0:T(1024)S(1)}, u32[]{:S(2)}, u32[]{:S(2)}) collective-permute-start(f32[8480]{0:T(1024)S(1)} %add.407), channel_id=1, source_target_pairs={{0,16},{16,0},{32,48},{48,32},{64,80},{80,64},{96,112},{112,96},{1... | collective-permute-start | bytes 101768 | tf_op jit(solution)/shard_map/ppermute | solution.py:31
  121.0 1.7 %collective-permute-done.3 = f32[8480]{0:T(1024)S(1)} collective-permute-done((f32[8480]{0:T(1024)S(1)}, f32[8480]{0:T(1024)S(1)}, u32[]{:S(2)}, u32[]{:S(2)}) %collective-permute-start.3) | collective-permute-done | bytes 33952 | tf_op jit(solution)/shard_map/ppermute | solution.py:31
  122.8 2.9 %collective-permute-start.4 = (f32[8480]{0:T(1024)S(1)}, f32[8480]{0:T(1024)S(1)}, u32[]{:S(2)}, u32[]{:S(2)}) collective-permute-start(f32[8480]{0:T(1024)S(1)} %add.408), channel_id=1, source_target_pairs={{0,32},{16,48},{32,0},{48,16},{64,96},{80,112},{96,64},{112,80},{1... | collective-permute-start | bytes 101768 | tf_op jit(solution)/shard_map/ppermute | solution.py:31
  125.6 2.7 %collective-permute-done.4 = f32[8480]{0:T(1024)S(1)} collective-permute-done((f32[8480]{0:T(1024)S(1)}, f32[8480]{0:T(1024)S(1)}, u32[]{:S(2)}, u32[]{:S(2)}) %collective-permute-start.4) | collective-permute-done | bytes 33952 | tf_op jit(solution)/shard_map/ppermute | solution.py:31
  128.3 3.5 %collective-permute-start.5 = (f32[8480]{0:T(1024)S(1)}, f32[8480]{0:T(1024)S(1)}, u32[]{:S(2)}, u32[]{:S(2)}) collective-permute-start(f32[8480]{0:T(1024)S(1)} %add.409), channel_id=1, source_target_pairs={{0,64},{16,80},{32,96},{48,112},{64,0},{80,16},{96,32},{112,48},{1... | collective-permute-start | bytes 101768 | tf_op jit(solution)/shard_map/ppermute | solution.py:31
  131.8 5.1 %collective-permute-done.5 = f32[8480]{0:T(1024)S(1)} collective-permute-done((f32[8480]{0:T(1024)S(1)}, f32[8480]{0:T(1024)S(1)}, u32[]{:S(2)}, u32[]{:S(2)}) %collective-permute-start.5) | collective-permute-done | bytes 33952 | tf_op jit(solution)/shard_map/ppermute | solution.py:31
  137.0 2.3 %collective-permute-start.6 = (f32[8480]{0:T(1024)S(1)}, f32[8480]{0:T(1024)S(1)}, u32[]{:S(2)}, u32[]{:S(2)}) collective-permute-start(f32[8480]{0:T(1024)S(1)} %add.410), channel_id=1, source_target_pairs={{0,128},{16,144},{32,160},{48,176},{64,192},{80,208},{96,224},{112... | collective-permute-start | bytes 101768 | tf_op jit(solution)/shard_map/ppermute | solution.py:31
  139.3 2.3 %collective-permute-done.6 = f32[8480]{0:T(1024)S(1)} collective-permute-done((f32[8480]{0:T(1024)S(1)}, f32[8480]{0:T(1024)S(1)}, u32[]{:S(2)}, u32[]{:S(2)}) %collective-permute-start.6) | collective-permute-done | bytes 33952 | tf_op jit(solution)/shard_map/ppermute | solution.py:31
  141.7 3.5 %collective-permute-start.7 = (f32[8480]{0:T(1024)S(1)}, f32[8480]{0:T(1024)S(1)}, u32[]{:S(2)}, u32[]{:S(2)}) collective-permute-start(f32[8480]{0:T(1024)S(1)} %add.411), channel_id=1, source_target_pairs={{0,256},{16,272},{32,288},{48,304},{64,320},{80,336},{96,352},{112... | collective-permute-start | bytes 101768 | tf_op jit(solution)/shard_map/ppermute | solution.py:31
  145.2 6.9 %collective-permute-start.1 = (f32[32,128]{1,0:T(8,128)S(1)}, f32[32,128]{1,0:T(8,128)S(1)}, u32[]{:S(2)}, u32[]{:S(2)}) collective-permute-start(f32[32,128]{1,0:T(8,128)S(1)} %get-tuple-element.7), channel_id=1, source_target_pairs={{0,1},{1,0},{2,3},{3,2},{4,5},{5,4},{6,7},{7,6},{8,9},{9,8},{10,11... | collective-permute-start | bytes 49160 | tf_op jit(solution)/shard_map/ppermute | solution.py:66
  (42 shorter events, 6.3 us)
Async XLA Ops:
  0.6 13.4 %copy-start = (bf16[32,4096]{1,0:T(8,128)(2,1)S(1)}, bf16[32,4096]{1,0:T(8,128)(2,1)}, u32[]{:S(2)}) copy-start(bf16[32,4096]{1,0:T(8,128)(2,1)} %param.3) | copy-start | bytes 786436
  1.7 12.3 %collective-permute-start = (f32[32,4096]{1,0:T(8,128)S(1)}, f32[32,4096]{1,0:T(8,128)S(1)}, u32[]{:S(2)}, u32[]{:S(2)}) collective-permute-start(f32[32,4096]{1,0:T(8,128)S(1)} %convert_element_type.33), channel_id=1, source_target_pairs={{0,1},{1,0},{2,3},{3,2},{4,5},{5,4},{6,7},{7,6},{8,9},{9,8},{10,11... | collective-permute-start | bytes 1572872 | tf_op jit(solution)/shard_map/ppermute | solution.py:49
  50.1 7.6 %copy-start.1 = (s32[256]{0:T(256)S(1)}, s32[256]{0:T(256)}, u32[]{:S(2)}) copy-start(s32[256]{0:T(256)} %param.5) | copy-start | bytes 3076
  50.1 33.4 %all-to-all-start = ((f32[64,32,128]{2,0,1:T(8,128)}), f32[64,32,128]{2,0,1:T(8,128)S(1)}, u32[]{:S(2)}, u32[]{:S(2)}) async-start(f32[64,32,128]{2,0,1:T(8,128)} %bitcast.17), calls=%async_computation | async-start | bytes 2097152 | tf_op jit(solution)/shard_map/all_to_all | solution.py:63
  105.5 12.5 %collective-permute-start.2 = (f32[8480]{0:T(1024)S(1)}, f32[8480]{0:T(1024)S(1)}, u32[]{:S(2)}, u32[]{:S(2)}) collective-permute-start(f32[8480]{0:T(1024)S(1)} %concatenate.19), channel_id=1, source_target_pairs={{0,1},{1,0},{2,3},{3,2},{4,5},{5,4},{6,7},{7,6},{8,9},{9,8},{10,11... | collective-permute-start | bytes 101768 | tf_op jit(solution)/shard_map/ppermute | solution.py:78
  118.1 4.7 %collective-permute-start.3 = (f32[8480]{0:T(1024)S(1)}, f32[8480]{0:T(1024)S(1)}, u32[]{:S(2)}, u32[]{:S(2)}) collective-permute-start(f32[8480]{0:T(1024)S(1)} %add.407), channel_id=1, source_target_pairs={{0,16},{16,0},{32,48},{48,32},{64,80},{80,64},{96,112},{112,96},{1... | collective-permute-start | bytes 101768 | tf_op jit(solution)/shard_map/ppermute | solution.py:31
  122.8 5.6 %collective-permute-start.4 = (f32[8480]{0:T(1024)S(1)}, f32[8480]{0:T(1024)S(1)}, u32[]{:S(2)}, u32[]{:S(2)}) collective-permute-start(f32[8480]{0:T(1024)S(1)} %add.408), channel_id=1, source_target_pairs={{0,32},{16,48},{32,0},{48,16},{64,96},{80,112},{96,64},{112,80},{1... | collective-permute-start | bytes 101768 | tf_op jit(solution)/shard_map/ppermute | solution.py:31
  128.3 8.6 %collective-permute-start.5 = (f32[8480]{0:T(1024)S(1)}, f32[8480]{0:T(1024)S(1)}, u32[]{:S(2)}, u32[]{:S(2)}) collective-permute-start(f32[8480]{0:T(1024)S(1)} %add.409), channel_id=1, source_target_pairs={{0,64},{16,80},{32,96},{48,112},{64,0},{80,16},{96,32},{112,48},{1... | collective-permute-start | bytes 101768 | tf_op jit(solution)/shard_map/ppermute | solution.py:31
  137.0 4.7 %collective-permute-start.6 = (f32[8480]{0:T(1024)S(1)}, f32[8480]{0:T(1024)S(1)}, u32[]{:S(2)}, u32[]{:S(2)}) collective-permute-start(f32[8480]{0:T(1024)S(1)} %add.410), channel_id=1, source_target_pairs={{0,128},{16,144},{32,160},{48,176},{64,192},{80,208},{96,224},{112... | collective-permute-start | bytes 101768 | tf_op jit(solution)/shard_map/ppermute | solution.py:31
  141.7 10.4 %collective-permute-start.7 = (f32[8480]{0:T(1024)S(1)}, f32[8480]{0:T(1024)S(1)}, u32[]{:S(2)}, u32[]{:S(2)}) collective-permute-start(f32[8480]{0:T(1024)S(1)} %add.411), channel_id=1, source_target_pairs={{0,256},{16,272},{32,288},{48,304},{64,320},{80,336},{96,352},{112... | collective-permute-start | bytes 101768 | tf_op jit(solution)/shard_map/ppermute | solution.py:31
  145.2 7.7 %collective-permute-start.1 = (f32[32,128]{1,0:T(8,128)S(1)}, f32[32,128]{1,0:T(8,128)S(1)}, u32[]{:S(2)}, u32[]{:S(2)}) collective-permute-start(f32[32,128]{1,0:T(8,128)S(1)} %get-tuple-element.7), channel_id=1, source_target_pairs={{0,1},{1,0},{2,3},{3,2},{4,5},{5,4},{6,7},{7,6},{8,9},{9,8},{10,11... | collective-permute-start | bytes 49160 | tf_op jit(solution)/shard_map/ppermute | solution.py:66
where the time goes:
time: 154 us
  starting transfers between devices  50 us (32%)
  waiting for transfers between devices  39 us (25%)
  matrix products  35.3 us (23%)
  blocking collectives  20.4 us (13%)
  local copies, waits for them, and re-layouts  3.56 us (2%)
  between operations  2.85 us (2%)
  other arithmetic  2.42 us (2%)
    dot_general x8, matrix products, local(): term = jnp.dot(gradient_slab, signs, preferred_element_type=jnp.float32)  34.9 us
    all_to_all x1, waiting for transfers between devices, local(): blocks = lax.all_to_all(blocks, 'param', 1, 1, tiled=True)  25.7 us
    all_gather x1, blocking collectives, local(): pool_rows = lax.all_gather(pair_projected, 'ey', axis=0, tiled=True)  20.4 us
    ppermute x5, starting transfers between devices, butterfly_sum(): values = values + lax.ppermute(values, axis, pairs)  15.1 us
    ppermute x5, waiting for transfers between devices, butterfly_sum(): values = values + lax.ppermute(values, axis, pairs)  12 us
    ppermute x1, starting transfers between devices, local(): packed = kept + lax.ppermute(outgoing, 'ec', swap)  11.7 us
    ppermute x1, starting transfers between devices, local(): lax.ppermute(adapter_gradients.astype(jnp.float32), 'ec', swap) * unit  8.79 us
    all_to_all x1, starting transfers between devices, local(): blocks = lax.all_to_all(blocks, 'param', 1, 1, tiled=True)  7.64 us
  transfers between devices with their start and end apart: 9, of which 7 were waited for; matrix products, arithmetic and copies ran while one was open for 1% of the time, Pallas kernels for 0%

commit v1 on v0

--- a/solution.py
+++ b/solution.py
@@ -47,7 +47,12 @@
 
     unit = ((sign_hash_keys[3] | 1) & 1).astype(jnp.float32)
     partner = lax.ppermute(adapter_gradients.astype(jnp.float32), "ec", swap) * unit
-    pair_gradients = jnp.concatenate([adapter_gradients, partner.astype(jnp.bfloat16)], axis=0)
+    partner = partner.astype(jnp.bfloat16)
+    pair_gradients = jnp.where(
+        core == 0,
+        jnp.concatenate([adapter_gradients, partner], axis=0),
+        jnp.concatenate([partner, adapter_gradients], axis=0),
+    )
     owner = lax.iota(jnp.int32, param_count)[:, None] * col_width
     col_ids = (owner + core * half_width + lax.iota(jnp.int32, half_width)[None, :]).reshape(-1)
     totals = None
@@ -58,27 +63,21 @@
         term = jnp.dot(gradient_slab, signs, preferred_element_type=jnp.float32)
         totals = term if totals is None else totals + term
 
-    pair_rows = 2 * resident_example
-    blocks = totals.reshape(pair_rows, param_count, half_width)
-    blocks = lax.all_to_all(blocks, "param", 1, 1, tiled=True)
-    pair_projected = jnp.sum(blocks, axis=1)
-    mine = pair_projected[:resident_example]
-    theirs = lax.ppermute(pair_projected[resident_example:], "ec", swap)
-    projected = jnp.where(core == 0, jnp.concatenate([mine, theirs], axis=1), jnp.concatenate([theirs, mine], axis=1))
+    blocks = totals.reshape(2, resident_example, param_count, half_width)
+    blocks = jnp.transpose(blocks, (2, 0, 1, 3)).reshape(2 * param_count, resident_example, half_width)
+    blocks = lax.all_to_all(blocks, ("param", "ec"), 0, 0, tiled=True)
+    blocks = jnp.sum(blocks.reshape(param_count, 2, resident_example, half_width), axis=0)
+    projected = jnp.transpose(blocks, (1, 0, 2)).reshape(resident_example, col_width)
 
-    pool_rows = lax.all_gather(pair_projected, "ey", axis=0, tiled=True)
-    wanted_core = (target_indices // resident_example) % 2
-    positions = (target_indices // pair_rows) * pair_rows + (wanted_core ^ core) * resident_example + target_indices % resident_example
-    target_rows = jnp.take(pool_rows, positions, axis=0)
-    partial_dots = jnp.dot(pair_projected, target_rows.T, precision=lax.Precision.HIGHEST)
-    pair_squares = jnp.sum(pair_projected * pair_projected, axis=1)
+    pool_rows = lax.all_gather(projected, ("ey", "ec"), axis=0, tiled=True)
+    target_rows = jnp.take(pool_rows, target_indices, axis=0)
+    partial_dots = jnp.dot(projected, target_rows.T, precision=lax.Precision.HIGHEST)
+    own_squares = jnp.sum(projected * projected, axis=1)
     target_squares = jnp.sum(target_rows * target_rows, axis=1)
-    outgoing = jnp.concatenate([partial_dots[resident_example:].reshape(-1), pair_squares[resident_example:], target_squares])
-    kept = jnp.concatenate([partial_dots[:resident_example].reshape(-1), pair_squares[:resident_example], target_squares])
-    packed = kept + lax.ppermute(outgoing, "ec", swap)
+    packed = jnp.concatenate([partial_dots.reshape(-1), own_squares, target_squares])
     packed = butterfly_sum(packed, "param", param_count)
-    dot_count = resident_example * target_rows.shape[0]
-    dots = packed[:dot_count].reshape(resident_example, target_rows.shape[0])
+    dot_count = partial_dots.size
+    dots = packed[:dot_count].reshape(partial_dots.shape)
     total_sq = packed[dot_count:dot_count + resident_example]
     target_sq = packed[dot_count + resident_example:]
     own_scale = jnp.sqrt(scale_k / (total_sq + norm_eps))

time: 154 us -> 143 us (0.929)
  the two profiles are of different devices: /device:TPU:1 before, /device:TPU:2 now
where the time goes in v1:
time: 143 us
  waiting for transfers between devices  41.8 us (29%)
  starting transfers between devices  36.8 us (26%)
  matrix products  35.3 us (25%)
  blocking collectives  19 us (13%)
  local copies, waits for them, and re-layouts  4.33 us (3%)
  between operations  2.89 us (2%)
  other arithmetic  2.49 us (2%)
    dot_general x8, matrix products, local(): term = jnp.dot(gradient_slab, signs, preferred_element_type=jnp.float32)  34.9 us
    all_to_all x1, waiting for transfers between devices, local(): blocks = lax.all_to_all(blocks, ('param', 'ec'), 0, 0, tiled=True)  27.1 us
    ppermute x5, starting transfers between devices, butterfly_sum(): values = values + lax.ppermute(values, axis, pairs)  20.8 us
    all_gather x1, blocking collectives, local(): pool_rows = lax.all_gather(projected, ('ey', 'ec'), axis=0, tiled=True)  19 us
    ppermute x5, waiting for transfers between devices, butterfly_sum(): values = values + lax.ppermute(values, axis, pairs)  14.7 us
    all_to_all x1, starting transfers between devices, local(): blocks = lax.all_to_all(blocks, ('param', 'ec'), 0, 0, tiled=True)  14.1 us
  transfers between devices with their start and end apart: 7, of which 6 were waited for; matrix products, arithmetic and copies ran while one was open for 1% of the time, Pallas kernels for 0%

profile of v1, /device:TPU:2, one launch (start us, length us, event | category | flops | bytes accessed | tf_op | source)
XLA Modules:
  0.0 142.6 jit_solution(14755766650671167249)
XLA Ops:
  1.7 1.9 %collective-permute-start = (f32[32,4096]{1,0:T(8,128)S(1)}, f32[32,4096]{1,0:T(8,128)S(1)}, u32[]{:S(2)}, u32[]{:S(2)}) collective-permute-start(f32[32,4096]{1,0:T(8,128)S(1)} %convert_element_type.33), channel_id=1, source_target_pairs={{0,1},{1,0},{2,3},{3,2},{4,5},{5,4},{6,7},{7,6},{8,9},{9,8},{10,11... | collective-permute-start | bytes 1572872 | tf_op jit(solution)/shard_map/ppermute | solution.py:49
  3.6 1.5 %fusion.154 = (s32[1]{0:T(128)}, s32[1]{0:T(128)}, s32[1]{0:T(128)}, s32[1]{0:T(128)}) fusion(s32[4]{0:T(128)} %param.4), kind=kLoop, calls=%fused_computation.217 | loop fusion | bytes 32 | tf_op jit(solution)/shard_map/slice | solution.py:13
  7.4 4.3 %fusion.87 = f32[64,4096]{1,0:T(8,128)S(1)} fusion(s32[]{:T(128)} %bitcast, s32[]{:T(128)} %bitcast.4, s32[4096]{0:T(1024)S(1)} %multiply_bitcast_fusion, s32[512]{0:T(512)S(1)} %get-tuple-element.15, bf16[64,4096]{1,0:T(8,128)(2,1)S(1)} %maximum_select_fusion), kind=kOutput, calls=%fused_computation.127 | convolution fusion | flops 295698432 | bytes 1132552 | tf_op jit(solution)/shard_map/dot_general | solution.py:63
  11.7 4.3 %convolution_add_fusion.6 = f32[64,4096]{1,0:T(8,128)S(1)} fusion(f32[64,4096]{1,0:T(8,128)S(1)} %fusion.87, s32[512]{0:T(512)S(1)} %get-tuple-element.14, s32[]{:T(128)} %bitcast, s32[]{:T(128)} %bitcast.4, s32[4096]{0:T(1024)S(1)} %multiply_bitcast_fusion, bf16[64,4096]{1,0:T(8,128)(2,1)S(1)} %maximum_select_fusion), kind=kOutput, calls=%fused_computation.63 | convolution fusion | flops 295960576 | bytes 2181128 | tf_op jit(solution)/shard_map/dot_general | solution.py:63
  16.0 4.3 %convolution_add_fusion.5 = f32[64,4096]{1,0:T(8,128)S(1)} fusion(f32[64,4096]{1,0:T(8,128)S(1)} %convolution_add_fusion.6, s32[512]{0:T(512)S(1)} %get-tuple-element.13, s32[]{:T(128)} %bitcast, s32[]{:T(128)} %bitcast.4, s32[4096]{0:T(1024)S(1)} %multiply_bitcast_fusion, bf16[64,4096]{1,0:T(8,128)(2,1)S(1)} %maximum_select_fusion), kind=kOutput, calls=%fused_computation.62 | convolution fusion | flops 295960576 | bytes 2181128 | tf_op jit(solution)/shard_map/dot_general | solution.py:63
  20.3 4.5 %convolution_add_fusion.4 = f32[64,4096]{1,0:T(8,128)S(1)} fusion(f32[64,4096]{1,0:T(8,128)S(1)} %convolution_add_fusion.5, s32[512]{0:T(512)S(1)} %get-tuple-element.12, s32[]{:T(128)} %bitcast, s32[]{:T(128)} %bitcast.4, s32[4096]{0:T(1024)S(1)} %multiply_bitcast_fusion, bf16[64,4096]{1,0:T(8,128)(2,1)S(1)} %maximum_select_fusion), kind=kOutput, calls=%fused_computation.61 | convolution fusion | flops 295960576 | bytes 2181128 | tf_op jit(solution)/shard_map/dot_general | solution.py:63
  24.8 4.3 %convolution_add_fusion.3 = f32[64,4096]{1,0:T(8,128)S(1)} fusion(f32[64,4096]{1,0:T(8,128)S(1)} %convolution_add_fusion.4, s32[512]{0:T(512)S(1)} %get-tuple-element.11, s32[]{:T(128)} %bitcast, s32[]{:T(128)} %bitcast.4, s32[4096]{0:T(1024)S(1)} %multiply_bitcast_fusion, bf16[64,4096]{1,0:T(8,128)(2,1)S(1)} %maximum_select_fusion), kind=kOutput, calls=%fused_computation.60 | convolution fusion | flops 295960576 | bytes 2181128 | tf_op jit(solution)/shard_map/dot_general | solution.py:63
  29.1 4.3 %convolution_add_fusion.2 = f32[64,4096]{1,0:T(8,128)S(1)} fusion(f32[64,4096]{1,0:T(8,128)S(1)} %convolution_add_fusion.3, s32[512]{0:T(512)S(1)} %get-tuple-element.10, s32[]{:T(128)} %bitcast, s32[]{:T(128)} %bitcast.4, s32[4096]{0:T(1024)S(1)} %multiply_bitcast_fusion, bf16[64,4096]{1,0:T(8,128)(2,1)S(1)} %maximum_select_fusion), kind=kOutput, calls=%fused_computation.59 | convolution fusion | flops 295960576 | bytes 2181128 | tf_op jit(solution)/shard_map/dot_general | solution.py:63
  33.5 4.5 %convolution_add_fusion.1 = f32[64,4096]{1,0:T(8,128)S(1)} fusion(f32[64,4096]{1,0:T(8,128)S(1)} %convolution_add_fusion.2, s32[512]{0:T(512)S(1)} %get-tuple-element.9, s32[]{:T(128)} %bitcast, s32[]{:T(128)} %bitcast.4, s32[4096]{0:T(1024)S(1)} %multiply_bitcast_fusion, bf16[64,4096]{1,0:T(8,128)(2,1)S(1)} %maximum_select_fusion), kind=kOutput, calls=%fused_computation.58 | convolution fusion | flops 295960576 | bytes 2181128 | tf_op jit(solution)/shard_map/dot_general | solution.py:63
  38.0 4.3 %fusion.88 = f32[8,8,32,128]{3,1,2,0:T(8,128)S(1)} fusion(f32[64,4096]{1,0:T(8,128)S(1)} %convolution_add_fusion.1, s32[512]{0:T(512)S(1)} %get-tuple-element.8, s32[]{:T(128)} %bitcast, s32[]{:T(128)} %bitcast.4, s32[4096]{0:T(1024)S(1)} %multiply_bitcast_fusion, bf16[64,4096]{1,0:T(8,128)(2,1)S(1)} %maximum_select_fusion), kind=kOutput, calls=%fused_computation.128 | convolution fusion | flops 295960576 | bytes 2181128 | tf_op jit(solution)/shard_map/dot_general | solution.py:63
  42.5 1.6 %copy.6 = f32[2,32,32,128]{3,1,0,2:T(8,128)} copy(f32[2,32,32,128]{3,2,1,0:T(8,128)S(1)} %bitcast.35) | data formatting | bytes 2097152 | tf_op jit(solution)/shard_map/reshape | solution.py:66
  44.1 14.1 %all-to-all-start = ((f32[64,32,128]{2,1,0:T(8,128)}), f32[64,32,128]{2,1,0:T(8,128)S(1)}, u32[]{:S(2)}, u32[]{:S(2)}) async-start(f32[64,32,128]{2,1,0:T(8,128)} %bitcast.6), calls=%async_computation | async-start | bytes 2097152 | tf_op jit(solution)/shard_map/all_to_all | solution.py:68
  58.3 27.1 %all-to-all-done = f32[64,32,128]{2,1,0:T(8,128)S(1)} async-done(((f32[64,32,128]{2,1,0:T(8,128)}), f32[64,32,128]{2,1,0:T(8,128)S(1)}, u32[]{:S(2)}, u32[]{:S(2)}) %all-to-all-start) | async-done | bytes 1048608 | tf_op jit(solution)/shard_map/all_to_all | solution.py:68
  85.4 19.0 %all_gather.3 = f32[512,256]{1,0:T(8,128)S(1)} all-gather(f32[32,256]{1,0:T(8,128)S(1)} %copy_bitcast_fusion), channel_id=1, replica_groups=mesh['param'=32,'ey'=8,'ec'=2] {'ey','ec'}, dimensions={0}, use_global_device_ids=true | all-gather | bytes 557056 | tf_op jit(solution)/shard_map/all_gather | solution.py:72
  106.2 3.3 %collective-permute-start.1 = (f32[8480]{0:T(1024)S(1)}, f32[8480]{0:T(1024)S(1)}, u32[]{:S(2)}, u32[]{:S(2)}) collective-permute-start(f32[8480]{0:T(1024)S(1)} %concatenate.11), channel_id=1, source_target_pairs={{0,16},{16,0},{32,48},{48,32},{64,80},{80,64},{96,112},{112,96},{1... | collective-permute-start | bytes 101768 | tf_op jit(solution)/shard_map/ppermute | solution.py:31
  109.5 2.6 %collective-permute-done.1 = f32[8480]{0:T(1024)S(1)} collective-permute-done((f32[8480]{0:T(1024)S(1)}, f32[8480]{0:T(1024)S(1)}, u32[]{:S(2)}, u32[]{:S(2)}) %collective-permute-start.1) | collective-permute-done | bytes 33952 | tf_op jit(solution)/shard_map/ppermute | solution.py:31
  112.1 4.8 %collective-permute-start.2 = (f32[8480]{0:T(1024)S(1)}, f32[8480]{0:T(1024)S(1)}, u32[]{:S(2)}, u32[]{:S(2)}) collective-permute-start(f32[8480]{0:T(1024)S(1)} %add.382), channel_id=1, source_target_pairs={{0,32},{16,48},{32,0},{48,16},{64,96},{80,112},{96,64},{112,80},{1... | collective-permute-start | bytes 101768 | tf_op jit(solution)/shard_map/ppermute | solution.py:31
  116.9 1.9 %collective-permute-done.2 = f32[8480]{0:T(1024)S(1)} collective-permute-done((f32[8480]{0:T(1024)S(1)}, f32[8480]{0:T(1024)S(1)}, u32[]{:S(2)}, u32[]{:S(2)}) %collective-permute-start.2) | collective-permute-done | bytes 33952 | tf_op jit(solution)/shard_map/ppermute | solution.py:31
  118.8 5.2 %collective-permute-start.3 = (f32[8480]{0:T(1024)S(1)}, f32[8480]{0:T(1024)S(1)}, u32[]{:S(2)}, u32[]{:S(2)}) collective-permute-start(f32[8480]{0:T(1024)S(1)} %add.383), channel_id=1, source_target_pairs={{0,64},{16,80},{32,96},{48,112},{64,0},{80,16},{96,32},{112,48},{1... | collective-permute-start | bytes 101768 | tf_op jit(solution)/shard_map/ppermute | solution.py:31
  124.1 4.5 %collective-permute-done.3 = f32[8480]{0:T(1024)S(1)} collective-permute-done((f32[8480]{0:T(1024)S(1)}, f32[8480]{0:T(1024)S(1)}, u32[]{:S(2)}, u32[]{:S(2)}) %collective-permute-start.3) | collective-permute-done | bytes 33952 | tf_op jit(solution)/shard_map/ppermute | solution.py:31
  128.6 3.4 %collective-permute-start.4 = (f32[8480]{0:T(1024)S(1)}, f32[8480]{0:T(1024)S(1)}, u32[]{:S(2)}, u32[]{:S(2)}) collective-permute-start(f32[8480]{0:T(1024)S(1)} %add.384), channel_id=1, source_target_pairs={{0,128},{16,144},{32,160},{48,176},{64,192},{80,208},{96,224},{112... | collective-permute-start | bytes 101768 | tf_op jit(solution)/shard_map/ppermute | solution.py:31
  132.1 2.4 %collective-permute-done.4 = f32[8480]{0:T(1024)S(1)} collective-permute-done((f32[8480]{0:T(1024)S(1)}, f32[8480]{0:T(1024)S(1)}, u32[]{:S(2)}, u32[]{:S(2)}) %collective-permute-start.4) | collective-permute-done | bytes 33952 | tf_op jit(solution)/shard_map/ppermute | solution.py:31
  134.5 4.0 %collective-permute-start.5 = (f32[8480]{0:T(1024)S(1)}, f32[8480]{0:T(1024)S(1)}, u32[]{:S(2)}, u32[]{:S(2)}) collective-permute-start(f32[8480]{0:T(1024)S(1)} %add.385), channel_id=1, source_target_pairs={{0,256},{16,272},{32,288},{48,304},{64,320},{80,336},{96,352},{112... | collective-permute-start | bytes 101768 | tf_op jit(solution)/shard_map/ppermute | solution.py:31
  138.5 3.3 %collective-permute-done.5 = f32[8480]{0:T(1024)S(1)} collective-permute-done((f32[8480]{0:T(1024)S(1)}, f32[8480]{0:T(1024)S(1)}, u32[]{:S(2)}, u32[]{:S(2)}) %collective-permute-start.5) | collective-permute-done | bytes 33952 | tf_op jit(solution)/shard_map/ppermute | solution.py:31
  (36 shorter events, 4.2 us)
Async XLA Ops:
  0.6 6.6 %copy-start = (bf16[32,4096]{1,0:T(8,128)(2,1)S(1)}, bf16[32,4096]{1,0:T(8,128)(2,1)}, u32[]{:S(2)}) copy-start(bf16[32,4096]{1,0:T(8,128)(2,1)} %param.3) | copy-start | bytes 786436
  1.7 5.5 %collective-permute-start = (f32[32,4096]{1,0:T(8,128)S(1)}, f32[32,4096]{1,0:T(8,128)S(1)}, u32[]{:S(2)}, u32[]{:S(2)}) collective-permute-start(f32[32,4096]{1,0:T(8,128)S(1)} %convert_element_type.33), channel_id=1, source_target_pairs={{0,1},{1,0},{2,3},{3,2},{4,5},{5,4},{6,7},{7,6},{8,9},{9,8},{10,11... | collective-permute-start | bytes 1572872 | tf_op jit(solution)/shard_map/ppermute | solution.py:49
  44.1 14.1 %copy-start.1 = (s32[256]{0:T(256)S(1)}, s32[256]{0:T(256)}, u32[]{:S(2)}) copy-start(s32[256]{0:T(256)} %param.5) | copy-start | bytes 3076
  44.1 41.3 %all-to-all-start = ((f32[64,32,128]{2,1,0:T(8,128)}), f32[64,32,128]{2,1,0:T(8,128)S(1)}, u32[]{:S(2)}, u32[]{:S(2)}) async-start(f32[64,32,128]{2,1,0:T(8,128)} %bitcast.6), calls=%async_computation | async-start | bytes 2097152 | tf_op jit(solution)/shard_map/all_to_all | solution.py:68
  106.2 5.8 %collective-permute-start.1 = (f32[8480]{0:T(1024)S(1)}, f32[8480]{0:T(1024)S(1)}, u32[]{:S(2)}, u32[]{:S(2)}) collective-permute-start(f32[8480]{0:T(1024)S(1)} %concatenate.11), channel_id=1, source_target_pairs={{0,16},{16,0},{32,48},{48,32},{64,80},{80,64},{96,112},{112,96},{1... | collective-permute-start | bytes 101768 | tf_op jit(solution)/shard_map/ppermute | solution.py:31
  112.1 6.7 %collective-permute-start.2 = (f32[8480]{0:T(1024)S(1)}, f32[8480]{0:T(1024)S(1)}, u32[]{:S(2)}, u32[]{:S(2)}) collective-permute-start(f32[8480]{0:T(1024)S(1)} %add.382), channel_id=1, source_target_pairs={{0,32},{16,48},{32,0},{48,16},{64,96},{80,112},{96,64},{112,80},{1... | collective-permute-start | bytes 101768 | tf_op jit(solution)/shard_map/ppermute | solution.py:31
  118.8 9.7 %collective-permute-start.3 = (f32[8480]{0:T(1024)S(1)}, f32[8480]{0:T(1024)S(1)}, u32[]{:S(2)}, u32[]{:S(2)}) collective-permute-start(f32[8480]{0:T(1024)S(1)} %add.383), channel_id=1, source_target_pairs={{0,64},{16,80},{32,96},{48,112},{64,0},{80,16},{96,32},{112,48},{1... | collective-permute-start | bytes 101768 | tf_op jit(solution)/shard_map/ppermute | solution.py:31
  128.6 5.8 %collective-permute-start.4 = (f32[8480]{0:T(1024)S(1)}, f32[8480]{0:T(1024)S(1)}, u32[]{:S(2)}, u32[]{:S(2)}) collective-permute-start(f32[8480]{0:T(1024)S(1)} %add.384), channel_id=1, source_target_pairs={{0,128},{16,144},{32,160},{48,176},{64,192},{80,208},{96,224},{112... | collective-permute-start | bytes 101768 | tf_op jit(solution)/shard_map/ppermute | solution.py:31
  134.5 7.3 %collective-permute-start.5 = (f32[8480]{0:T(1024)S(1)}, f32[8480]{0:T(1024)S(1)}, u32[]{:S(2)}, u32[]{:S(2)}) collective-permute-start(f32[8480]{0:T(1024)S(1)} %add.385), channel_id=1, source_target_pairs={{0,256},{16,272},{32,288},{48,304},{64,320},{80,336},{96,352},{112... | collective-permute-start | bytes 101768 | tf_op jit(solution)/shard_map/ppermute | solution.py:31

commit v2 on v1

--- a/solution.py
+++ b/solution.py
@@ -14,14 +14,16 @@
     mult_col = sign_hash_keys[1] | 1
     seed_add = sign_hash_keys[2]
     mix_mult = sign_hash_keys[3] | 1
-    row_ids = first_row + lax.iota(jnp.int32, row_count)[:, None]
-    hashed = row_ids * mult_row + col_ids[None, :] * mult_col + seed_add
+    row_ids = first_row + lax.iota(jnp.int32, row_count)
+    row_terms = row_ids * mult_row + seed_add
+    col_terms = col_ids * mult_col
+    hashed = row_terms[:, None] + col_terms[None, :]
     hashed = hashed ^ lax.shift_right_logical(hashed, jnp.full_like(hashed, 16))
     hashed = hashed * mix_mult
     hashed = hashed ^ lax.shift_right_logical(hashed, jnp.full_like(hashed, 13))
     hashed = hashed * jnp.int32(-1028477387)
     hashed = hashed ^ lax.shift_right_logical(hashed, jnp.full_like(hashed, 16))
-    return jnp.where(hashed < 0, 1.0, -1.0).astype(jnp.bfloat16)
+    return jnp.where(hashed < 0, jnp.bfloat16(1.0), jnp.bfloat16(-1.0))
 
 
 def butterfly_sum(values, axis, count):

time: 143 us -> 139 us (0.972)
  matrix products: 35.3 us -> 28.7 us
  other arithmetic: 2.49 us -> 5.2 us
    dot_general x8, matrix products: 34.9 us -> 28.3 us  [local(): term = jnp.dot(gradient_slab, signs, preferred_element_type=jnp.float32)]
    add x0 -> x4, other arithmetic: none -> 2.74 us  [sign_block(): row_terms = row_ids * mult_row + seed_add]
  transfers between devices with their start and end apart: 7 -> 7, of which waited for: 6 -> 6; matrix products, arithmetic and copies ran while one was open for 1% -> 3% of each run, Pallas kernels for 0% -> 0%
where the time goes in v2:
time: 139 us
  waiting for transfers between devices  41.8 us (30%)
  starting transfers between devices  36.8 us (26%)
  matrix products  28.7 us (21%)
  blocking collectives  19 us (14%)
  other arithmetic  5.2 us (4%)
  local copies, waits for them, and re-layouts  4.33 us (3%)
  between operations  2.76 us (2%)
    dot_general x8, matrix products, local(): term = jnp.dot(gradient_slab, signs, preferred_element_type=jnp.float32)  28.3 us
    all_to_all x1, waiting for transfers between devices, local(): blocks = lax.all_to_all(blocks, ('param', 'ec'), 0, 0, tiled=True)  27.1 us
    ppermute x5, starting transfers between devices, butterfly_sum(): values = values + lax.ppermute(values, axis, pairs)  20.8 us
    all_gather x1, blocking collectives, local(): pool_rows = lax.all_gather(projected, ('ey', 'ec'), axis=0, tiled=True)  19 us
    ppermute x5, waiting for transfers between devices, butterfly_sum(): values = values + lax.ppermute(values, axis, pairs)  14.7 us
    all_to_all x1, starting transfers between devices, local(): blocks = lax.all_to_all(blocks, ('param', 'ec'), 0, 0, tiled=True)  14.1 us
  transfers between devices with their start and end apart: 7, of which 6 were waited for; matrix products, arithmetic and copies ran while one was open for 3% of the time, Pallas kernels for 0%

profile of v2, /device:TPU:2, one launch (start us, length us, event | category | flops | bytes accessed | tf_op | source)
XLA Modules:
  0.0 138.6 jit_solution(7590507115831629570)
XLA Ops:
  1.7 1.9 %collective-permute-start = (f32[32,4096]{1,0:T(8,128)S(1)}, f32[32,4096]{1,0:T(8,128)S(1)}, u32[]{:S(2)}, u32[]{:S(2)}) collective-permute-start(f32[32,4096]{1,0:T(8,128)S(1)} %convert_element_type.9), channel_id=1, source_target_pairs={{0,1},{1,0},{2,3},{3,2},{4,5},{5,4},{6,7},{7,6},{8,9},{9,8},{10,11... | collective-permute-start | bytes 1572872 | tf_op jit(solution)/shard_map/ppermute | solution.py:51
  3.6 1.5 %fusion.167 = (s32[1]{0:T(128)}, s32[1]{0:T(128)}, s32[1]{0:T(128)}, s32[1]{0:T(128)}) fusion(s32[4]{0:T(128)} %param.4), kind=kLoop, calls=%fused_computation.212 | loop fusion | bytes 32 | tf_op jit(solution)/shard_map/slice | solution.py:13
  10.0 3.5 %fusion.81 = f32[64,4096]{1,0:T(8,128)S(1)} fusion(s32[]{:T(128)} %bitcast, s32[4096]{0:T(1024)S(1)} %multiply_bitcast_fusion, s32[512]{0:T(512)S(1)} %get-tuple-element.15, bf16[64,4096]{1,0:T(8,128)(2,1)S(1)} %maximum_select_fusion), kind=kOutput, calls=%fused_computation.106 | convolution fusion | flops 291504128 | bytes 1132548 | tf_op jit(solution)/shard_map/dot_general | solution.py:65
  13.4 3.5 %convolution_add_fusion.6 = f32[64,4096]{1,0:T(8,128)S(1)} fusion(f32[64,4096]{1,0:T(8,128)S(1)} %fusion.81, s32[512]{0:T(512)S(1)} %get-tuple-element.14, s32[]{:T(128)} %bitcast, s32[4096]{0:T(1024)S(1)} %multiply_bitcast_fusion, bf16[64,4096]{1,0:T(8,128)(2,1)S(1)} %maximum_select_fusion), kind=kOutput, calls=%fused_computation.63 | convolution fusion | flops 291766272 | bytes 2181124 | tf_op jit(solution)/shard_map/dot_general | solution.py:65
  16.9 3.5 %convolution_add_fusion.5 = f32[64,4096]{1,0:T(8,128)S(1)} fusion(f32[64,4096]{1,0:T(8,128)S(1)} %convolution_add_fusion.6, s32[512]{0:T(512)S(1)} %get-tuple-element.13, s32[]{:T(128)} %bitcast, s32[4096]{0:T(1024)S(1)} %multiply_bitcast_fusion, bf16[64,4096]{1,0:T(8,128)(2,1)S(1)} %maximum_select_fusion), kind=kOutput, calls=%fused_computation.62 | convolution fusion | flops 291766272 | bytes 2181124 | tf_op jit(solution)/shard_map/dot_general | solution.py:65
  20.4 3.7 %convolution_add_fusion.4 = f32[64,4096]{1,0:T(8,128)S(1)} fusion(f32[64,4096]{1,0:T(8,128)S(1)} %convolution_add_fusion.5, s32[512]{0:T(512)S(1)} %get-tuple-element.12, s32[]{:T(128)} %bitcast, s32[4096]{0:T(1024)S(1)} %multiply_bitcast_fusion, bf16[64,4096]{1,0:T(8,128)(2,1)S(1)} %maximum_select_fusion), kind=kOutput, calls=%fused_computation.61 | convolution fusion | flops 291766272 | bytes 2181124 | tf_op jit(solution)/shard_map/dot_general | solution.py:65
  24.1 3.5 %convolution_add_fusion.3 = f32[64,4096]{1,0:T(8,128)S(1)} fusion(f32[64,4096]{1,0:T(8,128)S(1)} %convolution_add_fusion.4, s32[512]{0:T(512)S(1)} %get-tuple-element.11, s32[]{:T(128)} %bitcast, s32[4096]{0:T(1024)S(1)} %multiply_bitcast_fusion, bf16[64,4096]{1,0:T(8,128)(2,1)S(1)} %maximum_select_fusion), kind=kOutput, calls=%fused_computation.60 | convolution fusion | flops 291766272 | bytes 2181124 | tf_op jit(solution)/shard_map/dot_general | solution.py:65
  27.6 3.5 %convolution_add_fusion.2 = f32[64,4096]{1,0:T(8,128)S(1)} fusion(f32[64,4096]{1,0:T(8,128)S(1)} %convolution_add_fusion.3, s32[512]{0:T(512)S(1)} %get-tuple-element.10, s32[]{:T(128)} %bitcast, s32[4096]{0:T(1024)S(1)} %multiply_bitcast_fusion, bf16[64,4096]{1,0:T(8,128)(2,1)S(1)} %maximum_select_fusion), kind=kOutput, calls=%fused_computation.59 | convolution fusion | flops 291766272 | bytes 2181124 | tf_op jit(solution)/shard_map/dot_general | solution.py:65
  31.1 3.5 %convolution_add_fusion.1 = f32[64,4096]{1,0:T(8,128)S(1)} fusion(f32[64,4096]{1,0:T(8,128)S(1)} %convolution_add_fusion.2, s32[512]{0:T(512)S(1)} %get-tuple-element.9, s32[]{:T(128)} %bitcast, s32[4096]{0:T(1024)S(1)} %multiply_bitcast_fusion, bf16[64,4096]{1,0:T(8,128)(2,1)S(1)} %maximum_select_fusion), kind=kOutput, calls=%fused_computation.58 | convolution fusion | flops 291766272 | bytes 2181124 | tf_op jit(solution)/shard_map/dot_general | solution.py:65
  34.6 3.7 %fusion.99 = f32[8,8,32,128]{3,1,2,0:T(8,128)S(1)} fusion(f32[64,4096]{1,0:T(8,128)S(1)} %convolution_add_fusion.1, s32[512]{0:T(512)S(1)} %get-tuple-element.8, s32[]{:T(128)} %bitcast, s32[4096]{0:T(1024)S(1)} %multiply_bitcast_fusion, bf16[64,4096]{1,0:T(8,128)(2,1)S(1)} %maximum_select_fusion), kind=kOutput, calls=%fused_computation.123 | convolution fusion | flops 291766272 | bytes 2181124 | tf_op jit(solution)/shard_map/dot_general | solution.py:65
  38.5 1.6 %copy.6 = f32[2,32,32,128]{3,1,0,2:T(8,128)} copy(f32[2,32,32,128]{3,2,1,0:T(8,128)S(1)} %bitcast.35) | data formatting | bytes 2097152 | tf_op jit(solution)/shard_map/reshape | solution.py:68
  40.1 14.1 %all-to-all-start = ((f32[64,32,128]{2,1,0:T(8,128)}), f32[64,32,128]{2,1,0:T(8,128)S(1)}, u32[]{:S(2)}, u32[]{:S(2)}) async-start(f32[64,32,128]{2,1,0:T(8,128)} %bitcast.6), calls=%async_computation | async-start | bytes 2097152 | tf_op jit(solution)/shard_map/all_to_all | solution.py:70
  54.2 27.1 %all-to-all-done = f32[64,32,128]{2,1,0:T(8,128)S(1)} async-done(((f32[64,32,128]{2,1,0:T(8,128)}), f32[64,32,128]{2,1,0:T(8,128)S(1)}, u32[]{:S(2)}, u32[]{:S(2)}) %all-to-all-start) | async-done | bytes 1048608 | tf_op jit(solution)/shard_map/all_to_all | solution.py:70
  81.4 19.0 %all_gather.3 = f32[512,256]{1,0:T(8,128)S(1)} all-gather(f32[32,256]{1,0:T(8,128)S(1)} %copy_bitcast_fusion), channel_id=1, replica_groups=mesh['param'=32,'ey'=8,'ec'=2] {'ey','ec'}, dimensions={0}, use_global_device_ids=true | all-gather | bytes 557056 | tf_op jit(solution)/shard_map/all_gather | solution.py:74
  102.2 3.3 %collective-permute-start.1 = (f32[8480]{0:T(1024)S(1)}, f32[8480]{0:T(1024)S(1)}, u32[]{:S(2)}, u32[]{:S(2)}) collective-permute-start(f32[8480]{0:T(1024)S(1)} %concatenate.11), channel_id=1, source_target_pairs={{0,16},{16,0},{32,48},{48,32},{64,80},{80,64},{96,112},{112,96},{1... | collective-permute-start | bytes 101768 | tf_op jit(solution)/shard_map/ppermute | solution.py:33
  105.5 2.6 %collective-permute-done.1 = f32[8480]{0:T(1024)S(1)} collective-permute-done((f32[8480]{0:T(1024)S(1)}, f32[8480]{0:T(1024)S(1)}, u32[]{:S(2)}, u32[]{:S(2)}) %collective-permute-start.1) | collective-permute-done | bytes 33952 | tf_op jit(solution)/shard_map/ppermute | solution.py:33
  108.1 4.8 %collective-permute-start.2 = (f32[8480]{0:T(1024)S(1)}, f32[8480]{0:T(1024)S(1)}, u32[]{:S(2)}, u32[]{:S(2)}) collective-permute-start(f32[8480]{0:T(1024)S(1)} %add.406), channel_id=1, source_target_pairs={{0,32},{16,48},{32,0},{48,16},{64,96},{80,112},{96,64},{112,80},{1... | collective-permute-start | bytes 101768 | tf_op jit(solution)/shard_map/ppermute | solution.py:33
  112.9 1.9 %collective-permute-done.2 = f32[8480]{0:T(1024)S(1)} collective-permute-done((f32[8480]{0:T(1024)S(1)}, f32[8480]{0:T(1024)S(1)}, u32[]{:S(2)}, u32[]{:S(2)}) %collective-permute-start.2) | collective-permute-done | bytes 33952 | tf_op jit(solution)/shard_map/ppermute | solution.py:33
  114.8 5.2 %collective-permute-start.3 = (f32[8480]{0:T(1024)S(1)}, f32[8480]{0:T(1024)S(1)}, u32[]{:S(2)}, u32[]{:S(2)}) collective-permute-start(f32[8480]{0:T(1024)S(1)} %add.407), channel_id=1, source_target_pairs={{0,64},{16,80},{32,96},{48,112},{64,0},{80,16},{96,32},{112,48},{1... | collective-permute-start | bytes 101768 | tf_op jit(solution)/shard_map/ppermute | solution.py:33
  120.1 4.5 %collective-permute-done.3 = f32[8480]{0:T(1024)S(1)} collective-permute-done((f32[8480]{0:T(1024)S(1)}, f32[8480]{0:T(1024)S(1)}, u32[]{:S(2)}, u32[]{:S(2)}) %collective-permute-start.3) | collective-permute-done | bytes 33952 | tf_op jit(solution)/shard_map/ppermute | solution.py:33
  124.6 3.4 %collective-permute-start.4 = (f32[8480]{0:T(1024)S(1)}, f32[8480]{0:T(1024)S(1)}, u32[]{:S(2)}, u32[]{:S(2)}) collective-permute-start(f32[8480]{0:T(1024)S(1)} %add.408), channel_id=1, source_target_pairs={{0,128},{16,144},{32,160},{48,176},{64,192},{80,208},{96,224},{112... | collective-permute-start | bytes 101768 | tf_op jit(solution)/shard_map/ppermute | solution.py:33
  128.0 2.4 %collective-permute-done.4 = f32[8480]{0:T(1024)S(1)} collective-permute-done((f32[8480]{0:T(1024)S(1)}, f32[8480]{0:T(1024)S(1)}, u32[]{:S(2)}, u32[]{:S(2)}) %collective-permute-start.4) | collective-permute-done | bytes 33952 | tf_op jit(solution)/shard_map/ppermute | solution.py:33
  130.4 4.0 %collective-permute-start.5 = (f32[8480]{0:T(1024)S(1)}, f32[8480]{0:T(1024)S(1)}, u32[]{:S(2)}, u32[]{:S(2)}) collective-permute-start(f32[8480]{0:T(1024)S(1)} %add.409), channel_id=1, source_target_pairs={{0,256},{16,272},{32,288},{48,304},{64,320},{80,336},{96,352},{112... | collective-permute-start | bytes 101768 | tf_op jit(solution)/shard_map/ppermute | solution.py:33
  134.5 3.3 %collective-permute-done.5 = f32[8480]{0:T(1024)S(1)} collective-permute-done((f32[8480]{0:T(1024)S(1)}, f32[8480]{0:T(1024)S(1)}, u32[]{:S(2)}, u32[]{:S(2)}) %collective-permute-start.5) | collective-permute-done | bytes 33952 | tf_op jit(solution)/shard_map/ppermute | solution.py:33
  (36 shorter events, 6.9 us)
Async XLA Ops:
  0.6 9.2 %copy-start = (bf16[32,4096]{1,0:T(8,128)(2,1)S(1)}, bf16[32,4096]{1,0:T(8,128)(2,1)}, u32[]{:S(2)}) copy-start(bf16[32,4096]{1,0:T(8,128)(2,1)} %param.3) | copy-start | bytes 786436
  1.7 8.1 %collective-permute-start = (f32[32,4096]{1,0:T(8,128)S(1)}, f32[32,4096]{1,0:T(8,128)S(1)}, u32[]{:S(2)}, u32[]{:S(2)}) collective-permute-start(f32[32,4096]{1,0:T(8,128)S(1)} %convert_element_type.9), channel_id=1, source_target_pairs={{0,1},{1,0},{2,3},{3,2},{4,5},{5,4},{6,7},{7,6},{8,9},{9,8},{10,11... | collective-permute-start | bytes 1572872 | tf_op jit(solution)/shard_map/ppermute | solution.py:51
  40.1 14.1 %copy-start.1 = (s32[256]{0:T(256)S(1)}, s32[256]{0:T(256)}, u32[]{:S(2)}) copy-start(s32[256]{0:T(256)} %param.5) | copy-start | bytes 3076
  40.1 41.2 %all-to-all-start = ((f32[64,32,128]{2,1,0:T(8,128)}), f32[64,32,128]{2,1,0:T(8,128)S(1)}, u32[]{:S(2)}, u32[]{:S(2)}) async-start(f32[64,32,128]{2,1,0:T(8,128)} %bitcast.6), calls=%async_computation | async-start | bytes 2097152 | tf_op jit(solution)/shard_map/all_to_all | solution.py:70
  102.2 5.8 %collective-permute-start.1 = (f32[8480]{0:T(1024)S(1)}, f32[8480]{0:T(1024)S(1)}, u32[]{:S(2)}, u32[]{:S(2)}) collective-permute-start(f32[8480]{0:T(1024)S(1)} %concatenate.11), channel_id=1, source_target_pairs={{0,16},{16,0},{32,48},{48,32},{64,80},{80,64},{96,112},{112,96},{1... | collective-permute-start | bytes 101768 | tf_op jit(solution)/shard_map/ppermute | solution.py:33
  108.1 6.7 %collective-permute-start.2 = (f32[8480]{0:T(1024)S(1)}, f32[8480]{0:T(1024)S(1)}, u32[]{:S(2)}, u32[]{:S(2)}) collective-permute-start(f32[8480]{0:T(1024)S(1)} %add.406), channel_id=1, source_target_pairs={{0,32},{16,48},{32,0},{48,16},{64,96},{80,112},{96,64},{112,80},{1... | collective-permute-start | bytes 101768 | tf_op jit(solution)/shard_map/ppermute | solution.py:33
  114.8 9.7 %collective-permute-start.3 = (f32[8480]{0:T(1024)S(1)}, f32[8480]{0:T(1024)S(1)}, u32[]{:S(2)}, u32[]{:S(2)}) collective-permute-start(f32[8480]{0:T(1024)S(1)} %add.407), channel_id=1, source_target_pairs={{0,64},{16,80},{32,96},{48,112},{64,0},{80,16},{96,32},{112,48},{1... | collective-permute-start | bytes 101768 | tf_op jit(solution)/shard_map/ppermute | solution.py:33
  124.6 5.8 %collective-permute-start.4 = (f32[8480]{0:T(1024)S(1)}, f32[8480]{0:T(1024)S(1)}, u32[]{:S(2)}, u32[]{:S(2)}) collective-permute-start(f32[8480]{0:T(1024)S(1)} %add.408), channel_id=1, source_target_pairs={{0,128},{16,144},{32,160},{48,176},{64,192},{80,208},{96,224},{112... | collective-permute-start | bytes 101768 | tf_op jit(solution)/shard_map/ppermute | solution.py:33
  130.4 7.3 %collective-permute-start.5 = (f32[8480]{0:T(1024)S(1)}, f32[8480]{0:T(1024)S(1)}, u32[]{:S(2)}, u32[]{:S(2)}) collective-permute-start(f32[8480]{0:T(1024)S(1)} %add.409), channel_id=1, source_target_pairs={{0,256},{16,272},{32,288},{48,304},{64,320},{80,336},{96,352},{112... | collective-permute-start | bytes 101768 | tf_op jit(solution)/shard_map/ppermute | solution.py:33

commit v3 on v2

--- a/solution.py
+++ b/solution.py
@@ -9,14 +9,16 @@
 norm_eps = 1e-06
 
 
-def sign_block(sign_hash_keys, first_row, row_count, col_ids):
+def hash_terms(sign_hash_keys, first_row, row_count, col_ids):
     mult_row = sign_hash_keys[0] | 1
     mult_col = sign_hash_keys[1] | 1
     seed_add = sign_hash_keys[2]
+    row_ids = first_row + lax.iota(jnp.int32, row_count)
+    return row_ids * mult_row + seed_add, col_ids * mult_col
+
+
+def sign_block(sign_hash_keys, row_terms, col_terms):
     mix_mult = sign_hash_keys[3] | 1
-    row_ids = first_row + lax.iota(jnp.int32, row_count)
-    row_terms = row_ids * mult_row + seed_add
-    col_terms = col_ids * mult_col
     hashed = row_terms[:, None] + col_terms[None, :]
     hashed = hashed ^ lax.shift_right_logical(hashed, jnp.full_like(hashed, 16))
     hashed = hashed * mix_mult
@@ -57,11 +59,12 @@
     )
     owner = lax.iota(jnp.int32, param_count)[:, None] * col_width
     col_ids = (owner + core * half_width + lax.iota(jnp.int32, half_width)[None, :]).reshape(-1)
+    row_terms, col_terms = hash_terms(sign_hash_keys, row_base, resident_rows, col_ids)
     totals = None
     for tile in range(turn_count):
         start_offset = tile * rows_per_tile
         gradient_slab = pair_gradients[:, start_offset:start_offset + rows_per_tile]
-        signs = sign_block(sign_hash_keys, row_base + start_offset, rows_per_tile, col_ids)
+        signs = sign_block(sign_hash_keys, row_terms[start_offset:start_offset + rows_per_tile], col_terms)
         term = jnp.dot(gradient_slab, signs, preferred_element_type=jnp.float32)
         totals = term if totals is None else totals + term
 

time: 139 us -> 137 us (0.986)
  other arithmetic: 5.2 us -> 3.02 us
    add x4 -> x1, other arithmetic: 2.74 us -> 0.56 us  [hash_terms(): return (row_ids * mult_row + seed_add, col_ids * mult_col)]
  transfers between devices with their start and end apart: 7 -> 7, of which waited for: 6 -> 6; matrix products, arithmetic and copies ran while one was open for 3% -> 2% of each run, Pallas kernels for 0% -> 0%
where the time goes in v3:
time: 137 us; the launch traced here: 136 us
  waiting for transfers between devices  41.8 us (31%)
  starting transfers between devices  36.8 us (27%)
  matrix products  28.7 us (21%)
  blocking collectives  19 us (14%)
  local copies, waits for them, and re-layouts  4.28 us (3%)
  other arithmetic  3.02 us (2%)
  between operations  2.8 us (2%)
    dot_general x8, matrix products, local(): term = jnp.dot(gradient_slab, signs, preferred_element_type=jnp.float32)  28.3 us
    all_to_all x1, waiting for transfers between devices, local(): blocks = lax.all_to_all(blocks, ('param', 'ec'), 0, 0, tiled=True)  27.1 us
    ppermute x5, starting transfers between devices, butterfly_sum(): values = values + lax.ppermute(values, axis, pairs)  20.8 us
    all_gather x1, blocking collectives, local(): pool_rows = lax.all_gather(projected, ('ey', 'ec'), axis=0, tiled=True)  19 us
    ppermute x5, waiting for transfers between devices, butterfly_sum(): values = values + lax.ppermute(values, axis, pairs)  14.7 us
    all_to_all x1, starting transfers between devices, local(): blocks = lax.all_to_all(blocks, ('param', 'ec'), 0, 0, tiled=True)  14.1 us
  transfers between devices with their start and end apart: 7, of which 6 were waited for; matrix products, arithmetic and copies ran while one was open for 2% of the time, Pallas kernels for 0%

profile of v3, /device:TPU:2, one launch (start us, length us, event | category | flops | bytes accessed | tf_op | source)
XLA Modules:
  0.0 136.4 jit_solution(14407505048217331539)
XLA Ops:
  1.7 1.9 %collective-permute-start = (f32[32,4096]{1,0:T(8,128)S(1)}, f32[32,4096]{1,0:T(8,128)S(1)}, u32[]{:S(2)}, u32[]{:S(2)}) collective-permute-start(f32[32,4096]{1,0:T(8,128)S(1)} %convert_element_type.9), channel_id=1, source_target_pairs={{0,1},{1,0},{2,3},{3,2},{4,5},{5,4},{6,7},{7,6},{8,9},{9,8},{10,11... | collective-permute-start | bytes 1572872 | tf_op jit(solution)/shard_map/ppermute | solution.py:53
  3.6 1.4 %fusion.168 = (s32[1]{0:T(128)}, s32[1]{0:T(128)}, s32[1]{0:T(128)}, s32[1]{0:T(128)}) fusion(s32[4]{0:T(128)} %param.4), kind=kLoop, calls=%fused_computation.206 | loop fusion | bytes 32 | tf_op jit(solution)/shard_map/slice | solution.py:13
  7.8 3.5 %fusion.81 = f32[64,4096]{1,0:T(8,128)S(1)} fusion(s32[]{:T(128)} %bitcast, s32[4096]{0:T(1024)S(1)} %multiply_bitcast_fusion, s32[512]{0:T(512)S(1)} %get-tuple-element.9, bf16[64,4096]{1,0:T(8,128)(2,1)S(1)} %maximum_select_fusion), kind=kOutput, calls=%fused_computation.106 | convolution fusion | flops 291504128 | bytes 1132548 | tf_op jit(solution)/shard_map/dot_general | solution.py:68
  11.2 3.5 %convolution_add_fusion.6 = f32[64,4096]{1,0:T(8,128)S(1)} fusion(f32[64,4096]{1,0:T(8,128)S(1)} %fusion.81, s32[512]{0:T(512)S(1)} %get-tuple-element.8, s32[]{:T(128)} %bitcast, s32[4096]{0:T(1024)S(1)} %multiply_bitcast_fusion, bf16[64,4096]{1,0:T(8,128)(2,1)S(1)} %maximum_select_fusion), kind=kOutput, calls=%fused_computation.63 | convolution fusion | flops 291766272 | bytes 2181124 | tf_op jit(solution)/shard_map/dot_general | solution.py:68
  14.7 3.5 %convolution_add_fusion.5 = f32[64,4096]{1,0:T(8,128)S(1)} fusion(f32[64,4096]{1,0:T(8,128)S(1)} %convolution_add_fusion.6, s32[512]{0:T(512)S(1)} %get-tuple-element.7, s32[]{:T(128)} %bitcast, s32[4096]{0:T(1024)S(1)} %multiply_bitcast_fusion, bf16[64,4096]{1,0:T(8,128)(2,1)S(1)} %maximum_select_fusion), kind=kOutput, calls=%fused_computation.62 | convolution fusion | flops 291766272 | bytes 2181124 | tf_op jit(solution)/shard_map/dot_general | solution.py:68
  18.2 3.7 %convolution_add_fusion.4 = f32[64,4096]{1,0:T(8,128)S(1)} fusion(f32[64,4096]{1,0:T(8,128)S(1)} %convolution_add_fusion.5, s32[512]{0:T(512)S(1)} %get-tuple-element.6, s32[]{:T(128)} %bitcast, s32[4096]{0:T(1024)S(1)} %multiply_bitcast_fusion, bf16[64,4096]{1,0:T(8,128)(2,1)S(1)} %maximum_select_fusion), kind=kOutput, calls=%fused_computation.61 | convolution fusion | flops 291766272 | bytes 2181124 | tf_op jit(solution)/shard_map/dot_general | solution.py:68
  21.9 3.5 %convolution_add_fusion.3 = f32[64,4096]{1,0:T(8,128)S(1)} fusion(f32[64,4096]{1,0:T(8,128)S(1)} %convolution_add_fusion.4, s32[512]{0:T(512)S(1)} %get-tuple-element.5, s32[]{:T(128)} %bitcast, s32[4096]{0:T(1024)S(1)} %multiply_bitcast_fusion, bf16[64,4096]{1,0:T(8,128)(2,1)S(1)} %maximum_select_fusion), kind=kOutput, calls=%fused_computation.60 | convolution fusion | flops 291766272 | bytes 2181124 | tf_op jit(solution)/shard_map/dot_general | solution.py:68
  25.4 3.5 %convolution_add_fusion.2 = f32[64,4096]{1,0:T(8,128)S(1)} fusion(f32[64,4096]{1,0:T(8,128)S(1)} %convolution_add_fusion.3, s32[512]{0:T(512)S(1)} %get-tuple-element.4, s32[]{:T(128)} %bitcast, s32[4096]{0:T(1024)S(1)} %multiply_bitcast_fusion, bf16[64,4096]{1,0:T(8,128)(2,1)S(1)} %maximum_select_fusion), kind=kOutput, calls=%fused_computation.59 | convolution fusion | flops 291766272 | bytes 2181124 | tf_op jit(solution)/shard_map/dot_general | solution.py:68
  28.9 3.5 %convolution_add_fusion.1 = f32[64,4096]{1,0:T(8,128)S(1)} fusion(f32[64,4096]{1,0:T(8,128)S(1)} %convolution_add_fusion.2, s32[512]{0:T(512)S(1)} %get-tuple-element.3, s32[]{:T(128)} %bitcast, s32[4096]{0:T(1024)S(1)} %multiply_bitcast_fusion, bf16[64,4096]{1,0:T(8,128)(2,1)S(1)} %maximum_select_fusion), kind=kOutput, calls=%fused_computation.58 | convolution fusion | flops 291766272 | bytes 2181124 | tf_op jit(solution)/shard_map/dot_general | solution.py:68
  32.4 3.7 %fusion.99 = f32[8,8,32,128]{3,1,2,0:T(8,128)S(1)} fusion(f32[64,4096]{1,0:T(8,128)S(1)} %convolution_add_fusion.1, s32[512]{0:T(512)S(1)} %get-tuple-element.2, s32[]{:T(128)} %bitcast, s32[4096]{0:T(1024)S(1)} %multiply_bitcast_fusion, bf16[64,4096]{1,0:T(8,128)(2,1)S(1)} %maximum_select_fusion), kind=kOutput, calls=%fused_computation.123 | convolution fusion | flops 291766272 | bytes 2181124 | tf_op jit(solution)/shard_map/dot_general | solution.py:68
  36.3 1.6 %copy.6 = f32[2,32,32,128]{3,1,0,2:T(8,128)} copy(f32[2,32,32,128]{3,2,1,0:T(8,128)S(1)} %bitcast.35) | data formatting | bytes 2097152 | tf_op jit(solution)/shard_map/reshape | solution.py:71
  37.9 14.1 %all-to-all-start = ((f32[64,32,128]{2,1,0:T(8,128)}), f32[64,32,128]{2,1,0:T(8,128)S(1)}, u32[]{:S(2)}, u32[]{:S(2)}) async-start(f32[64,32,128]{2,1,0:T(8,128)} %bitcast.6), calls=%async_computation | async-start | bytes 2097152 | tf_op jit(solution)/shard_map/all_to_all | solution.py:73
  52.1 27.1 %all-to-all-done = f32[64,32,128]{2,1,0:T(8,128)S(1)} async-done(((f32[64,32,128]{2,1,0:T(8,128)}), f32[64,32,128]{2,1,0:T(8,128)S(1)}, u32[]{:S(2)}, u32[]{:S(2)}) %all-to-all-start) | async-done | bytes 1048608 | tf_op jit(solution)/shard_map/all_to_all | solution.py:73
  79.2 19.0 %all_gather.3 = f32[512,256]{1,0:T(8,128)S(1)} all-gather(f32[32,256]{1,0:T(8,128)S(1)} %copy_bitcast_fusion), channel_id=1, replica_groups=mesh['param'=32,'ey'=8,'ec'=2] {'ey','ec'}, dimensions={0}, use_global_device_ids=true | all-gather | bytes 557056 | tf_op jit(solution)/shard_map/all_gather | solution.py:77
  100.0 3.3 %collective-permute-start.1 = (f32[8480]{0:T(1024)S(1)}, f32[8480]{0:T(1024)S(1)}, u32[]{:S(2)}, u32[]{:S(2)}) collective-permute-start(f32[8480]{0:T(1024)S(1)} %concatenate.11), channel_id=1, source_target_pairs={{0,16},{16,0},{32,48},{48,32},{64,80},{80,64},{96,112},{112,96},{1... | collective-permute-start | bytes 101768 | tf_op jit(solution)/shard_map/ppermute | solution.py:35
  103.3 2.6 %collective-permute-done.1 = f32[8480]{0:T(1024)S(1)} collective-permute-done((f32[8480]{0:T(1024)S(1)}, f32[8480]{0:T(1024)S(1)}, u32[]{:S(2)}, u32[]{:S(2)}) %collective-permute-start.1) | collective-permute-done | bytes 33952 | tf_op jit(solution)/shard_map/ppermute | solution.py:35
  105.9 4.8 %collective-permute-start.2 = (f32[8480]{0:T(1024)S(1)}, f32[8480]{0:T(1024)S(1)}, u32[]{:S(2)}, u32[]{:S(2)}) collective-permute-start(f32[8480]{0:T(1024)S(1)} %add.223), channel_id=1, source_target_pairs={{0,32},{16,48},{32,0},{48,16},{64,96},{80,112},{96,64},{112,80},{1... | collective-permute-start | bytes 101768 | tf_op jit(solution)/shard_map/ppermute | solution.py:35
  110.7 1.9 %collective-permute-done.2 = f32[8480]{0:T(1024)S(1)} collective-permute-done((f32[8480]{0:T(1024)S(1)}, f32[8480]{0:T(1024)S(1)}, u32[]{:S(2)}, u32[]{:S(2)}) %collective-permute-start.2) | collective-permute-done | bytes 33952 | tf_op jit(solution)/shard_map/ppermute | solution.py:35
  112.6 5.2 %collective-permute-start.3 = (f32[8480]{0:T(1024)S(1)}, f32[8480]{0:T(1024)S(1)}, u32[]{:S(2)}, u32[]{:S(2)}) collective-permute-start(f32[8480]{0:T(1024)S(1)} %add.224), channel_id=1, source_target_pairs={{0,64},{16,80},{32,96},{48,112},{64,0},{80,16},{96,32},{112,48},{1... | collective-permute-start | bytes 101768 | tf_op jit(solution)/shard_map/ppermute | solution.py:35
  117.9 4.5 %collective-permute-done.3 = f32[8480]{0:T(1024)S(1)} collective-permute-done((f32[8480]{0:T(1024)S(1)}, f32[8480]{0:T(1024)S(1)}, u32[]{:S(2)}, u32[]{:S(2)}) %collective-permute-start.3) | collective-permute-done | bytes 33952 | tf_op jit(solution)/shard_map/ppermute | solution.py:35
  122.4 3.4 %collective-permute-start.4 = (f32[8480]{0:T(1024)S(1)}, f32[8480]{0:T(1024)S(1)}, u32[]{:S(2)}, u32[]{:S(2)}) collective-permute-start(f32[8480]{0:T(1024)S(1)} %add.225), channel_id=1, source_target_pairs={{0,128},{16,144},{32,160},{48,176},{64,192},{80,208},{96,224},{112... | collective-permute-start | bytes 101768 | tf_op jit(solution)/shard_map/ppermute | solution.py:35
  125.8 2.4 %collective-permute-done.4 = f32[8480]{0:T(1024)S(1)} collective-permute-done((f32[8480]{0:T(1024)S(1)}, f32[8480]{0:T(1024)S(1)}, u32[]{:S(2)}, u32[]{:S(2)}) %collective-permute-start.4) | collective-permute-done | bytes 33952 | tf_op jit(solution)/shard_map/ppermute | solution.py:35
  128.2 4.0 %collective-permute-start.5 = (f32[8480]{0:T(1024)S(1)}, f32[8480]{0:T(1024)S(1)}, u32[]{:S(2)}, u32[]{:S(2)}) collective-permute-start(f32[8480]{0:T(1024)S(1)} %add.226), channel_id=1, source_target_pairs={{0,256},{16,272},{32,288},{48,304},{64,320},{80,336},{96,352},{112... | collective-permute-start | bytes 101768 | tf_op jit(solution)/shard_map/ppermute | solution.py:35
  132.3 3.3 %collective-permute-done.5 = f32[8480]{0:T(1024)S(1)} collective-permute-done((f32[8480]{0:T(1024)S(1)}, f32[8480]{0:T(1024)S(1)}, u32[]{:S(2)}, u32[]{:S(2)}) %collective-permute-start.5) | collective-permute-done | bytes 33952 | tf_op jit(solution)/shard_map/ppermute | solution.py:35
  (34 shorter events, 4.7 us)
Async XLA Ops:
  0.6 7.0 %copy-start = (bf16[32,4096]{1,0:T(8,128)(2,1)S(1)}, bf16[32,4096]{1,0:T(8,128)(2,1)}, u32[]{:S(2)}) copy-start(bf16[32,4096]{1,0:T(8,128)(2,1)} %param.3) | copy-start | bytes 786436
  1.7 5.9 %collective-permute-start = (f32[32,4096]{1,0:T(8,128)S(1)}, f32[32,4096]{1,0:T(8,128)S(1)}, u32[]{:S(2)}, u32[]{:S(2)}) collective-permute-start(f32[32,4096]{1,0:T(8,128)S(1)} %convert_element_type.9), channel_id=1, source_target_pairs={{0,1},{1,0},{2,3},{3,2},{4,5},{5,4},{6,7},{7,6},{8,9},{9,8},{10,11... | collective-permute-start | bytes 1572872 | tf_op jit(solution)/shard_map/ppermute | solution.py:53
  37.9 14.1 %copy-start.1 = (s32[256]{0:T(256)S(1)}, s32[256]{0:T(256)}, u32[]{:S(2)}) copy-start(s32[256]{0:T(256)} %param.5) | copy-start | bytes 3076
  37.9 41.2 %all-to-all-start = ((f32[64,32,128]{2,1,0:T(8,128)}), f32[64,32,128]{2,1,0:T(8,128)S(1)}, u32[]{:S(2)}, u32[]{:S(2)}) async-start(f32[64,32,128]{2,1,0:T(8,128)} %bitcast.6), calls=%async_computation | async-start | bytes 2097152 | tf_op jit(solution)/shard_map/all_to_all | solution.py:73
  100.0 5.8 %collective-permute-start.1 = (f32[8480]{0:T(1024)S(1)}, f32[8480]{0:T(1024)S(1)}, u32[]{:S(2)}, u32[]{:S(2)}) collective-permute-start(f32[8480]{0:T(1024)S(1)} %concatenate.11), channel_id=1, source_target_pairs={{0,16},{16,0},{32,48},{48,32},{64,80},{80,64},{96,112},{112,96},{1... | collective-permute-start | bytes 101768 | tf_op jit(solution)/shard_map/ppermute | solution.py:35
  105.9 6.7 %collective-permute-start.2 = (f32[8480]{0:T(1024)S(1)}, f32[8480]{0:T(1024)S(1)}, u32[]{:S(2)}, u32[]{:S(2)}) collective-permute-start(f32[8480]{0:T(1024)S(1)} %add.223), channel_id=1, source_target_pairs={{0,32},{16,48},{32,0},{48,16},{64,96},{80,112},{96,64},{112,80},{1... | collective-permute-start | bytes 101768 | tf_op jit(solution)/shard_map/ppermute | solution.py:35
  112.6 9.7 %collective-permute-start.3 = (f32[8480]{0:T(1024)S(1)}, f32[8480]{0:T(1024)S(1)}, u32[]{:S(2)}, u32[]{:S(2)}) collective-permute-start(f32[8480]{0:T(1024)S(1)} %add.224), channel_id=1, source_target_pairs={{0,64},{16,80},{32,96},{48,112},{64,0},{80,16},{96,32},{112,48},{1... | collective-permute-start | bytes 101768 | tf_op jit(solution)/shard_map/ppermute | solution.py:35
  122.4 5.8 %collective-permute-start.4 = (f32[8480]{0:T(1024)S(1)}, f32[8480]{0:T(1024)S(1)}, u32[]{:S(2)}, u32[]{:S(2)}) collective-permute-start(f32[8480]{0:T(1024)S(1)} %add.225), channel_id=1, source_target_pairs={{0,128},{16,144},{32,160},{48,176},{64,192},{80,208},{96,224},{112... | collective-permute-start | bytes 101768 | tf_op jit(solution)/shard_map/ppermute | solution.py:35
  128.2 7.3 %collective-permute-start.5 = (f32[8480]{0:T(1024)S(1)}, f32[8480]{0:T(1024)S(1)}, u32[]{:S(2)}, u32[]{:S(2)}) collective-permute-start(f32[8480]{0:T(1024)S(1)} %add.226), channel_id=1, source_target_pairs={{0,256},{16,272},{32,288},{48,304},{64,320},{80,336},{96,352},{112... | collective-permute-start | bytes 101768 | tf_op jit(solution)/shard_map/ppermute | solution.py:35

commit v4 on v3

--- a/solution.py
+++ b/solution.py
@@ -65,11 +65,15 @@
         start_offset = tile * rows_per_tile
         gradient_slab = pair_gradients[:, start_offset:start_offset + rows_per_tile]
         signs = sign_block(sign_hash_keys, row_terms[start_offset:start_offset + rows_per_tile], col_terms)
-        term = jnp.dot(gradient_slab, signs, preferred_element_type=jnp.float32)
+        term = jnp.einsum(
+            "cra,apj->pcrj",
+            gradient_slab.reshape(2, resident_example, rows_per_tile),
+            signs.reshape(rows_per_tile, param_count, half_width),
+            preferred_element_type=jnp.float32,
+        )
         totals = term if totals is None else totals + term
 
-    blocks = totals.reshape(2, resident_example, param_count, half_width)
-    blocks = jnp.transpose(blocks, (2, 0, 1, 3)).reshape(2 * param_count, resident_example, half_width)
+    blocks = totals.reshape(2 * param_count, resident_example, half_width)
     blocks = lax.all_to_all(blocks, ("param", "ec"), 0, 0, tiled=True)
     blocks = jnp.sum(blocks.reshape(param_count, 2, resident_example, half_width), axis=0)
     projected = jnp.transpose(blocks, (1, 0, 2)).reshape(resident_example, col_width)

time: 137 us -> 136 us (level)
  local copies, waits for them, and re-layouts: 4.28 us -> 2.62 us
    reshape x1 -> x0, local copies, waits for them, and re-layouts: 1.58 us -> none  [local(): blocks = totals.reshape(2, resident_example, param_count, half_width)]
where the time goes in v4:
time: 136 us
  waiting for transfers between devices  41.8 us (31%)
  starting transfers between devices  36.8 us (27%)
  matrix products  29.7 us (22%)
  blocking collectives  19 us (14%)
  other arithmetic  3.11 us (2%)
  between operations  2.76 us (2%)
  local copies, waits for them, and re-layouts  2.62 us (2%)
    dot_general x8, matrix products, local(): jnp.einsum('cra,apj->pcrj', gradient_slab.reshape(2, resident_example, ro...  29.3 us
    all_to_all x1, waiting for transfers between devices, local(): blocks = lax.all_to_all(blocks, ('param', 'ec'), 0, 0, tiled=True)  27.1 us
    ppermute x5, starting transfers between devices, butterfly_sum(): values = values + lax.ppermute(values, axis, pairs)  20.8 us
    all_gather x1, blocking collectives, local(): pool_rows = lax.all_gather(projected, ('ey', 'ec'), axis=0, tiled=True)  19 us
    ppermute x5, waiting for transfers between devices, butterfly_sum(): values = values + lax.ppermute(values, axis, pairs)  14.7 us
    all_to_all x1, starting transfers between devices, local(): blocks = lax.all_to_all(blocks, ('param', 'ec'), 0, 0, tiled=True)  14.1 us
  transfers between devices with their start and end apart: 7, of which 6 were waited for; matrix products, arithmetic and copies ran while one was open for 2% of the time, Pallas kernels for 0%

profile of v4, /device:TPU:2, one launch (start us, length us, event | category | flops | bytes accessed | tf_op | source)
XLA Modules:
  0.0 135.8 jit_solution(7914169528266450789)
XLA Ops:
  0.6 1.1 convert_element_type.9
  1.7 1.9 %collective-permute-start = (f32[32,4096]{1,0:T(8,128)S(1)}, f32[32,4096]{1,0:T(8,128)S(1)}, u32[]{:S(2)}, u32[]{:S(2)}) collective-permute-start(f32[32,4096]{1,0:T(8,128)S(1)} %convert_element_type.9), channel_id=1, source_target_pairs={{0,1},{1,0},{2,3},{3,2},{4,5},{5,4},{6,7},{7,6},{8,9},{9,8},{10,11... | collective-permute-start | bytes 1572872 | tf_op jit(solution)/shard_map/ppermute | solution.py:53
  3.6 1.5 %fusion.152 = (s32[1]{0:T(128)}, s32[1]{0:T(128)}, s32[1]{0:T(128)}, s32[1]{0:T(128)}) fusion(s32[4]{0:T(128)} %param.4), kind=kLoop, calls=%fused_computation.171 | loop fusion | bytes 32 | tf_op jit(solution)/shard_map/slice | solution.py:14
  8.0 3.5 %fusion.48 = f32[32,128,2,32]{1,3,2,0:T(8,128)S(1)} fusion(bf16[2,32,512,1]{2,1,0,3:T(8,128)(2,1)S(1)} %bitcast.123, s32[512]{0:T(512)S(1)} %get-tuple-element.14, s32[]{:T(128)} %bitcast.3, s32[32,128]{1,0:T(8,128)S(1)} %add_multiply_fusion), kind=kOutput, calls=%fused_computation.69 | convolution fusion | flops 291504128 | bytes 1132548 | tf_op jit(solution)/shard_map/cra,apj->pcrj/dot_general | solution.py:68
  11.4 3.5 %fusion.50 = f32[32,128,2,32]{1,3,2,0:T(8,128)S(1)} fusion(bf16[2,32,512,1]{2,1,0,3:T(8,128)(2,1)S(1)} %bitcast.122, s32[512]{0:T(512)S(1)} %get-tuple-element.15, s32[]{:T(128)} %bitcast.3, s32[32,128]{1,0:T(8,128)S(1)} %add_multiply_fusion), kind=kOutput, calls=%fused_computation.70 | convolution fusion | flops 291504128 | bytes 1132548 | tf_op jit(solution)/shard_map/cra,apj->pcrj/dot_general | solution.py:68
  14.9 3.5 %fusion.52 = f32[32,128,2,32]{1,3,2,0:T(8,128)S(1)} fusion(bf16[2,32,512,1]{2,1,0,3:T(8,128)(2,1)S(1)} %bitcast.121, s32[512]{0:T(512)S(1)} %get-tuple-element.16, s32[]{:T(128)} %bitcast.3, s32[32,128]{1,0:T(8,128)S(1)} %add_multiply_fusion), kind=kOutput, calls=%fused_computation.71 | convolution fusion | flops 291504128 | bytes 1132548 | tf_op jit(solution)/shard_map/cra,apj->pcrj/dot_general | solution.py:68
  18.4 3.6 %fusion.44 = f32[32,128,2,32]{1,3,2,0:T(8,128)S(1)} fusion(bf16[2,32,512,1]{2,1,0,3:T(8,128)(2,1)S(1)} %bitcast.120, s32[512]{0:T(512)S(1)} %get-tuple-element.12, s32[]{:T(128)} %bitcast.3, s32[32,128]{1,0:T(8,128)S(1)} %add_multiply_fusion), kind=kOutput, calls=%fused_computation.67 | convolution fusion | flops 291504128 | bytes 1132548 | tf_op jit(solution)/shard_map/cra,apj->pcrj/dot_general | solution.py:68
  22.0 3.5 %fusion.42 = f32[32,128,2,32]{1,3,2,0:T(8,128)S(1)} fusion(bf16[2,32,512,1]{2,1,0,3:T(8,128)(2,1)S(1)} %bitcast.119, s32[512]{0:T(512)S(1)} %get-tuple-element.11, s32[]{:T(128)} %bitcast.3, s32[32,128]{1,0:T(8,128)S(1)} %add_multiply_fusion), kind=kOutput, calls=%fused_computation.66 | convolution fusion | flops 291504128 | bytes 1132548 | tf_op jit(solution)/shard_map/cra,apj->pcrj/dot_general | solution.py:68
  25.5 3.5 %fusion.78 = f32[32,128,2,32]{1,3,2,0:T(8,128)S(1)} fusion(f32[32,128,2,32]{1,3,2,0:T(8,128)S(1)} %fusion.48, f32[32,128,2,32]{1,3,2,0:T(8,128)S(1)} %fusion.50, f32[32,128,2,32]{1,3,2,0:T(8,128)S(1)} %fusion.52, bf16[2,32,512,1]{2,1,0,3:T(8,128)(2,1)S(1)} %bitcast.118, s32[]{:T(128)} %bitcast.3, s32[32,128]{1,0:T(8,128)S(1)} %add_multiply_fusion, ...), kind=kOutput, calls=%fused_computation.91 | convolution fusion | flops 292290560 | bytes 4278276 | tf_op jit(solution)/shard_map/cra,apj->pcrj/dot_general | solution.py:68
  29.0 3.5 %fusion.87 = f32[32,128,2,32]{1,3,2,0:T(8,128)S(1)} fusion(f32[32,128,2,32]{1,3,2,0:T(8,128)S(1)} %fusion.42, f32[32,128,2,32]{1,3,2,0:T(8,128)S(1)} %fusion.44, f32[32,128,2,32]{1,3,2,0:T(8,128)S(1)} %fusion.78, bf16[2,32,512,1]{2,1,0,3:T(8,128)(2,1)S(1)} %bitcast.117, s32[512]{0:T(512)S(1)} %get-tuple-element.13, s32[]{:T(128)} %bitcast.3, ...), kind=kOutput, calls=%fused_computation.94 | convolution fusion | flops 292290560 | bytes 4278276 | tf_op jit(solution)/shard_map/cra,apj->pcrj/dot_general | solution.py:68
  32.6 4.7 %fusion.90 = f32[32,128,2,32]{1,3,2,0:T(8,128)} fusion(f32[32,128,2,32]{1,3,2,0:T(8,128)S(1)} %fusion.87, bf16[2,32,512,1]{2,1,0,3:T(8,128)(2,1)S(1)} %bitcast.116, s32[512]{0:T(512)S(1)} %get-tuple-element.10, s32[]{:T(128)} %bitcast.3, s32[32,128]{1,0:T(8,128)S(1)} %add_multiply_fusion), kind=kOutput, calls=%fused_computation.95 | convolution fusion | flops 291766272 | bytes 2181124 | tf_op jit(solution)/shard_map/cra,apj->pcrj/dot_general | solution.py:68
  37.3 14.1 %all-to-all-start = ((f32[64,32,128]{2,1,0:T(8,128)}), f32[64,32,128]{2,1,0:T(8,128)S(1)}, u32[]{:S(2)}, u32[]{:S(2)}) async-start(f32[64,32,128]{2,1,0:T(8,128)} %bitcast.37), calls=%async_computation | async-start | bytes 2097152 | tf_op jit(solution)/shard_map/all_to_all | solution.py:77
  51.5 27.1 %all-to-all-done = f32[64,32,128]{2,1,0:T(8,128)S(1)} async-done(((f32[64,32,128]{2,1,0:T(8,128)}), f32[64,32,128]{2,1,0:T(8,128)S(1)}, u32[]{:S(2)}, u32[]{:S(2)}) %all-to-all-start) | async-done | bytes 1048608 | tf_op jit(solution)/shard_map/all_to_all | solution.py:77
  78.6 19.0 %all_gather.3 = f32[512,256]{1,0:T(8,128)S(1)} all-gather(f32[32,256]{1,0:T(8,128)S(1)} %copy_bitcast_fusion), channel_id=1, replica_groups=mesh['param'=32,'ey'=8,'ec'=2] {'ey','ec'}, dimensions={0}, use_global_device_ids=true | all-gather | bytes 557056 | tf_op jit(solution)/shard_map/all_gather | solution.py:81
  99.4 3.3 %collective-permute-start.1 = (f32[8480]{0:T(1024)S(1)}, f32[8480]{0:T(1024)S(1)}, u32[]{:S(2)}, u32[]{:S(2)}) collective-permute-start(f32[8480]{0:T(1024)S(1)} %concatenate.11), channel_id=1, source_target_pairs={{0,16},{16,0},{32,48},{48,32},{64,80},{80,64},{96,112},{112,96},{1... | collective-permute-start | bytes 101768 | tf_op jit(solution)/shard_map/ppermute | solution.py:35
  102.7 2.6 %collective-permute-done.1 = f32[8480]{0:T(1024)S(1)} collective-permute-done((f32[8480]{0:T(1024)S(1)}, f32[8480]{0:T(1024)S(1)}, u32[]{:S(2)}, u32[]{:S(2)}) %collective-permute-start.1) | collective-permute-done | bytes 33952 | tf_op jit(solution)/shard_map/ppermute | solution.py:35
  105.3 4.8 %collective-permute-start.2 = (f32[8480]{0:T(1024)S(1)}, f32[8480]{0:T(1024)S(1)}, u32[]{:S(2)}, u32[]{:S(2)}) collective-permute-start(f32[8480]{0:T(1024)S(1)} %add.269), channel_id=1, source_target_pairs={{0,32},{16,48},{32,0},{48,16},{64,96},{80,112},{96,64},{112,80},{1... | collective-permute-start | bytes 101768 | tf_op jit(solution)/shard_map/ppermute | solution.py:35
  110.1 1.9 %collective-permute-done.2 = f32[8480]{0:T(1024)S(1)} collective-permute-done((f32[8480]{0:T(1024)S(1)}, f32[8480]{0:T(1024)S(1)}, u32[]{:S(2)}, u32[]{:S(2)}) %collective-permute-start.2) | collective-permute-done | bytes 33952 | tf_op jit(solution)/shard_map/ppermute | solution.py:35
  112.0 5.2 %collective-permute-start.3 = (f32[8480]{0:T(1024)S(1)}, f32[8480]{0:T(1024)S(1)}, u32[]{:S(2)}, u32[]{:S(2)}) collective-permute-start(f32[8480]{0:T(1024)S(1)} %add.270), channel_id=1, source_target_pairs={{0,64},{16,80},{32,96},{48,112},{64,0},{80,16},{96,32},{112,48},{1... | collective-permute-start | bytes 101768 | tf_op jit(solution)/shard_map/ppermute | solution.py:35
  117.3 4.5 %collective-permute-done.3 = f32[8480]{0:T(1024)S(1)} collective-permute-done((f32[8480]{0:T(1024)S(1)}, f32[8480]{0:T(1024)S(1)}, u32[]{:S(2)}, u32[]{:S(2)}) %collective-permute-start.3) | collective-permute-done | bytes 33952 | tf_op jit(solution)/shard_map/ppermute | solution.py:35
  121.8 3.4 %collective-permute-start.4 = (f32[8480]{0:T(1024)S(1)}, f32[8480]{0:T(1024)S(1)}, u32[]{:S(2)}, u32[]{:S(2)}) collective-permute-start(f32[8480]{0:T(1024)S(1)} %add.271), channel_id=1, source_target_pairs={{0,128},{16,144},{32,160},{48,176},{64,192},{80,208},{96,224},{112... | collective-permute-start | bytes 101768 | tf_op jit(solution)/shard_map/ppermute | solution.py:35
  125.2 2.4 %collective-permute-done.4 = f32[8480]{0:T(1024)S(1)} collective-permute-done((f32[8480]{0:T(1024)S(1)}, f32[8480]{0:T(1024)S(1)}, u32[]{:S(2)}, u32[]{:S(2)}) %collective-permute-start.4) | collective-permute-done | bytes 33952 | tf_op jit(solution)/shard_map/ppermute | solution.py:35
  127.6 4.0 %collective-permute-start.5 = (f32[8480]{0:T(1024)S(1)}, f32[8480]{0:T(1024)S(1)}, u32[]{:S(2)}, u32[]{:S(2)}) collective-permute-start(f32[8480]{0:T(1024)S(1)} %add.272), channel_id=1, source_target_pairs={{0,256},{16,272},{32,288},{48,304},{64,320},{80,336},{96,352},{112... | collective-permute-start | bytes 101768 | tf_op jit(solution)/shard_map/ppermute | solution.py:35
  131.7 3.3 %collective-permute-done.5 = f32[8480]{0:T(1024)S(1)} collective-permute-done((f32[8480]{0:T(1024)S(1)}, f32[8480]{0:T(1024)S(1)}, u32[]{:S(2)}, u32[]{:S(2)}) %collective-permute-start.5) | collective-permute-done | bytes 33952 | tf_op jit(solution)/shard_map/ppermute | solution.py:35
  (33 shorter events, 3.6 us)
Async XLA Ops:
  0.6 7.2 %copy-start = (bf16[32,4096]{1,0:T(8,128)(2,1)S(1)}, bf16[32,4096]{1,0:T(8,128)(2,1)}, u32[]{:S(2)}) copy-start(bf16[32,4096]{1,0:T(8,128)(2,1)} %param.3) | copy-start | bytes 786436
  1.7 6.1 %collective-permute-start = (f32[32,4096]{1,0:T(8,128)S(1)}, f32[32,4096]{1,0:T(8,128)S(1)}, u32[]{:S(2)}, u32[]{:S(2)}) collective-permute-start(f32[32,4096]{1,0:T(8,128)S(1)} %convert_element_type.9), channel_id=1, source_target_pairs={{0,1},{1,0},{2,3},{3,2},{4,5},{5,4},{6,7},{7,6},{8,9},{9,8},{10,11... | collective-permute-start | bytes 1572872 | tf_op jit(solution)/shard_map/ppermute | solution.py:53
  37.3 14.1 %copy-start.1 = (s32[256]{0:T(256)S(1)}, s32[256]{0:T(256)}, u32[]{:S(2)}) copy-start(s32[256]{0:T(256)} %param.5) | copy-start | bytes 3076
  37.3 41.3 %all-to-all-start = ((f32[64,32,128]{2,1,0:T(8,128)}), f32[64,32,128]{2,1,0:T(8,128)S(1)}, u32[]{:S(2)}, u32[]{:S(2)}) async-start(f32[64,32,128]{2,1,0:T(8,128)} %bitcast.37), calls=%async_computation | async-start | bytes 2097152 | tf_op jit(solution)/shard_map/all_to_all | solution.py:77
  99.4 5.8 %collective-permute-start.1 = (f32[8480]{0:T(1024)S(1)}, f32[8480]{0:T(1024)S(1)}, u32[]{:S(2)}, u32[]{:S(2)}) collective-permute-start(f32[8480]{0:T(1024)S(1)} %concatenate.11), channel_id=1, source_target_pairs={{0,16},{16,0},{32,48},{48,32},{64,80},{80,64},{96,112},{112,96},{1... | collective-permute-start | bytes 101768 | tf_op jit(solution)/shard_map/ppermute | solution.py:35
  105.3 6.7 %collective-permute-start.2 = (f32[8480]{0:T(1024)S(1)}, f32[8480]{0:T(1024)S(1)}, u32[]{:S(2)}, u32[]{:S(2)}) collective-permute-start(f32[8480]{0:T(1024)S(1)} %add.269), channel_id=1, source_target_pairs={{0,32},{16,48},{32,0},{48,16},{64,96},{80,112},{96,64},{112,80},{1... | collective-permute-start | bytes 101768 | tf_op jit(solution)/shard_map/ppermute | solution.py:35
  112.0 9.7 %collective-permute-start.3 = (f32[8480]{0:T(1024)S(1)}, f32[8480]{0:T(1024)S(1)}, u32[]{:S(2)}, u32[]{:S(2)}) collective-permute-start(f32[8480]{0:T(1024)S(1)} %add.270), channel_id=1, source_target_pairs={{0,64},{16,80},{32,96},{48,112},{64,0},{80,16},{96,32},{112,48},{1... | collective-permute-start | bytes 101768 | tf_op jit(solution)/shard_map/ppermute | solution.py:35
  121.8 5.8 %collective-permute-start.4 = (f32[8480]{0:T(1024)S(1)}, f32[8480]{0:T(1024)S(1)}, u32[]{:S(2)}, u32[]{:S(2)}) collective-permute-start(f32[8480]{0:T(1024)S(1)} %add.271), channel_id=1, source_target_pairs={{0,128},{16,144},{32,160},{48,176},{64,192},{80,208},{96,224},{112... | collective-permute-start | bytes 101768 | tf_op jit(solution)/shard_map/ppermute | solution.py:35
  127.6 7.3 %collective-permute-start.5 = (f32[8480]{0:T(1024)S(1)}, f32[8480]{0:T(1024)S(1)}, u32[]{:S(2)}, u32[]{:S(2)}) collective-permute-start(f32[8480]{0:T(1024)S(1)} %add.272), channel_id=1, source_target_pairs={{0,256},{16,272},{32,288},{48,304},{64,320},{80,336},{96,352},{112... | collective-permute-start | bytes 101768 | tf_op jit(solution)/shard_map/ppermute | solution.py:35

commit v5 on v4

--- a/solution.py
+++ b/solution.py
@@ -9,16 +9,14 @@
 norm_eps = 1e-06
 
 
-def hash_terms(sign_hash_keys, first_row, row_count, col_ids):
-    mult_row = sign_hash_keys[0] | 1
-    mult_col = sign_hash_keys[1] | 1
-    seed_add = sign_hash_keys[2]
+def hash_terms(hash_scalars, first_row, row_count, col_ids):
+    mult_row, mult_col, seed_add, _ = hash_scalars
     row_ids = first_row + lax.iota(jnp.int32, row_count)
     return row_ids * mult_row + seed_add, col_ids * mult_col
 
 
-def sign_block(sign_hash_keys, row_terms, col_terms):
-    mix_mult = sign_hash_keys[3] | 1
+def sign_block(hash_scalars, row_terms, col_terms):
+    mix_mult = hash_scalars[3]
     hashed = row_terms[:, None] + col_terms[None, :]
     hashed = hashed ^ lax.shift_right_logical(hashed, jnp.full_like(hashed, 16))
     hashed = hashed * mix_mult
@@ -49,8 +47,10 @@
     col_width = K // param_count
     half_width = col_width // 2
 
-    unit = ((sign_hash_keys[3] | 1) & 1).astype(jnp.float32)
-    partner = lax.ppermute(adapter_gradients.astype(jnp.float32), "ec", swap) * unit
+    hash_scalars = (sign_hash_keys[0] | 1, sign_hash_keys[1] | 1, sign_hash_keys[2], sign_hash_keys[3] | 1)
+    hash_scalars, widened = lax.optimization_barrier((hash_scalars, adapter_gradients.astype(jnp.float32)))
+    unit = (hash_scalars[3] & 1).astype(jnp.float32)
+    partner = lax.ppermute(widened, "ec", swap) * unit
     partner = partner.astype(jnp.bfloat16)
     pair_gradients = jnp.where(
         core == 0,
@@ -59,12 +59,12 @@
     )
     owner = lax.iota(jnp.int32, param_count)[:, None] * col_width
     col_ids = (owner + core * half_width + lax.iota(jnp.int32, half_width)[None, :]).reshape(-1)
-    row_terms, col_terms = hash_terms(sign_hash_keys, row_base, resident_rows, col_ids)
+    row_terms, col_terms = hash_terms(hash_scalars, row_base, resident_rows, col_ids)
     totals = None
     for tile in range(turn_count):
         start_offset = tile * rows_per_tile
         gradient_slab = pair_gradients[:, start_offset:start_offset + rows_per_tile]
-        signs = sign_block(sign_hash_keys, row_terms[start_offset:start_offset + rows_per_tile], col_terms)
+        signs = sign_block(hash_scalars, row_terms[start_offset:start_offset + rows_per_tile], col_terms)
         term = jnp.einsum(
             "cra,apj->pcrj",
             gradient_slab.reshape(2, resident_example, rows_per_tile),

time: 136 us -> 137 us (level)
  transfers between devices with their start and end apart: 7 -> 7, of which waited for: 6 -> 7; matrix products, arithmetic and copies ran while one was open for 2% -> 1% of each run, Pallas kernels for 0% -> 0%
where the time goes in v5:
time: 137 us
  waiting for transfers between devices  42.9 us (31%)
  starting transfers between devices  36.7 us (27%)
  matrix products  29.7 us (22%)
  blocking collectives  19 us (14%)
  other arithmetic  3.09 us (2%)
  between operations  2.71 us (2%)
  local copies, waits for them, and re-layouts  2.62 us (2%)
    dot_general x8, matrix products, local(): jnp.einsum('cra,apj->pcrj', gradient_slab.reshape(2, resident_example, ro...  29.3 us
    all_to_all x1, waiting for transfers between devices, local(): blocks = lax.all_to_all(blocks, ('param', 'ec'), 0, 0, tiled=True)  27.1 us
    ppermute x5, starting transfers between devices, butterfly_sum(): values = values + lax.ppermute(values, axis, pairs)  20.8 us
    all_gather x1, blocking collectives, local(): pool_rows = lax.all_gather(projected, ('ey', 'ec'), axis=0, tiled=True)  19 us
    ppermute x5, waiting for transfers between devices, butterfly_sum(): values = values + lax.ppermute(values, axis, pairs)  14.7 us
    all_to_all x1, starting transfers between devices, local(): blocks = lax.all_to_all(blocks, ('param', 'ec'), 0, 0, tiled=True)  14 us
  transfers between devices with their start and end apart: 7, of which 7 were waited for; matrix products, arithmetic and copies ran while one was open for 1% of the time, Pallas kernels for 0%

profile of v5, /device:TPU:2, one launch (start us, length us, event | category | flops | bytes accessed | tf_op | source)
XLA Modules:
  0.0 136.7 jit_solution(6522481420817842670)
XLA Ops:
  0.6 1.5 %fusion.152 = (s32[1]{0:T(128)}, s32[1]{0:T(128)}, s32[1]{0:T(128)}, s32[1]{0:T(128)}) fusion(s32[4]{0:T(128)} %param.4), kind=kLoop, calls=%fused_computation.171 | loop fusion | bytes 32 | tf_op jit(solution)/shard_map/slice | solution.py:50
  5.0 1.9 %collective-permute-start = (f32[32,4096]{1,0:T(8,128)S(1)}, f32[32,4096]{1,0:T(8,128)S(1)}, u32[]{:S(2)}, u32[]{:S(2)}) collective-permute-start(f32[32,4096]{1,0:T(8,128)S(1)} %convert_element_type.9), channel_id=1, source_target_pairs={{0,1},{1,0},{2,3},{3,2},{4,5},{5,4},{6,7},{7,6},{8,9},{9,8},{10,11... | collective-permute-start | bytes 1572872 | tf_op jit(solution)/shard_map/ppermute | solution.py:53
  7.7 1.1 collective-permute-done
  9.0 3.5 %fusion.50 = f32[32,128,2,32]{1,3,2,0:T(8,128)S(1)} fusion(bf16[2,32,512,1]{2,1,0,3:T(8,128)(2,1)S(1)} %bitcast.123, s32[512]{0:T(512)S(1)} %get-tuple-element.25, s32[]{:T(128)} %bitcast.3, s32[32,128]{1,0:T(8,128)S(1)} %add_multiply_fusion), kind=kOutput, calls=%fused_computation.70 | convolution fusion | flops 291504128 | bytes 1132548 | tf_op jit(solution)/shard_map/cra,apj->pcrj/dot_general | solution.py:68
  12.4 3.5 %fusion.52 = f32[32,128,2,32]{1,3,2,0:T(8,128)S(1)} fusion(bf16[2,32,512,1]{2,1,0,3:T(8,128)(2,1)S(1)} %bitcast.122, s32[512]{0:T(512)S(1)} %get-tuple-element.26, s32[]{:T(128)} %bitcast.3, s32[32,128]{1,0:T(8,128)S(1)} %add_multiply_fusion), kind=kOutput, calls=%fused_computation.71 | convolution fusion | flops 291504128 | bytes 1132548 | tf_op jit(solution)/shard_map/cra,apj->pcrj/dot_general | solution.py:68
  15.9 3.5 %fusion.48 = f32[32,128,2,32]{1,3,2,0:T(8,128)S(1)} fusion(bf16[2,32,512,1]{2,1,0,3:T(8,128)(2,1)S(1)} %bitcast.121, s32[512]{0:T(512)S(1)} %get-tuple-element.24, s32[]{:T(128)} %bitcast.3, s32[32,128]{1,0:T(8,128)S(1)} %add_multiply_fusion), kind=kOutput, calls=%fused_computation.69 | convolution fusion | flops 291504128 | bytes 1132548 | tf_op jit(solution)/shard_map/cra,apj->pcrj/dot_general | solution.py:68
  19.4 3.6 %fusion.44 = f32[32,128,2,32]{1,3,2,0:T(8,128)S(1)} fusion(bf16[2,32,512,1]{2,1,0,3:T(8,128)(2,1)S(1)} %bitcast.120, s32[512]{0:T(512)S(1)} %get-tuple-element.22, s32[]{:T(128)} %bitcast.3, s32[32,128]{1,0:T(8,128)S(1)} %add_multiply_fusion), kind=kOutput, calls=%fused_computation.67 | convolution fusion | flops 291504128 | bytes 1132548 | tf_op jit(solution)/shard_map/cra,apj->pcrj/dot_general | solution.py:68
  23.0 3.5 %fusion.42 = f32[32,128,2,32]{1,3,2,0:T(8,128)S(1)} fusion(bf16[2,32,512,1]{2,1,0,3:T(8,128)(2,1)S(1)} %bitcast.119, s32[512]{0:T(512)S(1)} %get-tuple-element.21, s32[]{:T(128)} %bitcast.3, s32[32,128]{1,0:T(8,128)S(1)} %add_multiply_fusion), kind=kOutput, calls=%fused_computation.66 | convolution fusion | flops 291504128 | bytes 1132548 | tf_op jit(solution)/shard_map/cra,apj->pcrj/dot_general | solution.py:68
  26.5 3.5 %fusion.78 = f32[32,128,2,32]{1,3,2,0:T(8,128)S(1)} fusion(f32[32,128,2,32]{1,3,2,0:T(8,128)S(1)} %fusion.48, f32[32,128,2,32]{1,3,2,0:T(8,128)S(1)} %fusion.50, f32[32,128,2,32]{1,3,2,0:T(8,128)S(1)} %fusion.52, bf16[2,32,512,1]{2,1,0,3:T(8,128)(2,1)S(1)} %bitcast.118, s32[]{:T(128)} %bitcast.3, s32[32,128]{1,0:T(8,128)S(1)} %add_multiply_fusion, ...), kind=kOutput, calls=%fused_computation.91 | convolution fusion | flops 292290560 | bytes 4278276 | tf_op jit(solution)/shard_map/cra,apj->pcrj/dot_general | solution.py:68
  30.0 3.5 %fusion.87 = f32[32,128,2,32]{1,3,2,0:T(8,128)S(1)} fusion(f32[32,128,2,32]{1,3,2,0:T(8,128)S(1)} %fusion.42, f32[32,128,2,32]{1,3,2,0:T(8,128)S(1)} %fusion.44, f32[32,128,2,32]{1,3,2,0:T(8,128)S(1)} %fusion.78, bf16[2,32,512,1]{2,1,0,3:T(8,128)(2,1)S(1)} %bitcast.117, s32[512]{0:T(512)S(1)} %get-tuple-element.23, s32[]{:T(128)} %bitcast.3, ...), kind=kOutput, calls=%fused_computation.94 | convolution fusion | flops 292290560 | bytes 4278276 | tf_op jit(solution)/shard_map/cra,apj->pcrj/dot_general | solution.py:68
  33.6 4.7 %fusion.90 = f32[32,128,2,32]{1,3,2,0:T(8,128)} fusion(f32[32,128,2,32]{1,3,2,0:T(8,128)S(1)} %fusion.87, bf16[2,32,512,1]{2,1,0,3:T(8,128)(2,1)S(1)} %bitcast.116, s32[512]{0:T(512)S(1)} %get-tuple-element.20, s32[]{:T(128)} %bitcast.3, s32[32,128]{1,0:T(8,128)S(1)} %add_multiply_fusion), kind=kOutput, calls=%fused_computation.95 | convolution fusion | flops 291766272 | bytes 2181124 | tf_op jit(solution)/shard_map/cra,apj->pcrj/dot_general | solution.py:68
  38.3 14.0 %all-to-all-start = ((f32[64,32,128]{2,1,0:T(8,128)}), f32[64,32,128]{2,1,0:T(8,128)S(1)}, u32[]{:S(2)}, u32[]{:S(2)}) async-start(f32[64,32,128]{2,1,0:T(8,128)} %bitcast.37), calls=%async_computation | async-start | bytes 2097152 | tf_op jit(solution)/shard_map/all_to_all | solution.py:77
  52.3 27.1 %all-to-all-done = f32[64,32,128]{2,1,0:T(8,128)S(1)} async-done(((f32[64,32,128]{2,1,0:T(8,128)}), f32[64,32,128]{2,1,0:T(8,128)S(1)}, u32[]{:S(2)}, u32[]{:S(2)}) %all-to-all-start) | async-done | bytes 1048608 | tf_op jit(solution)/shard_map/all_to_all | solution.py:77
  79.5 19.0 %all_gather.3 = f32[512,256]{1,0:T(8,128)S(1)} all-gather(f32[32,256]{1,0:T(8,128)S(1)} %copy_bitcast_fusion), channel_id=1, replica_groups=mesh['param'=32,'ey'=8,'ec'=2] {'ey','ec'}, dimensions={0}, use_global_device_ids=true | all-gather | bytes 557056 | tf_op jit(solution)/shard_map/all_gather | solution.py:81
  100.3 3.3 %collective-permute-start.1 = (f32[8480]{0:T(1024)S(1)}, f32[8480]{0:T(1024)S(1)}, u32[]{:S(2)}, u32[]{:S(2)}) collective-permute-start(f32[8480]{0:T(1024)S(1)} %concatenate.11), channel_id=1, source_target_pairs={{0,16},{16,0},{32,48},{48,32},{64,80},{80,64},{96,112},{112,96},{1... | collective-permute-start | bytes 101768 | tf_op jit(solution)/shard_map/ppermute | solution.py:33
  103.6 2.6 %collective-permute-done.1 = f32[8480]{0:T(1024)S(1)} collective-permute-done((f32[8480]{0:T(1024)S(1)}, f32[8480]{0:T(1024)S(1)}, u32[]{:S(2)}, u32[]{:S(2)}) %collective-permute-start.1) | collective-permute-done | bytes 33952 | tf_op jit(solution)/shard_map/ppermute | solution.py:33
  106.2 4.8 %collective-permute-start.2 = (f32[8480]{0:T(1024)S(1)}, f32[8480]{0:T(1024)S(1)}, u32[]{:S(2)}, u32[]{:S(2)}) collective-permute-start(f32[8480]{0:T(1024)S(1)} %add.269), channel_id=1, source_target_pairs={{0,32},{16,48},{32,0},{48,16},{64,96},{80,112},{96,64},{112,80},{1... | collective-permute-start | bytes 101768 | tf_op jit(solution)/shard_map/ppermute | solution.py:33
  111.0 1.9 %collective-permute-done.2 = f32[8480]{0:T(1024)S(1)} collective-permute-done((f32[8480]{0:T(1024)S(1)}, f32[8480]{0:T(1024)S(1)}, u32[]{:S(2)}, u32[]{:S(2)}) %collective-permute-start.2) | collective-permute-done | bytes 33952 | tf_op jit(solution)/shard_map/ppermute | solution.py:33
  112.9 5.2 %collective-permute-start.3 = (f32[8480]{0:T(1024)S(1)}, f32[8480]{0:T(1024)S(1)}, u32[]{:S(2)}, u32[]{:S(2)}) collective-permute-start(f32[8480]{0:T(1024)S(1)} %add.270), channel_id=1, source_target_pairs={{0,64},{16,80},{32,96},{48,112},{64,0},{80,16},{96,32},{112,48},{1... | collective-permute-start | bytes 101768 | tf_op jit(solution)/shard_map/ppermute | solution.py:33
  118.2 4.5 %collective-permute-done.3 = f32[8480]{0:T(1024)S(1)} collective-permute-done((f32[8480]{0:T(1024)S(1)}, f32[8480]{0:T(1024)S(1)}, u32[]{:S(2)}, u32[]{:S(2)}) %collective-permute-start.3) | collective-permute-done | bytes 33952 | tf_op jit(solution)/shard_map/ppermute | solution.py:33
  122.7 3.4 %collective-permute-start.4 = (f32[8480]{0:T(1024)S(1)}, f32[8480]{0:T(1024)S(1)}, u32[]{:S(2)}, u32[]{:S(2)}) collective-permute-start(f32[8480]{0:T(1024)S(1)} %add.271), channel_id=1, source_target_pairs={{0,128},{16,144},{32,160},{48,176},{64,192},{80,208},{96,224},{112... | collective-permute-start | bytes 101768 | tf_op jit(solution)/shard_map/ppermute | solution.py:33
  126.1 2.4 %collective-permute-done.4 = f32[8480]{0:T(1024)S(1)} collective-permute-done((f32[8480]{0:T(1024)S(1)}, f32[8480]{0:T(1024)S(1)}, u32[]{:S(2)}, u32[]{:S(2)}) %collective-permute-start.4) | collective-permute-done | bytes 33952 | tf_op jit(solution)/shard_map/ppermute | solution.py:33
  128.5 4.0 %collective-permute-start.5 = (f32[8480]{0:T(1024)S(1)}, f32[8480]{0:T(1024)S(1)}, u32[]{:S(2)}, u32[]{:S(2)}) collective-permute-start(f32[8480]{0:T(1024)S(1)} %add.272), channel_id=1, source_target_pairs={{0,256},{16,272},{32,288},{48,304},{64,320},{80,336},{96,352},{112... | collective-permute-start | bytes 101768 | tf_op jit(solution)/shard_map/ppermute | solution.py:33
  132.5 3.3 %collective-permute-done.5 = f32[8480]{0:T(1024)S(1)} collective-permute-done((f32[8480]{0:T(1024)S(1)}, f32[8480]{0:T(1024)S(1)}, u32[]{:S(2)}, u32[]{:S(2)}) %collective-permute-start.5) | collective-permute-done | bytes 33952 | tf_op jit(solution)/shard_map/ppermute | solution.py:33
  (33 shorter events, 4.7 us)
Async XLA Ops:
  0.6 8.2 %copy-start = (bf16[32,4096]{1,0:T(8,128)(2,1)S(1)}, bf16[32,4096]{1,0:T(8,128)(2,1)}, u32[]{:S(2)}) copy-start(bf16[32,4096]{1,0:T(8,128)(2,1)} %param.3) | copy-start | bytes 786436
  5.0 3.8 %collective-permute-start = (f32[32,4096]{1,0:T(8,128)S(1)}, f32[32,4096]{1,0:T(8,128)S(1)}, u32[]{:S(2)}, u32[]{:S(2)}) collective-permute-start(f32[32,4096]{1,0:T(8,128)S(1)} %convert_element_type.9), channel_id=1, source_target_pairs={{0,1},{1,0},{2,3},{3,2},{4,5},{5,4},{6,7},{7,6},{8,9},{9,8},{10,11... | collective-permute-start | bytes 1572872 | tf_op jit(solution)/shard_map/ppermute | solution.py:53
  38.3 14.0 %copy-start.1 = (s32[256]{0:T(256)S(1)}, s32[256]{0:T(256)}, u32[]{:S(2)}) copy-start(s32[256]{0:T(256)} %param.5) | copy-start | bytes 3076
  38.3 41.1 %all-to-all-start = ((f32[64,32,128]{2,1,0:T(8,128)}), f32[64,32,128]{2,1,0:T(8,128)S(1)}, u32[]{:S(2)}, u32[]{:S(2)}) async-start(f32[64,32,128]{2,1,0:T(8,128)} %bitcast.37), calls=%async_computation | async-start | bytes 2097152 | tf_op jit(solution)/shard_map/all_to_all | solution.py:77
  100.3 5.8 %collective-permute-start.1 = (f32[8480]{0:T(1024)S(1)}, f32[8480]{0:T(1024)S(1)}, u32[]{:S(2)}, u32[]{:S(2)}) collective-permute-start(f32[8480]{0:T(1024)S(1)} %concatenate.11), channel_id=1, source_target_pairs={{0,16},{16,0},{32,48},{48,32},{64,80},{80,64},{96,112},{112,96},{1... | collective-permute-start | bytes 101768 | tf_op jit(solution)/shard_map/ppermute | solution.py:33
  106.2 6.7 %collective-permute-start.2 = (f32[8480]{0:T(1024)S(1)}, f32[8480]{0:T(1024)S(1)}, u32[]{:S(2)}, u32[]{:S(2)}) collective-permute-start(f32[8480]{0:T(1024)S(1)} %add.269), channel_id=1, source_target_pairs={{0,32},{16,48},{32,0},{48,16},{64,96},{80,112},{96,64},{112,80},{1... | collective-permute-start | bytes 101768 | tf_op jit(solution)/shard_map/ppermute | solution.py:33
  112.9 9.7 %collective-permute-start.3 = (f32[8480]{0:T(1024)S(1)}, f32[8480]{0:T(1024)S(1)}, u32[]{:S(2)}, u32[]{:S(2)}) collective-permute-start(f32[8480]{0:T(1024)S(1)} %add.270), channel_id=1, source_target_pairs={{0,64},{16,80},{32,96},{48,112},{64,0},{80,16},{96,32},{112,48},{1... | collective-permute-start | bytes 101768 | tf_op jit(solution)/shard_map/ppermute | solution.py:33
  122.7 5.8 %collective-permute-start.4 = (f32[8480]{0:T(1024)S(1)}, f32[8480]{0:T(1024)S(1)}, u32[]{:S(2)}, u32[]{:S(2)}) collective-permute-start(f32[8480]{0:T(1024)S(1)} %add.271), channel_id=1, source_target_pairs={{0,128},{16,144},{32,160},{48,176},{64,192},{80,208},{96,224},{112... | collective-permute-start | bytes 101768 | tf_op jit(solution)/shard_map/ppermute | solution.py:33
  128.5 7.3 %collective-permute-start.5 = (f32[8480]{0:T(1024)S(1)}, f32[8480]{0:T(1024)S(1)}, u32[]{:S(2)}, u32[]{:S(2)}) collective-permute-start(f32[8480]{0:T(1024)S(1)} %add.272), channel_id=1, source_target_pairs={{0,256},{16,272},{32,288},{48,304},{64,320},{80,336},{96,352},{112... | collective-permute-start | bytes 101768 | tf_op jit(solution)/shard_map/ppermute | solution.py:33

commit v6 on v4

--- a/solution.py
+++ b/solution.py
@@ -9,19 +9,20 @@
 norm_eps = 1e-06
 
 
-def hash_terms(sign_hash_keys, first_row, row_count, col_ids):
+def hash_terms(sign_hash_keys, row_ids, col_ids):
     mult_row = sign_hash_keys[0] | 1
     mult_col = sign_hash_keys[1] | 1
     seed_add = sign_hash_keys[2]
-    row_ids = first_row + lax.iota(jnp.int32, row_count)
-    return row_ids * mult_row + seed_add, col_ids * mult_col
+    mix_mult = jnp.broadcast_to(sign_hash_keys[3] | 1, col_ids.shape)
+    terms = jnp.stack([row_ids * mult_row + seed_add, col_ids * mult_col, mix_mult])
+    terms = lax.optimization_barrier(terms)
+    return terms[0], terms[1], terms[2]
 
 
-def sign_block(sign_hash_keys, row_terms, col_terms):
-    mix_mult = sign_hash_keys[3] | 1
+def sign_block(mix_mult, row_terms, col_terms):
     hashed = row_terms[:, None] + col_terms[None, :]
     hashed = hashed ^ lax.shift_right_logical(hashed, jnp.full_like(hashed, 16))
-    hashed = hashed * mix_mult
+    hashed = hashed * mix_mult[None, :]
     hashed = hashed ^ lax.shift_right_logical(hashed, jnp.full_like(hashed, 13))
     hashed = hashed * jnp.int32(-1028477387)
     hashed = hashed ^ lax.shift_right_logical(hashed, jnp.full_like(hashed, 16))
@@ -49,22 +50,23 @@
     col_width = K // param_count
     half_width = col_width // 2
 
-    unit = ((sign_hash_keys[3] | 1) & 1).astype(jnp.float32)
-    partner = lax.ppermute(adapter_gradients.astype(jnp.float32), "ec", swap) * unit
+    owner = lax.iota(jnp.int32, param_count)[:, None] * col_width
+    col_ids = (owner + core * half_width + lax.iota(jnp.int32, half_width)[None, :]).reshape(-1)
+    row_ids = row_base + lax.iota(jnp.int32, resident_rows)
+    row_terms, col_terms, mix_mult = hash_terms(sign_hash_keys, row_ids, col_ids)
+    unit = (mix_mult[:resident_rows] & 1).astype(jnp.float32)
+    partner = lax.ppermute(adapter_gradients.astype(jnp.float32), "ec", swap) * unit[None, :]
     partner = partner.astype(jnp.bfloat16)
     pair_gradients = jnp.where(
         core == 0,
         jnp.concatenate([adapter_gradients, partner], axis=0),
         jnp.concatenate([partner, adapter_gradients], axis=0),
     )
-    owner = lax.iota(jnp.int32, param_count)[:, None] * col_width
-    col_ids = (owner + core * half_width + lax.iota(jnp.int32, half_width)[None, :]).reshape(-1)
-    row_terms, col_terms = hash_terms(sign_hash_keys, row_base, resident_rows, col_ids)
     totals = None
     for tile in range(turn_count):
         start_offset = tile * rows_per_tile
         gradient_slab = pair_gradients[:, start_offset:start_offset + rows_per_tile]
-        signs = sign_block(sign_hash_keys, row_terms[start_offset:start_offset + rows_per_tile], col_terms)
+        signs = sign_block(mix_mult, row_terms[start_offset:start_offset + rows_per_tile], col_terms)
         term = jnp.einsum(
             "cra,apj->pcrj",
             gradient_slab.reshape(2, resident_example, rows_per_tile),

time: 136 us -> 136 us (level)
  no operation moved by 1% of the time
where the time goes in v6:
time: 136 us
  waiting for transfers between devices  41.8 us (31%)
  starting transfers between devices  36.8 us (27%)
  matrix products  29.7 us (22%)
  blocking collectives  19 us (14%)
  other arithmetic  3.25 us (2%)
  between operations  2.77 us (2%)
  local copies, waits for them, and re-layouts  2.69 us (2%)
    dot_general x8, matrix products, local(): jnp.einsum('cra,apj->pcrj', gradient_slab.reshape(2, resident_example, ro...  29.3 us
    all_to_all x1, waiting for transfers between devices, local(): blocks = lax.all_to_all(blocks, ('param', 'ec'), 0, 0, tiled=True)  27.1 us
    ppermute x5, starting transfers between devices, butterfly_sum(): values = values + lax.ppermute(values, axis, pairs)  20.8 us
    all_gather x1, blocking collectives, local(): pool_rows = lax.all_gather(projected, ('ey', 'ec'), axis=0, tiled=True)  19 us
    ppermute x5, waiting for transfers between devices, butterfly_sum(): values = values + lax.ppermute(values, axis, pairs)  14.7 us
    all_to_all x1, starting transfers between devices, local(): blocks = lax.all_to_all(blocks, ('param', 'ec'), 0, 0, tiled=True)  14.1 us
  transfers between devices with their start and end apart: 7, of which 6 were waited for; matrix products, arithmetic and copies ran while one was open for 2% of the time, Pallas kernels for 0%

profile of v6, /device:TPU:2, one launch (start us, length us, event | category | flops | bytes accessed | tf_op | source)
XLA Modules:
  0.0 136.0 jit_solution(7700322125907490094)
XLA Ops:
  0.6 1.1 convert_element_type.10
  1.7 1.9 %collective-permute-start = (f32[32,4096]{1,0:T(8,128)S(1)}, f32[32,4096]{1,0:T(8,128)S(1)}, u32[]{:S(2)}, u32[]{:S(2)}) collective-permute-start(f32[32,4096]{1,0:T(8,128)S(1)} %convert_element_type.10), channel_id=1, source_target_pairs={{0,1},{1,0},{2,3},{3,2},{4,5},{5,4},{6,7},{7,6},{8,9},{9,8},{10,11... | collective-permute-start | bytes 1572872 | tf_op jit(solution)/shard_map/ppermute | solution.py:58
  3.6 1.5 %fusion.153 = (s32[1]{0:T(128)}, s32[1]{0:T(128)}, s32[1]{0:T(128)}, s32[1]{0:T(128)}) fusion(s32[4]{0:T(128)} %param.4), kind=kLoop, calls=%fused_computation.174 | loop fusion | bytes 32 | tf_op jit(solution)/shard_map/slice | solution.py:16
  8.2 3.5 %fusion.48 = f32[32,128,2,32]{1,3,2,0:T(8,128)S(1)} fusion(bf16[2,32,512,1]{2,1,0,3:T(8,128)(2,1)S(1)} %bitcast.135, s32[512]{0:T(512)S(1)} %bitcast.161, s32[32,128]{1,0:T(8,128)S(1)} %bitcast.146, s32[32,128]{1,0:T(8,128)S(1)} %bitcast.138), kind=kOutput, calls=%fused_computation.69 | convolution fusion | flops 291504128 | bytes 1148928 | tf_op jit(solution)/shard_map/cra,apj->pcrj/dot_general | solution.py:70
  11.7 3.5 %fusion.50 = f32[32,128,2,32]{1,3,2,0:T(8,128)S(1)} fusion(bf16[2,32,512,1]{2,1,0,3:T(8,128)(2,1)S(1)} %bitcast.134, s32[512]{0:T(512)S(1)} %bitcast.160, s32[32,128]{1,0:T(8,128)S(1)} %bitcast.147, s32[32,128]{1,0:T(8,128)S(1)} %bitcast.139), kind=kOutput, calls=%fused_computation.70 | convolution fusion | flops 291504128 | bytes 1148928 | tf_op jit(solution)/shard_map/cra,apj->pcrj/dot_general | solution.py:70
  15.1 3.5 %fusion.52 = f32[32,128,2,32]{1,3,2,0:T(8,128)S(1)} fusion(bf16[2,32,512,1]{2,1,0,3:T(8,128)(2,1)S(1)} %bitcast.133, s32[512]{0:T(512)S(1)} %bitcast.159, s32[32,128]{1,0:T(8,128)S(1)} %bitcast.148, s32[32,128]{1,0:T(8,128)S(1)} %bitcast.140), kind=kOutput, calls=%fused_computation.71 | convolution fusion | flops 291504128 | bytes 1148928 | tf_op jit(solution)/shard_map/cra,apj->pcrj/dot_general | solution.py:70
  18.6 3.6 %fusion.44 = f32[32,128,2,32]{1,3,2,0:T(8,128)S(1)} fusion(bf16[2,32,512,1]{2,1,0,3:T(8,128)(2,1)S(1)} %bitcast.132, s32[512]{0:T(512)S(1)} %bitcast.158, s32[32,128]{1,0:T(8,128)S(1)} %bitcast.149, s32[32,128]{1,0:T(8,128)S(1)} %bitcast.141), kind=kOutput, calls=%fused_computation.67 | convolution fusion | flops 291504128 | bytes 1148928 | tf_op jit(solution)/shard_map/cra,apj->pcrj/dot_general | solution.py:70
  22.2 3.5 %fusion.42 = f32[32,128,2,32]{1,3,2,0:T(8,128)S(1)} fusion(bf16[2,32,512,1]{2,1,0,3:T(8,128)(2,1)S(1)} %bitcast.131, s32[512]{0:T(512)S(1)} %bitcast.157, s32[32,128]{1,0:T(8,128)S(1)} %bitcast.150, s32[32,128]{1,0:T(8,128)S(1)} %bitcast.142), kind=kOutput, calls=%fused_computation.66 | convolution fusion | flops 291504128 | bytes 1148928 | tf_op jit(solution)/shard_map/cra,apj->pcrj/dot_general | solution.py:70
  25.7 3.5 %fusion.78 = f32[32,128,2,32]{1,3,2,0:T(8,128)S(1)} fusion(f32[32,128,2,32]{1,3,2,0:T(8,128)S(1)} %fusion.48, f32[32,128,2,32]{1,3,2,0:T(8,128)S(1)} %fusion.50, f32[32,128,2,32]{1,3,2,0:T(8,128)S(1)} %fusion.52, bf16[2,32,512,1]{2,1,0,3:T(8,128)(2,1)S(1)} %bitcast.130, s32[32,128]{1,0:T(8,128)S(1)} %bitcast.151, s32[32,128]{1,0:T(8,128)S(1)} %bitcast.143, ...), kind=kOutput, calls=%fused_computation.91 | convolution fusion | flops 292290560 | bytes 4294656 | tf_op jit(solution)/shard_map/cra,apj->pcrj/dot_general | solution.py:70
  29.2 3.5 %fusion.87 = f32[32,128,2,32]{1,3,2,0:T(8,128)S(1)} fusion(f32[32,128,2,32]{1,3,2,0:T(8,128)S(1)} %fusion.42, f32[32,128,2,32]{1,3,2,0:T(8,128)S(1)} %fusion.44, f32[32,128,2,32]{1,3,2,0:T(8,128)S(1)} %fusion.78, bf16[2,32,512,1]{2,1,0,3:T(8,128)(2,1)S(1)} %bitcast.129, s32[512]{0:T(512)S(1)} %bitcast.155, s32[32,128]{1,0:T(8,128)S(1)} %bitcast.152, ...), kind=kOutput, calls=%fused_computation.94 | convolution fusion | flops 292290560 | bytes 4294656 | tf_op jit(solution)/shard_map/cra,apj->pcrj/dot_general | solution.py:70
  32.8 4.7 %fusion.90 = f32[32,128,2,32]{1,3,2,0:T(8,128)} fusion(f32[32,128,2,32]{1,3,2,0:T(8,128)S(1)} %fusion.87, bf16[2,32,512,1]{2,1,0,3:T(8,128)(2,1)S(1)} %bitcast.128, s32[512]{0:T(512)S(1)} %bitcast.154, s32[32,128]{1,0:T(8,128)S(1)} %bitcast.153, s32[32,128]{1,0:T(8,128)S(1)} %bitcast.145), kind=kOutput, calls=%fused_computation.95 | convolution fusion | flops 291766272 | bytes 2197504 | tf_op jit(solution)/shard_map/cra,apj->pcrj/dot_general | solution.py:70
  37.5 14.1 %all-to-all-start = ((f32[64,32,128]{2,1,0:T(8,128)}), f32[64,32,128]{2,1,0:T(8,128)S(1)}, u32[]{:S(2)}, u32[]{:S(2)}) async-start(f32[64,32,128]{2,1,0:T(8,128)} %bitcast.49), calls=%async_computation | async-start | bytes 2097152 | tf_op jit(solution)/shard_map/all_to_all | solution.py:79
  51.7 27.1 %all-to-all-done = f32[64,32,128]{2,1,0:T(8,128)S(1)} async-done(((f32[64,32,128]{2,1,0:T(8,128)}), f32[64,32,128]{2,1,0:T(8,128)S(1)}, u32[]{:S(2)}, u32[]{:S(2)}) %all-to-all-start) | async-done | bytes 1048608 | tf_op jit(solution)/shard_map/all_to_all | solution.py:79
  78.8 19.0 %all_gather.3 = f32[512,256]{1,0:T(8,128)S(1)} all-gather(f32[32,256]{1,0:T(8,128)S(1)} %copy_bitcast_fusion), channel_id=1, replica_groups=mesh['param'=32,'ey'=8,'ec'=2] {'ey','ec'}, dimensions={0}, use_global_device_ids=true | all-gather | bytes 557056 | tf_op jit(solution)/shard_map/all_gather | solution.py:83
  99.6 3.3 %collective-permute-start.1 = (f32[8480]{0:T(1024)S(1)}, f32[8480]{0:T(1024)S(1)}, u32[]{:S(2)}, u32[]{:S(2)}) collective-permute-start(f32[8480]{0:T(1024)S(1)} %concatenate.11), channel_id=1, source_target_pairs={{0,16},{16,0},{32,48},{48,32},{64,80},{80,64},{96,112},{112,96},{1... | collective-permute-start | bytes 101768 | tf_op jit(solution)/shard_map/ppermute | solution.py:36
  102.9 2.6 %collective-permute-done.1 = f32[8480]{0:T(1024)S(1)} collective-permute-done((f32[8480]{0:T(1024)S(1)}, f32[8480]{0:T(1024)S(1)}, u32[]{:S(2)}, u32[]{:S(2)}) %collective-permute-start.1) | collective-permute-done | bytes 33952 | tf_op jit(solution)/shard_map/ppermute | solution.py:36
  105.5 4.8 %collective-permute-start.2 = (f32[8480]{0:T(1024)S(1)}, f32[8480]{0:T(1024)S(1)}, u32[]{:S(2)}, u32[]{:S(2)}) collective-permute-start(f32[8480]{0:T(1024)S(1)} %add.314), channel_id=1, source_target_pairs={{0,32},{16,48},{32,0},{48,16},{64,96},{80,112},{96,64},{112,80},{1... | collective-permute-start | bytes 101768 | tf_op jit(solution)/shard_map/ppermute | solution.py:36
  110.3 1.9 %collective-permute-done.2 = f32[8480]{0:T(1024)S(1)} collective-permute-done((f32[8480]{0:T(1024)S(1)}, f32[8480]{0:T(1024)S(1)}, u32[]{:S(2)}, u32[]{:S(2)}) %collective-permute-start.2) | collective-permute-done | bytes 33952 | tf_op jit(solution)/shard_map/ppermute | solution.py:36
  112.2 5.2 %collective-permute-start.3 = (f32[8480]{0:T(1024)S(1)}, f32[8480]{0:T(1024)S(1)}, u32[]{:S(2)}, u32[]{:S(2)}) collective-permute-start(f32[8480]{0:T(1024)S(1)} %add.315), channel_id=1, source_target_pairs={{0,64},{16,80},{32,96},{48,112},{64,0},{80,16},{96,32},{112,48},{1... | collective-permute-start | bytes 101768 | tf_op jit(solution)/shard_map/ppermute | solution.py:36
  117.5 4.5 %collective-permute-done.3 = f32[8480]{0:T(1024)S(1)} collective-permute-done((f32[8480]{0:T(1024)S(1)}, f32[8480]{0:T(1024)S(1)}, u32[]{:S(2)}, u32[]{:S(2)}) %collective-permute-start.3) | collective-permute-done | bytes 33952 | tf_op jit(solution)/shard_map/ppermute | solution.py:36
  122.0 3.4 %collective-permute-start.4 = (f32[8480]{0:T(1024)S(1)}, f32[8480]{0:T(1024)S(1)}, u32[]{:S(2)}, u32[]{:S(2)}) collective-permute-start(f32[8480]{0:T(1024)S(1)} %add.316), channel_id=1, source_target_pairs={{0,128},{16,144},{32,160},{48,176},{64,192},{80,208},{96,224},{112... | collective-permute-start | bytes 101768 | tf_op jit(solution)/shard_map/ppermute | solution.py:36
  125.4 2.4 %collective-permute-done.4 = f32[8480]{0:T(1024)S(1)} collective-permute-done((f32[8480]{0:T(1024)S(1)}, f32[8480]{0:T(1024)S(1)}, u32[]{:S(2)}, u32[]{:S(2)}) %collective-permute-start.4) | collective-permute-done | bytes 33952 | tf_op jit(solution)/shard_map/ppermute | solution.py:36
  127.8 4.0 %collective-permute-start.5 = (f32[8480]{0:T(1024)S(1)}, f32[8480]{0:T(1024)S(1)}, u32[]{:S(2)}, u32[]{:S(2)}) collective-permute-start(f32[8480]{0:T(1024)S(1)} %add.317), channel_id=1, source_target_pairs={{0,256},{16,272},{32,288},{48,304},{64,320},{80,336},{96,352},{112... | collective-permute-start | bytes 101768 | tf_op jit(solution)/shard_map/ppermute | solution.py:36
  131.9 3.3 %collective-permute-done.5 = f32[8480]{0:T(1024)S(1)} collective-permute-done((f32[8480]{0:T(1024)S(1)}, f32[8480]{0:T(1024)S(1)}, u32[]{:S(2)}, u32[]{:S(2)}) %collective-permute-start.5) | collective-permute-done | bytes 33952 | tf_op jit(solution)/shard_map/ppermute | solution.py:36
  (36 shorter events, 3.8 us)
Async XLA Ops:
  0.6 7.4 %copy-start = (bf16[32,4096]{1,0:T(8,128)(2,1)S(1)}, bf16[32,4096]{1,0:T(8,128)(2,1)}, u32[]{:S(2)}) copy-start(bf16[32,4096]{1,0:T(8,128)(2,1)} %param.3) | copy-start | bytes 786436
  1.7 6.3 %collective-permute-start = (f32[32,4096]{1,0:T(8,128)S(1)}, f32[32,4096]{1,0:T(8,128)S(1)}, u32[]{:S(2)}, u32[]{:S(2)}) collective-permute-start(f32[32,4096]{1,0:T(8,128)S(1)} %convert_element_type.10), channel_id=1, source_target_pairs={{0,1},{1,0},{2,3},{3,2},{4,5},{5,4},{6,7},{7,6},{8,9},{9,8},{10,11... | collective-permute-start | bytes 1572872 | tf_op jit(solution)/shard_map/ppermute | solution.py:58
  37.5 14.1 %copy-start.1 = (s32[256]{0:T(256)S(1)}, s32[256]{0:T(256)}, u32[]{:S(2)}) copy-start(s32[256]{0:T(256)} %param.5) | copy-start | bytes 3076
  37.5 41.2 %all-to-all-start = ((f32[64,32,128]{2,1,0:T(8,128)}), f32[64,32,128]{2,1,0:T(8,128)S(1)}, u32[]{:S(2)}, u32[]{:S(2)}) async-start(f32[64,32,128]{2,1,0:T(8,128)} %bitcast.49), calls=%async_computation | async-start | bytes 2097152 | tf_op jit(solution)/shard_map/all_to_all | solution.py:79
  99.6 5.8 %collective-permute-start.1 = (f32[8480]{0:T(1024)S(1)}, f32[8480]{0:T(1024)S(1)}, u32[]{:S(2)}, u32[]{:S(2)}) collective-permute-start(f32[8480]{0:T(1024)S(1)} %concatenate.11), channel_id=1, source_target_pairs={{0,16},{16,0},{32,48},{48,32},{64,80},{80,64},{96,112},{112,96},{1... | collective-permute-start | bytes 101768 | tf_op jit(solution)/shard_map/ppermute | solution.py:36
  105.5 6.7 %collective-permute-start.2 = (f32[8480]{0:T(1024)S(1)}, f32[8480]{0:T(1024)S(1)}, u32[]{:S(2)}, u32[]{:S(2)}) collective-permute-start(f32[8480]{0:T(1024)S(1)} %add.314), channel_id=1, source_target_pairs={{0,32},{16,48},{32,0},{48,16},{64,96},{80,112},{96,64},{112,80},{1... | collective-permute-start | bytes 101768 | tf_op jit(solution)/shard_map/ppermute | solution.py:36
  112.2 9.7 %collective-permute-start.3 = (f32[8480]{0:T(1024)S(1)}, f32[8480]{0:T(1024)S(1)}, u32[]{:S(2)}, u32[]{:S(2)}) collective-permute-start(f32[8480]{0:T(1024)S(1)} %add.315), channel_id=1, source_target_pairs={{0,64},{16,80},{32,96},{48,112},{64,0},{80,16},{96,32},{112,48},{1... | collective-permute-start | bytes 101768 | tf_op jit(solution)/shard_map/ppermute | solution.py:36
  122.0 5.8 %collective-permute-start.4 = (f32[8480]{0:T(1024)S(1)}, f32[8480]{0:T(1024)S(1)}, u32[]{:S(2)}, u32[]{:S(2)}) collective-permute-start(f32[8480]{0:T(1024)S(1)} %add.316), channel_id=1, source_target_pairs={{0,128},{16,144},{32,160},{48,176},{64,192},{80,208},{96,224},{112... | collective-permute-start | bytes 101768 | tf_op jit(solution)/shard_map/ppermute | solution.py:36
  127.8 7.3 %collective-permute-start.5 = (f32[8480]{0:T(1024)S(1)}, f32[8480]{0:T(1024)S(1)}, u32[]{:S(2)}, u32[]{:S(2)}) collective-permute-start(f32[8480]{0:T(1024)S(1)} %add.317), channel_id=1, source_target_pairs={{0,256},{16,272},{32,288},{48,304},{64,320},{80,336},{96,352},{112... | collective-permute-start | bytes 101768 | tf_op jit(solution)/shard_map/ppermute | solution.py:36

commit v7 on v4

--- a/solution.py
+++ b/solution.py
@@ -79,7 +79,8 @@
     projected = jnp.transpose(blocks, (1, 0, 2)).reshape(resident_example, col_width)
 
     pool_rows = lax.all_gather(projected, ("ey", "ec"), axis=0, tiled=True)
-    target_rows = jnp.take(pool_rows, target_indices, axis=0)
+    picks = (target_indices[:, None] == lax.iota(jnp.int32, pool_rows.shape[0])[None, :]).astype(jnp.float32)
+    target_rows = jnp.dot(picks, pool_rows, precision=lax.Precision.HIGHEST)
     partial_dots = jnp.dot(projected, target_rows.T, precision=lax.Precision.HIGHEST)
     own_squares = jnp.sum(projected * projected, axis=1)
     target_squares = jnp.sum(target_rows * target_rows, axis=1)

time: 136 us -> 134 us (0.985)
  blocking collectives: 19 us -> 59.9 us
  waiting for transfers between devices: 41.8 us -> 14.7 us
  starting transfers between devices: 36.8 us -> 22.7 us
    all_to_all x0 -> x1, blocking collectives: none -> 40.9 us  [local(): blocks = lax.all_to_all(blocks, ('param', 'ec'), 0, 0, tiled=True)]
    all_to_all x1 -> x0, waiting for transfers between devices: 27.1 us -> none  [local(): blocks = lax.all_to_all(blocks, ('param', 'ec'), 0, 0, tiled=True)]
    all_to_all x1 -> x0, starting transfers between devices: 14.1 us -> none  [local(): blocks = lax.all_to_all(blocks, ('param', 'ec'), 0, 0, tiled=True)]
  transfers between devices with their start and end apart: 7 -> 6, of which waited for: 6 -> 5; matrix products, arithmetic and copies ran while one was open for 2% -> 2% of each run, Pallas kernels for 0% -> 0%
where the time goes in v7:
time: 134 us
  blocking collectives  59.9 us (45%)
  matrix products  29.2 us (22%)
  starting transfers between devices  22.7 us (17%)
  waiting for transfers between devices  14.7 us (11%)
  other arithmetic  2.91 us (2%)
  between operations  2.73 us (2%)
  local copies, waits for them, and re-layouts  1.65 us (1%)
    all_to_all x1, blocking collectives, local(): blocks = lax.all_to_all(blocks, ('param', 'ec'), 0, 0, tiled=True)  40.9 us
    dot_general x8, matrix products, local(): jnp.einsum('cra,apj->pcrj', gradient_slab.reshape(2, resident_example, ro...  28.3 us
    ppermute x5, starting transfers between devices, butterfly_sum(): values = values + lax.ppermute(values, axis, pairs)  20.8 us
    all_gather x1, blocking collectives, local(): pool_rows = lax.all_gather(projected, ('ey', 'ec'), axis=0, tiled=True)  19 us
    ppermute x5, waiting for transfers between devices, butterfly_sum(): values = values + lax.ppermute(values, axis, pairs)  14.7 us
  transfers between devices with their start and end apart: 6, of which 5 were waited for; matrix products, arithmetic and copies ran while one was open for 2% of the time, Pallas kernels for 0%

profile of v7, /device:TPU:2, one launch (start us, length us, event | category | flops | bytes accessed | tf_op | source)
XLA Modules:
  0.0 133.8 jit_solution(14204575090020934049)
XLA Ops:
  0.6 1.1 convert_element_type.10
  1.7 1.9 %collective-permute-start = (f32[32,4096]{1,0:T(8,128)S(1)}, f32[32,4096]{1,0:T(8,128)S(1)}, u32[]{:S(2)}, u32[]{:S(2)}) collective-permute-start(f32[32,4096]{1,0:T(8,128)S(1)} %convert_element_type.10), channel_id=1, source_target_pairs={{0,1},{1,0},{2,3},{3,2},{4,5},{5,4},{6,7},{7,6},{8,9},{9,8},{10,11... | collective-permute-start | bytes 1572872 | tf_op jit(solution)/shard_map/ppermute | solution.py:53
  3.6 1.5 %fusion.150 = (s32[1]{0:T(128)}, s32[1]{0:T(128)}, s32[1]{0:T(128)}, s32[1]{0:T(128)}) fusion(s32[4]{0:T(128)} %param.4), kind=kLoop, calls=%fused_computation.166 | loop fusion | bytes 32 | tf_op jit(solution)/shard_map/slice | solution.py:14
  8.0 3.5 %fusion.48 = f32[32,128,2,32]{1,3,2,0:T(8,128)S(1)} fusion(bf16[2,32,512,1]{2,1,0,3:T(8,128)(2,1)S(1)} %bitcast.126, s32[512]{0:T(512)S(1)} %get-tuple-element.14, s32[]{:T(128)} %bitcast.3, s32[32,128]{1,0:T(8,128)S(1)} %add_multiply_fusion), kind=kOutput, calls=%fused_computation.68 | convolution fusion | flops 291504128 | bytes 1132548 | tf_op jit(solution)/shard_map/cra,apj->pcrj/dot_general | solution.py:68
  11.4 3.5 %fusion.50 = f32[32,128,2,32]{1,3,2,0:T(8,128)S(1)} fusion(bf16[2,32,512,1]{2,1,0,3:T(8,128)(2,1)S(1)} %bitcast.125, s32[512]{0:T(512)S(1)} %get-tuple-element.15, s32[]{:T(128)} %bitcast.3, s32[32,128]{1,0:T(8,128)S(1)} %add_multiply_fusion), kind=kOutput, calls=%fused_computation.69 | convolution fusion | flops 291504128 | bytes 1132548 | tf_op jit(solution)/shard_map/cra,apj->pcrj/dot_general | solution.py:68
  14.9 3.5 %fusion.52 = f32[32,128,2,32]{1,3,2,0:T(8,128)S(1)} fusion(bf16[2,32,512,1]{2,1,0,3:T(8,128)(2,1)S(1)} %bitcast.124, s32[512]{0:T(512)S(1)} %get-tuple-element.16, s32[]{:T(128)} %bitcast.3, s32[32,128]{1,0:T(8,128)S(1)} %add_multiply_fusion), kind=kOutput, calls=%fused_computation.70 | convolution fusion | flops 291504128 | bytes 1132548 | tf_op jit(solution)/shard_map/cra,apj->pcrj/dot_general | solution.py:68
  18.4 3.6 %fusion.44 = f32[32,128,2,32]{1,3,2,0:T(8,128)S(1)} fusion(bf16[2,32,512,1]{2,1,0,3:T(8,128)(2,1)S(1)} %bitcast.123, s32[512]{0:T(512)S(1)} %get-tuple-element.12, s32[]{:T(128)} %bitcast.3, s32[32,128]{1,0:T(8,128)S(1)} %add_multiply_fusion), kind=kOutput, calls=%fused_computation.66 | convolution fusion | flops 291504128 | bytes 1132548 | tf_op jit(solution)/shard_map/cra,apj->pcrj/dot_general | solution.py:68
  22.0 3.5 %fusion.42 = f32[32,128,2,32]{1,3,2,0:T(8,128)S(1)} fusion(bf16[2,32,512,1]{2,1,0,3:T(8,128)(2,1)S(1)} %bitcast.122, s32[512]{0:T(512)S(1)} %get-tuple-element.11, s32[]{:T(128)} %bitcast.3, s32[32,128]{1,0:T(8,128)S(1)} %add_multiply_fusion), kind=kOutput, calls=%fused_computation.65 | convolution fusion | flops 291504128 | bytes 1132548 | tf_op jit(solution)/shard_map/cra,apj->pcrj/dot_general | solution.py:68
  25.5 3.5 %fusion.78 = f32[32,128,2,32]{1,3,2,0:T(8,128)S(1)} fusion(f32[32,128,2,32]{1,3,2,0:T(8,128)S(1)} %fusion.48, f32[32,128,2,32]{1,3,2,0:T(8,128)S(1)} %fusion.50, f32[32,128,2,32]{1,3,2,0:T(8,128)S(1)} %fusion.52, bf16[2,32,512,1]{2,1,0,3:T(8,128)(2,1)S(1)} %bitcast.121, s32[]{:T(128)} %bitcast.3, s32[32,128]{1,0:T(8,128)S(1)} %add_multiply_fusion, ...), kind=kOutput, calls=%fused_computation.90 | convolution fusion | flops 292290560 | bytes 4278276 | tf_op jit(solution)/shard_map/cra,apj->pcrj/dot_general | solution.py:68
  29.0 3.5 %fusion.87 = f32[32,128,2,32]{1,3,2,0:T(8,128)S(1)} fusion(f32[32,128,2,32]{1,3,2,0:T(8,128)S(1)} %fusion.42, f32[32,128,2,32]{1,3,2,0:T(8,128)S(1)} %fusion.44, f32[32,128,2,32]{1,3,2,0:T(8,128)S(1)} %fusion.78, bf16[2,32,512,1]{2,1,0,3:T(8,128)(2,1)S(1)} %bitcast.120, s32[512]{0:T(512)S(1)} %get-tuple-element.13, s32[]{:T(128)} %bitcast.3, ...), kind=kOutput, calls=%fused_computation.93 | convolution fusion | flops 292290560 | bytes 4278276 | tf_op jit(solution)/shard_map/cra,apj->pcrj/dot_general | solution.py:68
  32.6 3.7 %fusion.90 = f32[32,128,2,32]{1,3,2,0:T(8,128)S(1)} fusion(f32[32,128,2,32]{1,3,2,0:T(8,128)S(1)} %fusion.87, bf16[2,32,512,1]{2,1,0,3:T(8,128)(2,1)S(1)} %bitcast.119, s32[512]{0:T(512)S(1)} %get-tuple-element.10, s32[]{:T(128)} %bitcast.3, s32[32,128]{1,0:T(8,128)S(1)} %add_multiply_fusion), kind=kOutput, calls=%fused_computation.94 | convolution fusion | flops 291766272 | bytes 2181124 | tf_op jit(solution)/shard_map/cra,apj->pcrj/dot_general | solution.py:68
  36.3 40.9 %all_to_all.5 = f32[64,32,128]{2,1,0:T(8,128)S(1)} all-to-all(f32[64,32,128]{2,1,0:T(8,128)S(1)} %bitcast.117), channel_id=1, replica_groups=mesh['param'=32,'ey'=8,'ec'=2] {'param','ec'}, dimensions={0} | all-to-all | bytes 2097152 | tf_op jit(solution)/shard_map/all_to_all | solution.py:77
  77.4 19.0 %all_gather.3 = f32[512,256]{1,0:T(8,128)S(1)} all-gather(f32[32,256]{1,0:T(8,128)S(1)} %copy_bitcast_fusion), channel_id=1, replica_groups=mesh['param'=32,'ey'=8,'ec'=2] {'ey','ec'}, dimensions={0}, use_global_device_ids=true | all-gather | bytes 557056 | tf_op jit(solution)/shard_map/all_gather | solution.py:81
  97.4 3.3 %collective-permute-start.1 = (f32[8480]{0:T(1024)S(1)}, f32[8480]{0:T(1024)S(1)}, u32[]{:S(2)}, u32[]{:S(2)}) collective-permute-start(f32[8480]{0:T(1024)S(1)} %concatenate.11), channel_id=1, source_target_pairs={{0,16},{16,0},{32,48},{48,32},{64,80},{80,64},{96,112},{112,96},{1... | collective-permute-start | bytes 101768 | tf_op jit(solution)/shard_map/ppermute | solution.py:35
  100.7 2.6 %collective-permute-done.1 = f32[8480]{0:T(1024)S(1)} collective-permute-done((f32[8480]{0:T(1024)S(1)}, f32[8480]{0:T(1024)S(1)}, u32[]{:S(2)}, u32[]{:S(2)}) %collective-permute-start.1) | collective-permute-done | bytes 33952 | tf_op jit(solution)/shard_map/ppermute | solution.py:35
  103.3 4.8 %collective-permute-start.2 = (f32[8480]{0:T(1024)S(1)}, f32[8480]{0:T(1024)S(1)}, u32[]{:S(2)}, u32[]{:S(2)}) collective-permute-start(f32[8480]{0:T(1024)S(1)} %add.259), channel_id=1, source_target_pairs={{0,32},{16,48},{32,0},{48,16},{64,96},{80,112},{96,64},{112,80},{1... | collective-permute-start | bytes 101768 | tf_op jit(solution)/shard_map/ppermute | solution.py:35
  108.1 1.9 %collective-permute-done.2 = f32[8480]{0:T(1024)S(1)} collective-permute-done((f32[8480]{0:T(1024)S(1)}, f32[8480]{0:T(1024)S(1)}, u32[]{:S(2)}, u32[]{:S(2)}) %collective-permute-start.2) | collective-permute-done | bytes 33952 | tf_op jit(solution)/shard_map/ppermute | solution.py:35
  110.0 5.2 %collective-permute-start.3 = (f32[8480]{0:T(1024)S(1)}, f32[8480]{0:T(1024)S(1)}, u32[]{:S(2)}, u32[]{:S(2)}) collective-permute-start(f32[8480]{0:T(1024)S(1)} %add.260), channel_id=1, source_target_pairs={{0,64},{16,80},{32,96},{48,112},{64,0},{80,16},{96,32},{112,48},{1... | collective-permute-start | bytes 101768 | tf_op jit(solution)/shard_map/ppermute | solution.py:35
  115.3 4.5 %collective-permute-done.3 = f32[8480]{0:T(1024)S(1)} collective-permute-done((f32[8480]{0:T(1024)S(1)}, f32[8480]{0:T(1024)S(1)}, u32[]{:S(2)}, u32[]{:S(2)}) %collective-permute-start.3) | collective-permute-done | bytes 33952 | tf_op jit(solution)/shard_map/ppermute | solution.py:35
  119.8 3.4 %collective-permute-start.4 = (f32[8480]{0:T(1024)S(1)}, f32[8480]{0:T(1024)S(1)}, u32[]{:S(2)}, u32[]{:S(2)}) collective-permute-start(f32[8480]{0:T(1024)S(1)} %add.261), channel_id=1, source_target_pairs={{0,128},{16,144},{32,160},{48,176},{64,192},{80,208},{96,224},{112... | collective-permute-start | bytes 101768 | tf_op jit(solution)/shard_map/ppermute | solution.py:35
  123.2 2.4 %collective-permute-done.4 = f32[8480]{0:T(1024)S(1)} collective-permute-done((f32[8480]{0:T(1024)S(1)}, f32[8480]{0:T(1024)S(1)}, u32[]{:S(2)}, u32[]{:S(2)}) %collective-permute-start.4) | collective-permute-done | bytes 33952 | tf_op jit(solution)/shard_map/ppermute | solution.py:35
  125.6 4.0 %collective-permute-start.5 = (f32[8480]{0:T(1024)S(1)}, f32[8480]{0:T(1024)S(1)}, u32[]{:S(2)}, u32[]{:S(2)}) collective-permute-start(f32[8480]{0:T(1024)S(1)} %add.262), channel_id=1, source_target_pairs={{0,256},{16,272},{32,288},{48,304},{64,320},{80,336},{96,352},{112... | collective-permute-start | bytes 101768 | tf_op jit(solution)/shard_map/ppermute | solution.py:35
  129.6 3.3 %collective-permute-done.5 = f32[8480]{0:T(1024)S(1)} collective-permute-done((f32[8480]{0:T(1024)S(1)}, f32[8480]{0:T(1024)S(1)}, u32[]{:S(2)}, u32[]{:S(2)}) %collective-permute-start.5) | collective-permute-done | bytes 33952 | tf_op jit(solution)/shard_map/ppermute | solution.py:35
  133.1 0.7 multiply_multiply_fusion
  (28 shorter events, 2.2 us)
Async XLA Ops:
  0.6 7.2 %copy-start = (bf16[32,4096]{1,0:T(8,128)(2,1)S(1)}, bf16[32,4096]{1,0:T(8,128)(2,1)}, u32[]{:S(2)}) copy-start(bf16[32,4096]{1,0:T(8,128)(2,1)} %param.3) | copy-start | bytes 786436
  1.7 6.1 %collective-permute-start = (f32[32,4096]{1,0:T(8,128)S(1)}, f32[32,4096]{1,0:T(8,128)S(1)}, u32[]{:S(2)}, u32[]{:S(2)}) collective-permute-start(f32[32,4096]{1,0:T(8,128)S(1)} %convert_element_type.10), channel_id=1, source_target_pairs={{0,1},{1,0},{2,3},{3,2},{4,5},{5,4},{6,7},{7,6},{8,9},{9,8},{10,11... | collective-permute-start | bytes 1572872 | tf_op jit(solution)/shard_map/ppermute | solution.py:53
  77.2 19.2 %copy-start.1 = (s32[256]{0:T(256)S(1)}, s32[256]{0:T(256)}, u32[]{:S(2)}) copy-start(s32[256]{0:T(256)} %param.5) | copy-start | bytes 3076
  97.4 5.8 %collective-permute-start.1 = (f32[8480]{0:T(1024)S(1)}, f32[8480]{0:T(1024)S(1)}, u32[]{:S(2)}, u32[]{:S(2)}) collective-permute-start(f32[8480]{0:T(1024)S(1)} %concatenate.11), channel_id=1, source_target_pairs={{0,16},{16,0},{32,48},{48,32},{64,80},{80,64},{96,112},{112,96},{1... | collective-permute-start | bytes 101768 | tf_op jit(solution)/shard_map/ppermute | solution.py:35
  103.3 6.7 %collective-permute-start.2 = (f32[8480]{0:T(1024)S(1)}, f32[8480]{0:T(1024)S(1)}, u32[]{:S(2)}, u32[]{:S(2)}) collective-permute-start(f32[8480]{0:T(1024)S(1)} %add.259), channel_id=1, source_target_pairs={{0,32},{16,48},{32,0},{48,16},{64,96},{80,112},{96,64},{112,80},{1... | collective-permute-start | bytes 101768 | tf_op jit(solution)/shard_map/ppermute | solution.py:35
  110.0 9.7 %collective-permute-start.3 = (f32[8480]{0:T(1024)S(1)}, f32[8480]{0:T(1024)S(1)}, u32[]{:S(2)}, u32[]{:S(2)}) collective-permute-start(f32[8480]{0:T(1024)S(1)} %add.260), channel_id=1, source_target_pairs={{0,64},{16,80},{32,96},{48,112},{64,0},{80,16},{96,32},{112,48},{1... | collective-permute-start | bytes 101768 | tf_op jit(solution)/shard_map/ppermute | solution.py:35
  119.8 5.8 %collective-permute-start.4 = (f32[8480]{0:T(1024)S(1)}, f32[8480]{0:T(1024)S(1)}, u32[]{:S(2)}, u32[]{:S(2)}) collective-permute-start(f32[8480]{0:T(1024)S(1)} %add.261), channel_id=1, source_target_pairs={{0,128},{16,144},{32,160},{48,176},{64,192},{80,208},{96,224},{112... | collective-permute-start | bytes 101768 | tf_op jit(solution)/shard_map/ppermute | solution.py:35
  125.6 7.3 %collective-permute-start.5 = (f32[8480]{0:T(1024)S(1)}, f32[8480]{0:T(1024)S(1)}, u32[]{:S(2)}, u32[]{:S(2)}) collective-permute-start(f32[8480]{0:T(1024)S(1)} %add.262), channel_id=1, source_target_pairs={{0,256},{16,272},{32,288},{48,304},{64,320},{80,336},{96,352},{112... | collective-permute-start | bytes 101768 | tf_op jit(solution)/shard_map/ppermute | solution.py:35

commit v8 on v7

--- a/solution.py
+++ b/solution.py
@@ -42,7 +42,7 @@
     row_base = lax.axis_index("param") * jnp.int32(resident_rows)
     core = lax.axis_index("ec")
     swap = [(0, 1), (1, 0)]
-    turn_count = 8
+    turn_count = 4
     rows_per_tile = resident_rows // turn_count
     scale_k = jnp.float32(K)
     param_count = lax.psum(1, "param")

time: 134 us -> 133 us (level)
    dot_general x8 -> x4, matrix products: 28.3 us -> 27.4 us  [local(): jnp.einsum('cra,apj->pcrj', gradient_slab.reshape(2, resident_example, ro...]
where the time goes in v8:
time: 133 us
  blocking collectives  59.9 us (45%)
  matrix products  28.3 us (21%)
  starting transfers between devices  22.7 us (17%)
  waiting for transfers between devices  14.7 us (11%)
  other arithmetic  2.91 us (2%)
  between operations  2.7 us (2%)
  local copies, waits for them, and re-layouts  1.65 us (1%)
    all_to_all x1, blocking collectives, local(): blocks = lax.all_to_all(blocks, ('param', 'ec'), 0, 0, tiled=True)  40.9 us
    dot_general x4, matrix products, local(): jnp.einsum('cra,apj->pcrj', gradient_slab.reshape(2, resident_example, ro...  27.4 us
    ppermute x5, starting transfers between devices, butterfly_sum(): values = values + lax.ppermute(values, axis, pairs)  20.8 us
    all_gather x1, blocking collectives, local(): pool_rows = lax.all_gather(projected, ('ey', 'ec'), axis=0, tiled=True)  19 us
    ppermute x5, waiting for transfers between devices, butterfly_sum(): values = values + lax.ppermute(values, axis, pairs)  14.7 us
  transfers between devices with their start and end apart: 6, of which 5 were waited for; matrix products, arithmetic and copies ran while one was open for 2% of the time, Pallas kernels for 0%

profile of v8, /device:TPU:2, one launch (start us, length us, event | category | flops | bytes accessed | tf_op | source)
XLA Modules:
  0.0 132.9 jit_solution(12911021806161068723)
XLA Ops:
  0.6 1.1 convert_element_type.10
  1.7 1.9 %collective-permute-start = (f32[32,4096]{1,0:T(8,128)S(1)}, f32[32,4096]{1,0:T(8,128)S(1)}, u32[]{:S(2)}, u32[]{:S(2)}) collective-permute-start(f32[32,4096]{1,0:T(8,128)S(1)} %convert_element_type.10), channel_id=1, source_target_pairs={{0,1},{1,0},{2,3},{3,2},{4,5},{5,4},{6,7},{7,6},{8,9},{9,8},{10,11... | collective-permute-start | bytes 1572872 | tf_op jit(solution)/shard_map/ppermute | solution.py:53
  3.6 1.5 %fusion.78 = (s32[1]{0:T(128)}, s32[1]{0:T(128)}, s32[1]{0:T(128)}, s32[1]{0:T(128)}) fusion(s32[4]{0:T(128)} %param.4), kind=kLoop, calls=%fused_computation.94 | loop fusion | bytes 32 | tf_op jit(solution)/shard_map/slice | solution.py:14
  7.0 0.7 multiply_add_fusion
  8.0 6.7 %fusion.20 = f32[32,128,2,32]{1,3,2,0:T(8,128)S(1)} fusion(bf16[2,32,1024,1]{2,1,0,3:T(8,128)(2,1)S(1)} %bitcast.78, s32[1024]{0:T(1024)S(1)} %get-tuple-element.7, s32[]{:T(128)} %bitcast.3, s32[32,128]{1,0:T(8,128)S(1)} %add_multiply_fusion), kind=kOutput, calls=%fused_computation.32 | convolution fusion | flops 583008256 | bytes 1200132 | tf_op jit(solution)/shard_map/cra,apj->pcrj/dot_general | solution.py:68
  14.7 6.9 %fusion.22 = f32[32,128,2,32]{1,3,2,0:T(8,128)S(1)} fusion(bf16[2,32,1024,1]{2,1,0,3:T(8,128)(2,1)S(1)} %bitcast.77, s32[1024]{0:T(1024)S(1)} %get-tuple-element.8, s32[]{:T(128)} %bitcast.3, s32[32,128]{1,0:T(8,128)S(1)} %add_multiply_fusion), kind=kOutput, calls=%fused_computation.33 | convolution fusion | flops 583008256 | bytes 1200132 | tf_op jit(solution)/shard_map/cra,apj->pcrj/dot_general | solution.py:68
  21.6 6.7 %fusion.24 = f32[32,128,2,32]{1,3,2,0:T(8,128)S(1)} fusion(bf16[2,32,1024,1]{2,1,0,3:T(8,128)(2,1)S(1)} %bitcast.76, s32[1024]{0:T(1024)S(1)} %get-tuple-element.9, s32[]{:T(128)} %bitcast.3, s32[32,128]{1,0:T(8,128)S(1)} %add_multiply_fusion), kind=kOutput, calls=%fused_computation.34 | convolution fusion | flops 583008256 | bytes 1200132 | tf_op jit(solution)/shard_map/cra,apj->pcrj/dot_general | solution.py:68
  28.3 7.0 %fusion.42 = f32[32,128,2,32]{1,3,2,0:T(8,128)S(1)} fusion(f32[32,128,2,32]{1,3,2,0:T(8,128)S(1)} %fusion.20, f32[32,128,2,32]{1,3,2,0:T(8,128)S(1)} %fusion.22, f32[32,128,2,32]{1,3,2,0:T(8,128)S(1)} %fusion.24, bf16[2,32,1024,1]{2,1,0,3:T(8,128)(2,1)S(1)} %bitcast.75, s32[]{:T(128)} %bitcast.3, s32[32,128]{1,0:T(8,128)S(1)} %add_multiply_fusion, ...), kind=kOutput, calls=%fused_computation.46 | convolution fusion | flops 583794688 | bytes 4345860 | tf_op jit(solution)/shard_map/cra,apj->pcrj/dot_general | solution.py:68
  35.4 40.9 %all_to_all.5 = f32[64,32,128]{2,1,0:T(8,128)S(1)} all-to-all(f32[64,32,128]{2,1,0:T(8,128)S(1)} %bitcast.73), channel_id=1, replica_groups=mesh['param'=32,'ey'=8,'ec'=2] {'param','ec'}, dimensions={0} | all-to-all | bytes 2097152 | tf_op jit(solution)/shard_map/all_to_all | solution.py:77
  76.3 0.1 fusion.47
  76.5 19.0 %all_gather.3 = f32[512,256]{1,0:T(8,128)S(1)} all-gather(f32[32,256]{1,0:T(8,128)S(1)} %copy_bitcast_fusion), channel_id=1, replica_groups=mesh['param'=32,'ey'=8,'ec'=2] {'ey','ec'}, dimensions={0}, use_global_device_ids=true | all-gather | bytes 557056 | tf_op jit(solution)/shard_map/all_gather | solution.py:81
  95.5 0.7 multiply_reduce_fusion
  96.2 0.2 convolution_bitcast_fusion
  96.5 3.3 %collective-permute-start.1 = (f32[8480]{0:T(1024)S(1)}, f32[8480]{0:T(1024)S(1)}, u32[]{:S(2)}, u32[]{:S(2)}) collective-permute-start(f32[8480]{0:T(1024)S(1)} %concatenate.11), channel_id=1, source_target_pairs={{0,16},{16,0},{32,48},{48,32},{64,80},{80,64},{96,112},{112,96},{1... | collective-permute-start | bytes 101768 | tf_op jit(solution)/shard_map/ppermute | solution.py:35
  99.8 2.6 %collective-permute-done.1 = f32[8480]{0:T(1024)S(1)} collective-permute-done((f32[8480]{0:T(1024)S(1)}, f32[8480]{0:T(1024)S(1)}, u32[]{:S(2)}, u32[]{:S(2)}) %collective-permute-start.1) | collective-permute-done | bytes 33952 | tf_op jit(solution)/shard_map/ppermute | solution.py:35
  102.4 4.8 %collective-permute-start.2 = (f32[8480]{0:T(1024)S(1)}, f32[8480]{0:T(1024)S(1)}, u32[]{:S(2)}, u32[]{:S(2)}) collective-permute-start(f32[8480]{0:T(1024)S(1)} %add.170), channel_id=1, source_target_pairs={{0,32},{16,48},{32,0},{48,16},{64,96},{80,112},{96,64},{112,80},{1... | collective-permute-start | bytes 101768 | tf_op jit(solution)/shard_map/ppermute | solution.py:35
  107.2 1.9 %collective-permute-done.2 = f32[8480]{0:T(1024)S(1)} collective-permute-done((f32[8480]{0:T(1024)S(1)}, f32[8480]{0:T(1024)S(1)}, u32[]{:S(2)}, u32[]{:S(2)}) %collective-permute-start.2) | collective-permute-done | bytes 33952 | tf_op jit(solution)/shard_map/ppermute | solution.py:35
  109.1 5.2 %collective-permute-start.3 = (f32[8480]{0:T(1024)S(1)}, f32[8480]{0:T(1024)S(1)}, u32[]{:S(2)}, u32[]{:S(2)}) collective-permute-start(f32[8480]{0:T(1024)S(1)} %add.171), channel_id=1, source_target_pairs={{0,64},{16,80},{32,96},{48,112},{64,0},{80,16},{96,32},{112,48},{1... | collective-permute-start | bytes 101768 | tf_op jit(solution)/shard_map/ppermute | solution.py:35
  114.3 4.5 %collective-permute-done.3 = f32[8480]{0:T(1024)S(1)} collective-permute-done((f32[8480]{0:T(1024)S(1)}, f32[8480]{0:T(1024)S(1)}, u32[]{:S(2)}, u32[]{:S(2)}) %collective-permute-start.3) | collective-permute-done | bytes 33952 | tf_op jit(solution)/shard_map/ppermute | solution.py:35
  118.9 3.4 %collective-permute-start.4 = (f32[8480]{0:T(1024)S(1)}, f32[8480]{0:T(1024)S(1)}, u32[]{:S(2)}, u32[]{:S(2)}) collective-permute-start(f32[8480]{0:T(1024)S(1)} %add.172), channel_id=1, source_target_pairs={{0,128},{16,144},{32,160},{48,176},{64,192},{80,208},{96,224},{112... | collective-permute-start | bytes 101768 | tf_op jit(solution)/shard_map/ppermute | solution.py:35
  122.3 2.4 %collective-permute-done.4 = f32[8480]{0:T(1024)S(1)} collective-permute-done((f32[8480]{0:T(1024)S(1)}, f32[8480]{0:T(1024)S(1)}, u32[]{:S(2)}, u32[]{:S(2)}) %collective-permute-start.4) | collective-permute-done | bytes 33952 | tf_op jit(solution)/shard_map/ppermute | solution.py:35
  124.7 4.0 %collective-permute-start.5 = (f32[8480]{0:T(1024)S(1)}, f32[8480]{0:T(1024)S(1)}, u32[]{:S(2)}, u32[]{:S(2)}) collective-permute-start(f32[8480]{0:T(1024)S(1)} %add.173), channel_id=1, source_target_pairs={{0,256},{16,272},{32,288},{48,304},{64,320},{80,336},{96,352},{112... | collective-permute-start | bytes 101768 | tf_op jit(solution)/shard_map/ppermute | solution.py:35
  128.7 3.3 %collective-permute-done.5 = f32[8480]{0:T(1024)S(1)} collective-permute-done((f32[8480]{0:T(1024)S(1)}, f32[8480]{0:T(1024)S(1)}, u32[]{:S(2)}, u32[]{:S(2)}) %collective-permute-start.5) | collective-permute-done | bytes 33952 | tf_op jit(solution)/shard_map/ppermute | solution.py:35
  132.2 0.7 multiply_multiply_fusion
  (24 shorter events, 0.6 us)
Async XLA Ops:
  0.6 7.2 %copy-start = (bf16[32,4096]{1,0:T(8,128)(2,1)S(1)}, bf16[32,4096]{1,0:T(8,128)(2,1)}, u32[]{:S(2)}) copy-start(bf16[32,4096]{1,0:T(8,128)(2,1)} %param.3) | copy-start | bytes 786436
  1.7 6.1 %collective-permute-start = (f32[32,4096]{1,0:T(8,128)S(1)}, f32[32,4096]{1,0:T(8,128)S(1)}, u32[]{:S(2)}, u32[]{:S(2)}) collective-permute-start(f32[32,4096]{1,0:T(8,128)S(1)} %convert_element_type.10), channel_id=1, source_target_pairs={{0,1},{1,0},{2,3},{3,2},{4,5},{5,4},{6,7},{7,6},{8,9},{9,8},{10,11... | collective-permute-start | bytes 1572872 | tf_op jit(solution)/shard_map/ppermute | solution.py:53
  76.3 19.2 %copy-start.1 = (s32[256]{0:T(256)S(1)}, s32[256]{0:T(256)}, u32[]{:S(2)}) copy-start(s32[256]{0:T(256)} %param.5) | copy-start | bytes 3076
  96.5 5.8 %collective-permute-start.1 = (f32[8480]{0:T(1024)S(1)}, f32[8480]{0:T(1024)S(1)}, u32[]{:S(2)}, u32[]{:S(2)}) collective-permute-start(f32[8480]{0:T(1024)S(1)} %concatenate.11), channel_id=1, source_target_pairs={{0,16},{16,0},{32,48},{48,32},{64,80},{80,64},{96,112},{112,96},{1... | collective-permute-start | bytes 101768 | tf_op jit(solution)/shard_map/ppermute | solution.py:35
  102.4 6.7 %collective-permute-start.2 = (f32[8480]{0:T(1024)S(1)}, f32[8480]{0:T(1024)S(1)}, u32[]{:S(2)}, u32[]{:S(2)}) collective-permute-start(f32[8480]{0:T(1024)S(1)} %add.170), channel_id=1, source_target_pairs={{0,32},{16,48},{32,0},{48,16},{64,96},{80,112},{96,64},{112,80},{1... | collective-permute-start | bytes 101768 | tf_op jit(solution)/shard_map/ppermute | solution.py:35
  109.1 9.7 %collective-permute-start.3 = (f32[8480]{0:T(1024)S(1)}, f32[8480]{0:T(1024)S(1)}, u32[]{:S(2)}, u32[]{:S(2)}) collective-permute-start(f32[8480]{0:T(1024)S(1)} %add.171), channel_id=1, source_target_pairs={{0,64},{16,80},{32,96},{48,112},{64,0},{80,16},{96,32},{112,48},{1... | collective-permute-start | bytes 101768 | tf_op jit(solution)/shard_map/ppermute | solution.py:35
  118.9 5.8 %collective-permute-start.4 = (f32[8480]{0:T(1024)S(1)}, f32[8480]{0:T(1024)S(1)}, u32[]{:S(2)}, u32[]{:S(2)}) collective-permute-start(f32[8480]{0:T(1024)S(1)} %add.172), channel_id=1, source_target_pairs={{0,128},{16,144},{32,160},{48,176},{64,192},{80,208},{96,224},{112... | collective-permute-start | bytes 101768 | tf_op jit(solution)/shard_map/ppermute | solution.py:35
  124.7 7.3 %collective-permute-start.5 = (f32[8480]{0:T(1024)S(1)}, f32[8480]{0:T(1024)S(1)}, u32[]{:S(2)}, u32[]{:S(2)}) collective-permute-start(f32[8480]{0:T(1024)S(1)} %add.173), channel_id=1, source_target_pairs={{0,256},{16,272},{32,288},{48,304},{64,320},{80,336},{96,352},{112... | collective-permute-start | bytes 101768 | tf_op jit(solution)/shard_map/ppermute | solution.py:35

commit v9 on v8

--- a/solution.py
+++ b/solution.py
@@ -42,7 +42,7 @@
     row_base = lax.axis_index("param") * jnp.int32(resident_rows)
     core = lax.axis_index("ec")
     swap = [(0, 1), (1, 0)]
-    turn_count = 4
+    turn_count = 2
     rows_per_tile = resident_rows // turn_count
     scale_k = jnp.float32(K)
     param_count = lax.psum(1, "param")

time: 133 us -> 133 us (level)
    dot_general x4 -> x2, matrix products: 27.4 us -> 27 us  [local(): jnp.einsum('cra,apj->pcrj', gradient_slab.reshape(2, resident_example, ro...]
where the time goes in v9:
time: 133 us; the launch traced here: 132 us
  blocking collectives  59.9 us (45%)
  matrix products  27.9 us (21%)
  starting transfers between devices  22.7 us (17%)
  waiting for transfers between devices  14.7 us (11%)
  other arithmetic  2.91 us (2%)
  between operations  2.7 us (2%)
  local copies, waits for them, and re-layouts  1.65 us (1%)
    all_to_all x1, blocking collectives, local(): blocks = lax.all_to_all(blocks, ('param', 'ec'), 0, 0, tiled=True)  40.9 us
    dot_general x2, matrix products, local(): jnp.einsum('cra,apj->pcrj', gradient_slab.reshape(2, resident_example, ro...  27 us
    ppermute x5, starting transfers between devices, butterfly_sum(): values = values + lax.ppermute(values, axis, pairs)  20.8 us
    all_gather x1, blocking collectives, local(): pool_rows = lax.all_gather(projected, ('ey', 'ec'), axis=0, tiled=True)  19 us
    ppermute x5, waiting for transfers between devices, butterfly_sum(): values = values + lax.ppermute(values, axis, pairs)  14.7 us
  transfers between devices with their start and end apart: 6, of which 5 were waited for; matrix products, arithmetic and copies ran while one was open for 2% of the time, Pallas kernels for 0%

profile of v9, /device:TPU:2, one launch (start us, length us, event | category | flops | bytes accessed | tf_op | source)
XLA Modules:
  0.0 132.4 jit_solution(819672193502317939)
XLA Ops:
  0.6 1.1 convert_element_type.10
  1.7 1.9 %collective-permute-start = (f32[32,4096]{1,0:T(8,128)S(1)}, f32[32,4096]{1,0:T(8,128)S(1)}, u32[]{:S(2)}, u32[]{:S(2)}) collective-permute-start(f32[32,4096]{1,0:T(8,128)S(1)} %convert_element_type.10), channel_id=1, source_target_pairs={{0,1},{1,0},{2,3},{3,2},{4,5},{5,4},{6,7},{7,6},{8,9},{9,8},{10,11... | collective-permute-start | bytes 1572872 | tf_op jit(solution)/shard_map/ppermute | solution.py:53
  3.6 1.5 %fusion.42 = (s32[1]{0:T(128)}, s32[1]{0:T(128)}, s32[1]{0:T(128)}, s32[1]{0:T(128)}) fusion(s32[4]{0:T(128)} %param.4), kind=kLoop, calls=%fused_computation.58 | loop fusion | bytes 32 | tf_op jit(solution)/shard_map/slice | solution.py:14
  7.0 0.7 multiply_add_fusion
  7.8 0.1 maximum_select_fusion
  8.0 13.4 %fusion.10 = f32[32,128,2,32]{1,3,2,0:T(8,128)S(1)} fusion(bf16[2,32,2048,1]{2,1,0,3:T(8,128)(2,1)S(1)} %bitcast.53, s32[2048]{0:T(1024)S(1)} %get-tuple-element.5, s32[]{:T(128)} %bitcast.3, s32[32,128]{1,0:T(8,128)S(1)} %add_multiply_fusion), kind=kOutput, calls=%fused_computation.16 | convolution fusion | flops 1166016512 | bytes 1335300 | tf_op jit(solution)/shard_map/cra,apj->pcrj/dot_general | solution.py:68
  21.4 13.5 %fusion.18 = f32[32,128,2,32]{1,3,2,0:T(8,128)S(1)} fusion(f32[32,128,2,32]{1,3,2,0:T(8,128)S(1)} %fusion.10, bf16[2,32,2048,1]{2,1,0,3:T(8,128)(2,1)S(1)} %bitcast.52, s32[]{:T(128)} %bitcast.3, s32[32,128]{1,0:T(8,128)S(1)} %add_multiply_fusion, s32[2048]{0:T(1024)S(1)} %get-tuple-element.4), kind=kOutput, calls=%fused_computation.22 | convolution fusion | flops 1166278656 | bytes 2383876 | tf_op jit(solution)/shard_map/cra,apj->pcrj/dot_general | solution.py:68
  34.9 40.9 %all_to_all.5 = f32[64,32,128]{2,1,0:T(8,128)S(1)} all-to-all(f32[64,32,128]{2,1,0:T(8,128)S(1)} %bitcast.51), channel_id=1, replica_groups=mesh['param'=32,'ey'=8,'ec'=2] {'param','ec'}, dimensions={0} | all-to-all | bytes 2097152 | tf_op jit(solution)/shard_map/all_to_all | solution.py:77
  75.9 0.1 fusion.23
  76.0 19.0 %all_gather.3 = f32[512,256]{1,0:T(8,128)S(1)} all-gather(f32[32,256]{1,0:T(8,128)S(1)} %copy_bitcast_fusion), channel_id=1, replica_groups=mesh['param'=32,'ey'=8,'ec'=2] {'ey','ec'}, dimensions={0}, use_global_device_ids=true | all-gather | bytes 557056 | tf_op jit(solution)/shard_map/all_gather | solution.py:81
  95.0 0.7 multiply_reduce_fusion
  95.7 0.2 convolution_bitcast_fusion
  96.1 3.3 %collective-permute-start.1 = (f32[8480]{0:T(1024)S(1)}, f32[8480]{0:T(1024)S(1)}, u32[]{:S(2)}, u32[]{:S(2)}) collective-permute-start(f32[8480]{0:T(1024)S(1)} %concatenate.11), channel_id=1, source_target_pairs={{0,16},{16,0},{32,48},{48,32},{64,80},{80,64},{96,112},{112,96},{1... | collective-permute-start | bytes 101768 | tf_op jit(solution)/shard_map/ppermute | solution.py:35
  99.3 2.6 %collective-permute-done.1 = f32[8480]{0:T(1024)S(1)} collective-permute-done((f32[8480]{0:T(1024)S(1)}, f32[8480]{0:T(1024)S(1)}, u32[]{:S(2)}, u32[]{:S(2)}) %collective-permute-start.1) | collective-permute-done | bytes 33952 | tf_op jit(solution)/shard_map/ppermute | solution.py:35
  101.9 4.8 %collective-permute-start.2 = (f32[8480]{0:T(1024)S(1)}, f32[8480]{0:T(1024)S(1)}, u32[]{:S(2)}, u32[]{:S(2)}) collective-permute-start(f32[8480]{0:T(1024)S(1)} %add.124), channel_id=1, source_target_pairs={{0,32},{16,48},{32,0},{48,16},{64,96},{80,112},{96,64},{112,80},{1... | collective-permute-start | bytes 101768 | tf_op jit(solution)/shard_map/ppermute | solution.py:35
  106.7 1.9 %collective-permute-done.2 = f32[8480]{0:T(1024)S(1)} collective-permute-done((f32[8480]{0:T(1024)S(1)}, f32[8480]{0:T(1024)S(1)}, u32[]{:S(2)}, u32[]{:S(2)}) %collective-permute-start.2) | collective-permute-done | bytes 33952 | tf_op jit(solution)/shard_map/ppermute | solution.py:35
  108.7 5.2 %collective-permute-start.3 = (f32[8480]{0:T(1024)S(1)}, f32[8480]{0:T(1024)S(1)}, u32[]{:S(2)}, u32[]{:S(2)}) collective-permute-start(f32[8480]{0:T(1024)S(1)} %add.125), channel_id=1, source_target_pairs={{0,64},{16,80},{32,96},{48,112},{64,0},{80,16},{96,32},{112,48},{1... | collective-permute-start | bytes 101768 | tf_op jit(solution)/shard_map/ppermute | solution.py:35
  113.9 4.5 %collective-permute-done.3 = f32[8480]{0:T(1024)S(1)} collective-permute-done((f32[8480]{0:T(1024)S(1)}, f32[8480]{0:T(1024)S(1)}, u32[]{:S(2)}, u32[]{:S(2)}) %collective-permute-start.3) | collective-permute-done | bytes 33952 | tf_op jit(solution)/shard_map/ppermute | solution.py:35
  118.4 3.4 %collective-permute-start.4 = (f32[8480]{0:T(1024)S(1)}, f32[8480]{0:T(1024)S(1)}, u32[]{:S(2)}, u32[]{:S(2)}) collective-permute-start(f32[8480]{0:T(1024)S(1)} %add.126), channel_id=1, source_target_pairs={{0,128},{16,144},{32,160},{48,176},{64,192},{80,208},{96,224},{112... | collective-permute-start | bytes 101768 | tf_op jit(solution)/shard_map/ppermute | solution.py:35
  121.9 2.4 %collective-permute-done.4 = f32[8480]{0:T(1024)S(1)} collective-permute-done((f32[8480]{0:T(1024)S(1)}, f32[8480]{0:T(1024)S(1)}, u32[]{:S(2)}, u32[]{:S(2)}) %collective-permute-start.4) | collective-permute-done | bytes 33952 | tf_op jit(solution)/shard_map/ppermute | solution.py:35
  124.3 4.0 %collective-permute-start.5 = (f32[8480]{0:T(1024)S(1)}, f32[8480]{0:T(1024)S(1)}, u32[]{:S(2)}, u32[]{:S(2)}) collective-permute-start(f32[8480]{0:T(1024)S(1)} %add.127), channel_id=1, source_target_pairs={{0,256},{16,272},{32,288},{48,304},{64,320},{80,336},{96,352},{112... | collective-permute-start | bytes 101768 | tf_op jit(solution)/shard_map/ppermute | solution.py:35
  128.3 3.3 %collective-permute-done.5 = f32[8480]{0:T(1024)S(1)} collective-permute-done((f32[8480]{0:T(1024)S(1)}, f32[8480]{0:T(1024)S(1)}, u32[]{:S(2)}, u32[]{:S(2)}) %collective-permute-start.5) | collective-permute-done | bytes 33952 | tf_op jit(solution)/shard_map/ppermute | solution.py:35
  131.6 0.1 fusion.25
  131.7 0.7 multiply_multiply_fusion
  (22 shorter events, 0.4 us)
Async XLA Ops:
  0.6 7.2 %copy-start = (bf16[32,4096]{1,0:T(8,128)(2,1)S(1)}, bf16[32,4096]{1,0:T(8,128)(2,1)}, u32[]{:S(2)}) copy-start(bf16[32,4096]{1,0:T(8,128)(2,1)} %param.3) | copy-start | bytes 786436
  1.7 6.1 %collective-permute-start = (f32[32,4096]{1,0:T(8,128)S(1)}, f32[32,4096]{1,0:T(8,128)S(1)}, u32[]{:S(2)}, u32[]{:S(2)}) collective-permute-start(f32[32,4096]{1,0:T(8,128)S(1)} %convert_element_type.10), channel_id=1, source_target_pairs={{0,1},{1,0},{2,3},{3,2},{4,5},{5,4},{6,7},{7,6},{8,9},{9,8},{10,11... | collective-permute-start | bytes 1572872 | tf_op jit(solution)/shard_map/ppermute | solution.py:53
  75.8 19.2 %copy-start.1 = (s32[256]{0:T(256)S(1)}, s32[256]{0:T(256)}, u32[]{:S(2)}) copy-start(s32[256]{0:T(256)} %param.5) | copy-start | bytes 3076
  96.1 5.8 %collective-permute-start.1 = (f32[8480]{0:T(1024)S(1)}, f32[8480]{0:T(1024)S(1)}, u32[]{:S(2)}, u32[]{:S(2)}) collective-permute-start(f32[8480]{0:T(1024)S(1)} %concatenate.11), channel_id=1, source_target_pairs={{0,16},{16,0},{32,48},{48,32},{64,80},{80,64},{96,112},{112,96},{1... | collective-permute-start | bytes 101768 | tf_op jit(solution)/shard_map/ppermute | solution.py:35
  101.9 6.7 %collective-permute-start.2 = (f32[8480]{0:T(1024)S(1)}, f32[8480]{0:T(1024)S(1)}, u32[]{:S(2)}, u32[]{:S(2)}) collective-permute-start(f32[8480]{0:T(1024)S(1)} %add.124), channel_id=1, source_target_pairs={{0,32},{16,48},{32,0},{48,16},{64,96},{80,112},{96,64},{112,80},{1... | collective-permute-start | bytes 101768 | tf_op jit(solution)/shard_map/ppermute | solution.py:35
  108.7 9.7 %collective-permute-start.3 = (f32[8480]{0:T(1024)S(1)}, f32[8480]{0:T(1024)S(1)}, u32[]{:S(2)}, u32[]{:S(2)}) collective-permute-start(f32[8480]{0:T(1024)S(1)} %add.125), channel_id=1, source_target_pairs={{0,64},{16,80},{32,96},{48,112},{64,0},{80,16},{96,32},{112,48},{1... | collective-permute-start | bytes 101768 | tf_op jit(solution)/shard_map/ppermute | solution.py:35
  118.4 5.8 %collective-permute-start.4 = (f32[8480]{0:T(1024)S(1)}, f32[8480]{0:T(1024)S(1)}, u32[]{:S(2)}, u32[]{:S(2)}) collective-permute-start(f32[8480]{0:T(1024)S(1)} %add.126), channel_id=1, source_target_pairs={{0,128},{16,144},{32,160},{48,176},{64,192},{80,208},{96,224},{112... | collective-permute-start | bytes 101768 | tf_op jit(solution)/shard_map/ppermute | solution.py:35
  124.3 7.3 %collective-permute-start.5 = (f32[8480]{0:T(1024)S(1)}, f32[8480]{0:T(1024)S(1)}, u32[]{:S(2)}, u32[]{:S(2)}) collective-permute-start(f32[8480]{0:T(1024)S(1)} %add.127), channel_id=1, source_target_pairs={{0,256},{16,272},{32,288},{48,304},{64,320},{80,336},{96,352},{112... | collective-permute-start | bytes 101768 | tf_op jit(solution)/shard_map/ppermute | solution.py:35

commit v10 on v9

--- a/solution.py
+++ b/solution.py
@@ -93,7 +93,7 @@
     own_scale = jnp.sqrt(scale_k / (total_sq + norm_eps))
     target_scale = jnp.sqrt(scale_k / (target_sq + norm_eps))
     features = projected * own_scale[:, None]
-    scores = dots * own_scale[:, None] * target_scale[None, :] / scale_k
+    scores = dots * own_scale[:, None] * (target_scale / scale_k)[None, :]
     return (features, scores)
 
 

time: 133 us -> 133 us (level)
  no operation moved by 1% of the time
where the time goes in v10:
time: 133 us; the launch traced here: 132 us
  blocking collectives  59.9 us (45%)
  matrix products  27.9 us (21%)
  starting transfers between devices  22.7 us (17%)
  waiting for transfers between devices  14.7 us (11%)
  other arithmetic  2.91 us (2%)
  between operations  2.71 us (2%)
  local copies, waits for them, and re-layouts  1.64 us (1%)
    all_to_all x1, blocking collectives, local(): blocks = lax.all_to_all(blocks, ('param', 'ec'), 0, 0, tiled=True)  40.9 us
    dot_general x2, matrix products, local(): jnp.einsum('cra,apj->pcrj', gradient_slab.reshape(2, resident_example, ro...  27 us
    ppermute x5, starting transfers between devices, butterfly_sum(): values = values + lax.ppermute(values, axis, pairs)  20.8 us
    all_gather x1, blocking collectives, local(): pool_rows = lax.all_gather(projected, ('ey', 'ec'), axis=0, tiled=True)  19 us
    ppermute x5, waiting for transfers between devices, butterfly_sum(): values = values + lax.ppermute(values, axis, pairs)  14.7 us
  transfers between devices with their start and end apart: 6, of which 5 were waited for; matrix products, arithmetic and copies ran while one was open for 2% of the time, Pallas kernels for 0%

profile of v10, /device:TPU:2, one launch (start us, length us, event | category | flops | bytes accessed | tf_op | source)
XLA Modules:
  0.0 132.4 jit_solution(7650724657482630751)
XLA Ops:
  0.6 1.1 convert_element_type.10
  1.7 1.9 %collective-permute-start = (f32[32,4096]{1,0:T(8,128)S(1)}, f32[32,4096]{1,0:T(8,128)S(1)}, u32[]{:S(2)}, u32[]{:S(2)}) collective-permute-start(f32[32,4096]{1,0:T(8,128)S(1)} %convert_element_type.10), channel_id=1, source_target_pairs={{0,1},{1,0},{2,3},{3,2},{4,5},{5,4},{6,7},{7,6},{8,9},{9,8},{10,11... | collective-permute-start | bytes 1572872 | tf_op jit(solution)/shard_map/ppermute | solution.py:53
  3.6 1.5 %fusion.43 = (s32[1]{0:T(128)}, s32[1]{0:T(128)}, s32[1]{0:T(128)}, s32[1]{0:T(128)}) fusion(s32[4]{0:T(128)} %param.4), kind=kLoop, calls=%fused_computation.59 | loop fusion | bytes 32 | tf_op jit(solution)/shard_map/slice | solution.py:14
  7.0 0.7 multiply_add_fusion
  7.8 0.1 maximum_select_fusion
  8.0 13.4 %fusion.10 = f32[32,128,2,32]{1,3,2,0:T(8,128)S(1)} fusion(bf16[2,32,2048,1]{2,1,0,3:T(8,128)(2,1)S(1)} %bitcast.53, s32[2048]{0:T(1024)S(1)} %get-tuple-element.5, s32[]{:T(128)} %bitcast.3, s32[32,128]{1,0:T(8,128)S(1)} %add_multiply_fusion), kind=kOutput, calls=%fused_computation.16 | convolution fusion | flops 1166016512 | bytes 1335300 | tf_op jit(solution)/shard_map/cra,apj->pcrj/dot_general | solution.py:68
  21.4 13.5 %fusion.18 = f32[32,128,2,32]{1,3,2,0:T(8,128)S(1)} fusion(f32[32,128,2,32]{1,3,2,0:T(8,128)S(1)} %fusion.10, bf16[2,32,2048,1]{2,1,0,3:T(8,128)(2,1)S(1)} %bitcast.52, s32[]{:T(128)} %bitcast.3, s32[32,128]{1,0:T(8,128)S(1)} %add_multiply_fusion, s32[2048]{0:T(1024)S(1)} %get-tuple-element.4), kind=kOutput, calls=%fused_computation.22 | convolution fusion | flops 1166278656 | bytes 2383876 | tf_op jit(solution)/shard_map/cra,apj->pcrj/dot_general | solution.py:68
  34.9 40.9 %all_to_all.5 = f32[64,32,128]{2,1,0:T(8,128)S(1)} all-to-all(f32[64,32,128]{2,1,0:T(8,128)S(1)} %bitcast.51), channel_id=1, replica_groups=mesh['param'=32,'ey'=8,'ec'=2] {'param','ec'}, dimensions={0} | all-to-all | bytes 2097152 | tf_op jit(solution)/shard_map/all_to_all | solution.py:77
  75.9 0.1 fusion.23
  76.0 19.0 %all_gather.3 = f32[512,256]{1,0:T(8,128)S(1)} all-gather(f32[32,256]{1,0:T(8,128)S(1)} %copy_bitcast_fusion), channel_id=1, replica_groups=mesh['param'=32,'ey'=8,'ec'=2] {'ey','ec'}, dimensions={0}, use_global_device_ids=true | all-gather | bytes 557056 | tf_op jit(solution)/shard_map/all_gather | solution.py:81
  95.0 0.7 multiply_reduce_fusion
  95.7 0.2 convolution_bitcast_fusion
  96.1 3.3 %collective-permute-start.1 = (f32[8480]{0:T(1024)S(1)}, f32[8480]{0:T(1024)S(1)}, u32[]{:S(2)}, u32[]{:S(2)}) collective-permute-start(f32[8480]{0:T(1024)S(1)} %concatenate.11), channel_id=1, source_target_pairs={{0,16},{16,0},{32,48},{48,32},{64,80},{80,64},{96,112},{112,96},{1... | collective-permute-start | bytes 101768 | tf_op jit(solution)/shard_map/ppermute | solution.py:35
  99.3 2.6 %collective-permute-done.1 = f32[8480]{0:T(1024)S(1)} collective-permute-done((f32[8480]{0:T(1024)S(1)}, f32[8480]{0:T(1024)S(1)}, u32[]{:S(2)}, u32[]{:S(2)}) %collective-permute-start.1) | collective-permute-done | bytes 33952 | tf_op jit(solution)/shard_map/ppermute | solution.py:35
  101.9 4.8 %collective-permute-start.2 = (f32[8480]{0:T(1024)S(1)}, f32[8480]{0:T(1024)S(1)}, u32[]{:S(2)}, u32[]{:S(2)}) collective-permute-start(f32[8480]{0:T(1024)S(1)} %add.124), channel_id=1, source_target_pairs={{0,32},{16,48},{32,0},{48,16},{64,96},{80,112},{96,64},{112,80},{1... | collective-permute-start | bytes 101768 | tf_op jit(solution)/shard_map/ppermute | solution.py:35
  106.7 1.9 %collective-permute-done.2 = f32[8480]{0:T(1024)S(1)} collective-permute-done((f32[8480]{0:T(1024)S(1)}, f32[8480]{0:T(1024)S(1)}, u32[]{:S(2)}, u32[]{:S(2)}) %collective-permute-start.2) | collective-permute-done | bytes 33952 | tf_op jit(solution)/shard_map/ppermute | solution.py:35
  108.7 5.2 %collective-permute-start.3 = (f32[8480]{0:T(1024)S(1)}, f32[8480]{0:T(1024)S(1)}, u32[]{:S(2)}, u32[]{:S(2)}) collective-permute-start(f32[8480]{0:T(1024)S(1)} %add.125), channel_id=1, source_target_pairs={{0,64},{16,80},{32,96},{48,112},{64,0},{80,16},{96,32},{112,48},{1... | collective-permute-start | bytes 101768 | tf_op jit(solution)/shard_map/ppermute | solution.py:35
  113.9 4.5 %collective-permute-done.3 = f32[8480]{0:T(1024)S(1)} collective-permute-done((f32[8480]{0:T(1024)S(1)}, f32[8480]{0:T(1024)S(1)}, u32[]{:S(2)}, u32[]{:S(2)}) %collective-permute-start.3) | collective-permute-done | bytes 33952 | tf_op jit(solution)/shard_map/ppermute | solution.py:35
  118.4 3.4 %collective-permute-start.4 = (f32[8480]{0:T(1024)S(1)}, f32[8480]{0:T(1024)S(1)}, u32[]{:S(2)}, u32[]{:S(2)}) collective-permute-start(f32[8480]{0:T(1024)S(1)} %add.126), channel_id=1, source_target_pairs={{0,128},{16,144},{32,160},{48,176},{64,192},{80,208},{96,224},{112... | collective-permute-start | bytes 101768 | tf_op jit(solution)/shard_map/ppermute | solution.py:35
  121.9 2.4 %collective-permute-done.4 = f32[8480]{0:T(1024)S(1)} collective-permute-done((f32[8480]{0:T(1024)S(1)}, f32[8480]{0:T(1024)S(1)}, u32[]{:S(2)}, u32[]{:S(2)}) %collective-permute-start.4) | collective-permute-done | bytes 33952 | tf_op jit(solution)/shard_map/ppermute | solution.py:35
  124.3 4.0 %collective-permute-start.5 = (f32[8480]{0:T(1024)S(1)}, f32[8480]{0:T(1024)S(1)}, u32[]{:S(2)}, u32[]{:S(2)}) collective-permute-start(f32[8480]{0:T(1024)S(1)} %add.127), channel_id=1, source_target_pairs={{0,256},{16,272},{32,288},{48,304},{64,320},{80,336},{96,352},{112... | collective-permute-start | bytes 101768 | tf_op jit(solution)/shard_map/ppermute | solution.py:35
  128.3 3.3 %collective-permute-done.5 = f32[8480]{0:T(1024)S(1)} collective-permute-done((f32[8480]{0:T(1024)S(1)}, f32[8480]{0:T(1024)S(1)}, u32[]{:S(2)}, u32[]{:S(2)}) %collective-permute-start.5) | collective-permute-done | bytes 33952 | tf_op jit(solution)/shard_map/ppermute | solution.py:35
  131.6 0.1 fusion.26
  131.7 0.7 multiply_multiply_fusion
  (22 shorter events, 0.4 us)
Async XLA Ops:
  0.6 7.2 %copy-start = (bf16[32,4096]{1,0:T(8,128)(2,1)S(1)}, bf16[32,4096]{1,0:T(8,128)(2,1)}, u32[]{:S(2)}) copy-start(bf16[32,4096]{1,0:T(8,128)(2,1)} %param.3) | copy-start | bytes 786436
  1.7 6.1 %collective-permute-start = (f32[32,4096]{1,0:T(8,128)S(1)}, f32[32,4096]{1,0:T(8,128)S(1)}, u32[]{:S(2)}, u32[]{:S(2)}) collective-permute-start(f32[32,4096]{1,0:T(8,128)S(1)} %convert_element_type.10), channel_id=1, source_target_pairs={{0,1},{1,0},{2,3},{3,2},{4,5},{5,4},{6,7},{7,6},{8,9},{9,8},{10,11... | collective-permute-start | bytes 1572872 | tf_op jit(solution)/shard_map/ppermute | solution.py:53
  75.8 19.2 %copy-start.1 = (s32[256]{0:T(256)S(1)}, s32[256]{0:T(256)}, u32[]{:S(2)}) copy-start(s32[256]{0:T(256)} %param.5) | copy-start | bytes 3076
  96.1 5.8 %collective-permute-start.1 = (f32[8480]{0:T(1024)S(1)}, f32[8480]{0:T(1024)S(1)}, u32[]{:S(2)}, u32[]{:S(2)}) collective-permute-start(f32[8480]{0:T(1024)S(1)} %concatenate.11), channel_id=1, source_target_pairs={{0,16},{16,0},{32,48},{48,32},{64,80},{80,64},{96,112},{112,96},{1... | collective-permute-start | bytes 101768 | tf_op jit(solution)/shard_map/ppermute | solution.py:35
  101.9 6.7 %collective-permute-start.2 = (f32[8480]{0:T(1024)S(1)}, f32[8480]{0:T(1024)S(1)}, u32[]{:S(2)}, u32[]{:S(2)}) collective-permute-start(f32[8480]{0:T(1024)S(1)} %add.124), channel_id=1, source_target_pairs={{0,32},{16,48},{32,0},{48,16},{64,96},{80,112},{96,64},{112,80},{1... | collective-permute-start | bytes 101768 | tf_op jit(solution)/shard_map/ppermute | solution.py:35
  108.7 9.7 %collective-permute-start.3 = (f32[8480]{0:T(1024)S(1)}, f32[8480]{0:T(1024)S(1)}, u32[]{:S(2)}, u32[]{:S(2)}) collective-permute-start(f32[8480]{0:T(1024)S(1)} %add.125), channel_id=1, source_target_pairs={{0,64},{16,80},{32,96},{48,112},{64,0},{80,16},{96,32},{112,48},{1... | collective-permute-start | bytes 101768 | tf_op jit(solution)/shard_map/ppermute | solution.py:35
  118.4 5.8 %collective-permute-start.4 = (f32[8480]{0:T(1024)S(1)}, f32[8480]{0:T(1024)S(1)}, u32[]{:S(2)}, u32[]{:S(2)}) collective-permute-start(f32[8480]{0:T(1024)S(1)} %add.126), channel_id=1, source_target_pairs={{0,128},{16,144},{32,160},{48,176},{64,192},{80,208},{96,224},{112... | collective-permute-start | bytes 101768 | tf_op jit(solution)/shard_map/ppermute | solution.py:35
  124.3 7.3 %collective-permute-start.5 = (f32[8480]{0:T(1024)S(1)}, f32[8480]{0:T(1024)S(1)}, u32[]{:S(2)}, u32[]{:S(2)}) collective-permute-start(f32[8480]{0:T(1024)S(1)} %add.127), channel_id=1, source_target_pairs={{0,256},{16,272},{32,288},{48,304},{64,320},{80,336},{96,352},{112... | collective-permute-start | bytes 101768 | tf_op jit(solution)/shard_map/ppermute | solution.py:35
